TPU v7x, 1024 devices: a whole 4x8x16 slice. The times are simulated.
1024 devices in a mesh: fsdp: 8 (over x, y_hi), ctx: 32 (over z, core), head: 4 (over y_lo).
Axes of the slice: x: 4, y: 8 (y_hi: 2, y_lo: 4; y = y_hi * 4 + y_lo), z: 16, core: 2. Of those that a mesh axis runs over, the one named last changes fastest.
Arguments:
- q_raw: bfloat16 [8, 4096, 4096], P('fsdp', 'ctx', 'head'), may hold values from -6 to 6
- unnormed_keys: bfloat16 [8, 4096, 2048], P('fsdp', 'ctx', 'head'), may hold values from -6 to 6
- value_input: bfloat16 [8, 4096, 2048], P('fsdp', 'ctx', 'head'), may hold values from -6 to 6
- d_out: bfloat16 [8, 4096, 4096], P('fsdp', 'ctx', 'head'), may hold values from -6 to 6
- file_ids: int32 [8, 4096], P('fsdp', 'ctx'), may hold values from 0 to 15, never falling along the last dimension, each value on 1 to 512 neighbouring positions
- q_gain: float32 [128], replicated, may hold values from 0.5 to 2.5
- k_gain: float32 [128], replicated, may hold values from 0.4 to 2.2
Outputs:
- attended: bfloat16 [8, 4096, 4096], P('fsdp', 'ctx', 'head')
- dq_raw: bfloat16 [8, 4096, 4096], P('fsdp', 'ctx', 'head')
- dk_raw: bfloat16 [8, 4096, 2048], P('fsdp', 'ctx', 'head')
- dv: bfloat16 [8, 4096, 2048], P('fsdp', 'ctx', 'head')
- dq_gain: float32 [128], replicated
- dk_gain: float32 [128], replicated
Inputs may be any that keep to these rules, and one draw needn't show every extreme that they name: `file_ids`: in each sequence the file numbers never fall, every file number from 0 up occurs, every file has 1 to min(4095, 512) tokens, and some file has exactly that many.
All inputs are finite; a program needn't handle non-finite values.
Results may differ from a plain program's by a relative error of at most 0.013.
Values may be sent and summed in bfloat16 or wider, within the bound.
No kernel may reach another device: no remote copies, remote signals or barrier semaphores. Data moves between devices by JAX's collectives and lax.ppermute only.
A program may use at most 32 MiB of HBM per device.

v0:
```python
import jax
import jax.numpy as jnp
from jax import lax
from jax.sharding import PartitionSpec as P

HEAD_WIDTH = 128
WINDOW = 256
QPAS = 168


EPSILON = 1e-06
THETA_BASE = 10000.0
NEGATIVE = -1e30


def passed_along(value, axis, by):
    devices = lax.axis_size(axis)
    pairs = [(i, i + by) for i in range(devices) if 0 <= i + by < devices]
    return lax.ppermute(value, axis, pairs)


def rotate(values, positions):
    half_dim = values.shape[-1] // 2
    frequency = THETA_BASE ** (-(jnp.arange(half_dim, dtype=jnp.float32) * 2.0 / values.shape[-1]))
    angles = positions.astype(jnp.float32)[:, None] * frequency[None, :]
    cosine = jnp.cos(angles)[:, None, :]
    sine_part = jnp.sin(angles)[:, None, :]
    first_half = values[..., :half_dim]
    second = values[..., half_dim:]
    return jnp.concatenate(
        [first_half * cosine - second * sine_part, second * cosine + first_half * sine_part],
        axis=-1,
    )


def unrotate(values, positions):
    half_dim = values.shape[-1] // 2
    frequency = THETA_BASE ** (-(jnp.arange(half_dim, dtype=jnp.float32) * 2.0 / values.shape[-1]))
    angles = positions.astype(jnp.float32)[:, None] * frequency[None, :]
    cosine = jnp.cos(angles)[:, None, :]
    sine_part = jnp.sin(angles)[:, None, :]
    first_half = values[..., :half_dim]
    second = values[..., half_dim:]
    return jnp.concatenate(
        [first_half * cosine + second * sine_part, second * cosine - first_half * sine_part],
        axis=-1,
    )


def normalize(raw_rows, gain_row, positions, head_count):
    values = raw_rows.astype(jnp.float32).reshape(raw_rows.shape[0], head_count, -1)
    inverse = lax.rsqrt(jnp.mean(values * values, axis=-1, keepdims=True) + EPSILON)
    unit_rows = values * inverse
    return (unit_rows, inverse, rotate(unit_rows * gain_row, positions).astype(jnp.bfloat16))


def restore(grad_rot, unit_rows, inverse, gain_row, positions):
    normed = unrotate(grad_rot, positions)
    gain_term = jnp.sum(normed * unit_rows, axis=(0, 1))
    scaled = normed * gain_row
    grad_raw = inverse * (scaled - unit_rows * jnp.mean(scaled * unit_rows, axis=-1, keepdims=True))
    return (grad_raw, gain_term)


def visible(query_pos, query_file, key_pos, key_file):
    earlier = key_pos[None, :] <= query_pos[:, None]
    inside = query_pos[:, None] - key_pos[None, :] < WINDOW
    same_file = key_file[None, :] == query_file[:, None]
    return earlier & inside & same_file & (key_pos[None, :] >= 0)


def scores_of(queries, key_rows, allowed):
    logit_scores = QPAS ** (-0.5) * jnp.einsum(
        "qhgd,khd->hgqk", queries, key_rows, preferred_element_type=jnp.float32
    )
    return jnp.where(allowed[None, None], logit_scores, NEGATIVE)


def body(q_raw, unnormed_keys, value_input, d_out, file_ids, q_gain, k_gain):
    row_count = q_raw.shape[1]
    qheads = q_raw.shape[2] // HEAD_WIDTH
    kheads = unnormed_keys.shape[2] // HEAD_WIDTH
    group_size = qheads // kheads
    ctx_size = lax.axis_size("ctx")
    ctx_place = lax.axis_index("ctx")
    reach_count = min((WINDOW + row_count - 1) // row_count, ctx_size - 1)
    scale_factor = QPAS ** (-0.5)
    positions = ctx_place * row_count + jnp.arange(row_count, dtype=jnp.int32)
    file_row = file_ids[0]
    q_unit, q_inv, q_rot = normalize(q_raw[0], q_gain, positions, qheads)
    k_unit, k_inv, k_rot = normalize(unnormed_keys[0], k_gain, positions, kheads)
    value_own = value_input[0].reshape(row_count, kheads, HEAD_WIDTH)
    key_list, value_list, file_list = ([], [], [])
    for offset in range(reach_count, 0, -1):
        key_far, value_far, file_far = passed_along((k_rot, value_own, file_row), "ctx", offset)
        key_list.append(key_far)
        value_list.append(value_far)
        file_list.append(file_far)
    key_rows = jnp.concatenate(key_list + [k_rot], axis=0)
    value_rows = jnp.concatenate(value_list + [value_own], axis=0)
    key_files = jnp.concatenate(file_list + [file_row], axis=0)
    key_pos = (ctx_place - reach_count) * row_count + jnp.arange(
        (reach_count + 1) * row_count, dtype=jnp.int32
    )
    allowed = visible(positions, file_row, key_pos, key_files)
    queries = q_rot.reshape(row_count, kheads, group_size, HEAD_WIDTH)
    out_grads = d_out[0].reshape(row_count, kheads, group_size, HEAD_WIDTH)
    logit_scores = scores_of(queries, key_rows, allowed)
    row_peak = jnp.max(logit_scores, axis=-1, keepdims=True)
    log_total = (
        row_peak + jnp.log(jnp.sum(jnp.exp(logit_scores - row_peak), axis=-1, keepdims=True))
    )[..., 0]
    weights = jnp.exp(logit_scores - log_total[..., None])
    weights_low = weights.astype(jnp.bfloat16)
    attended = jnp.einsum(
        "hgqk,khd->qhgd", weights_low, value_rows, preferred_element_type=jnp.float32
    ).astype(jnp.bfloat16)
    row_delta = jnp.einsum(
        "qhgd,qhgd->hgq", out_grads.astype(jnp.float32), attended.astype(jnp.float32)
    )
    dprobs = jnp.einsum("qhgd,khd->hgqk", out_grads, value_rows, preferred_element_type=jnp.float32)
    dscores = (weights * (dprobs - row_delta[..., None])).astype(jnp.bfloat16)
    grad_queries = scale_factor * jnp.einsum(
        "hgqk,khd->qhgd", dscores, key_rows, preferred_element_type=jnp.float32
    )
    grad_keys = scale_factor * jnp.einsum(
        "hgqk,qhgd->khd", dscores, queries, preferred_element_type=jnp.float32
    )
    grad_values = jnp.einsum(
        "hgqk,qhgd->khd", weights_low, out_grads, preferred_element_type=jnp.float32
    )
    key_own = grad_keys[reach_count * row_count :]
    value_grad = grad_values[reach_count * row_count :]
    for offset in range(1, reach_count + 1):
        low_row = (reach_count - offset) * row_count
        back_keys, back_values = passed_along(
            (grad_keys[low_row : low_row + row_count], grad_values[low_row : low_row + row_count]),
            "ctx",
            -offset,
        )
        key_own = key_own + back_keys
        value_grad = value_grad + back_values
    dq_grad, q_term = restore(
        grad_queries.reshape(row_count, qheads, HEAD_WIDTH), q_unit, q_inv, q_gain, positions
    )
    dk_grad, k_term = restore(key_own, k_unit, k_inv, k_gain, positions)
    q_total, k_total = lax.psum((q_term, k_term), ("fsdp", "ctx", "head"))
    return (
        attended.reshape(1, row_count, -1),
        dq_grad.astype(jnp.bfloat16).reshape(1, row_count, -1),
        dk_grad.astype(jnp.bfloat16).reshape(1, row_count, -1),
        value_grad.astype(jnp.bfloat16).reshape(1, row_count, -1),
        q_total,
        k_total,
    )


def solution(mesh):
    in_specs = (
        P("fsdp", "ctx", "head"),
        P("fsdp", "ctx", "head"),
        P("fsdp", "ctx", "head"),
        P("fsdp", "ctx", "head"),
        P("fsdp", "ctx"),
        P(),
        P(),
    )
    out_specs = (
        P("fsdp", "ctx", "head"),
        P("fsdp", "ctx", "head"),
        P("fsdp", "ctx", "head"),
        P("fsdp", "ctx", "head"),
        P(),
        P(),
    )
    return jax.shard_map(body, mesh=mesh, in_specs=in_specs, out_specs=out_specs, check_vma=False)
```

profile of v0, /device:TPU:1, one launch (start us, length us, event | category | flops | bytes accessed | tf_op | source)
XLA Modules:
  0.0 204.7 jit_solution(17052804696396478866)
XLA Ops:
  0.7 1.1 copy.80
  1.8 0.1 copy.81
  2.0 0.3 multiply_cosine_fusion
  2.3 0.8 multiply_multiply_fusion.1
  3.1 0.1 subtract_convert_fusion.1
  3.3 0.1 pad_maximum_fusion.3
  3.4 4.8 %collective-permute-start.4 = (bf16[128,4,128]{2,0,1:T(8,128)(2,1)S(1)}, bf16[128,4,128]{2,0,1:T(8,128)(2,1)S(1)}, u32[]{:S(2)}, u32[]{:S(2)}) collective-permute-start(bf16[128,4,128]{2,0,1:T(8,128)(2,1)S(1)} %pad_maximum_fusion.3), channel_id=1, source_target_pairs={{0,8},{4,12},{8,16},{12,20},{16,24},{20,28},{24,32},{28,36},{32,40... | collective-permute-start | bytes 393224 | tf_op jit(solution)/shard_map/ppermute | solution.py:19
  8.3 4.8 %collective-permute-start.5 = (bf16[128,4,128]{2,0,1:T(8,128)(2,1)S(1)}, bf16[128,4,128]{2,0,1:T(8,128)(2,1)S(1)}, u32[]{:S(2)}, u32[]{:S(2)}) collective-permute-start(bf16[128,4,128]{2,0,1:T(8,128)(2,1)S(1)} %pad_maximum_fusion.3), channel_id=1, source_target_pairs={{0,4},{4,8},{8,12},{12,16},{16,20},{20,24},{24,28},{28,32},{32,36}... | collective-permute-start | bytes 393224 | tf_op jit(solution)/shard_map/ppermute | solution.py:19
  13.1 4.0 %collective-permute-start.2 = (s32[128]{0:T(128)S(1)}, s32[128]{0:T(128)S(1)}, u32[]{:S(2)}, u32[]{:S(2)}) collective-permute-start(s32[128]{0:T(128)S(1)} %bitcast.119), channel_id=1, source_target_pairs={{0,8},{4,12},{8,16},{12,20},{16,24},{20,28},{24,32},{28,36},{32,40... | collective-permute-start | bytes 1544 | tf_op jit(solution)/shard_map/ppermute | solution.py:19
  17.1 2.2 %collective-permute-start.3 = (s32[128]{0:T(128)S(1)}, s32[128]{0:T(128)S(1)}, u32[]{:S(2)}, u32[]{:S(2)}) collective-permute-start(s32[128]{0:T(128)S(1)} %bitcast.120), channel_id=1, source_target_pairs={{0,4},{4,8},{8,12},{12,16},{16,20},{20,24},{24,28},{28,32},{32,36}... | collective-permute-start | bytes 1544 | tf_op jit(solution)/shard_map/ppermute | solution.py:19
  19.4 0.8 copy.79
  20.1 5.9 %collective-permute-start = (bf16[128,4,128]{0,2,1:T(8,128)(2,1)}, bf16[128,4,128]{0,2,1:T(8,128)(2,1)}, u32[]{:S(2)}, u32[]{:S(2)}) collective-permute-start(bf16[128,4,128]{0,2,1:T(8,128)(2,1)} %bitcast.2), channel_id=1, source_target_pairs={{0,8},{4,12},{8,16},{12,20},{16,24},{20,28},{24,32},{28,36},{32,40... | collective-permute-start | bytes 393224 | tf_op jit(solution)/shard_map/ppermute | solution.py:19
  26.0 0.6 broadcast_bitcast_fusion.1
  26.6 0.1 copy.127
  26.7 0.2 multiply_reduce_fusion.3
  27.0 0.2 multiply_multiply_fusion
  27.2 0.3 subtract_convert_fusion
  27.5 0.7 copy.83
  28.3 0.7 copy.82
  29.0 0.2 reshape_squeeze.7
  29.2 0.2 copy.97
  29.4 0.2 mul.377
  29.6 0.9 mul.390
  30.5 3.7 %collective-permute-start.1 = (bf16[128,4,128]{0,2,1:T(8,128)(2,1)}, bf16[128,4,128]{0,2,1:T(8,128)(2,1)S(1)}, u32[]{:S(2)}, u32[]{:S(2)}) collective-permute-start(bf16[128,4,128]{0,2,1:T(8,128)(2,1)} %bitcast.2), channel_id=1, source_target_pairs={{0,4},{4,8},{8,12},{12,16},{16,20},{20,24},{24,28},{28,32},{32,36}... | collective-permute-start | bytes 393224 | tf_op jit(solution)/shard_map/ppermute | solution.py:19
  34.3 0.2 fusion.15
  34.5 0.6 copy-done.26
  35.2 1.8 fusion.25
  37.0 0.2 exponential_reduce_fusion
  37.3 2.3 %bitcast_convert_fusion = (f32[4,2,128,128]{2,3,1,0:T(8,128)}, bf16[4,128,2,128]{3,1,2,0:T(8,128)(2,1)}) fusion(f32[4,2,128,384]{2,3,1,0:T(8,128)S(1)} %get-tuple-element.57, f32[4,2,128]{2,1,0:T(2,128)S(1)} %bitcast.114, bf16[128,4,128]{0,2,1:T(8,128)(2,1)} %bitcast.2, bf16[128,4,128]{0,2,1:T(8,128)(2,1)S(1)} %collective-permute-done.1, ...), kind=kOutput, calls=%fused_computation.43 | convolution fusion | flops 102891520 | bytes 2756608 | tf_op jit(solution)/shard_map/hgqk,khd->qhgd/dot_general | solution.py:115
  39.6 1.4 copy.110
  41.0 1.5 multiply_reduce_fusion
  42.5 1.0 copy.111
  43.5 0.4 convolution_bitcast_fusion.1
  43.9 0.5 copy-done.17
  44.5 1.5 fusion.1
  46.1 0.4 fusion.4
  46.5 0.8 fusion.23
  47.3 1.9 collective-permute-start.6
  49.3 1.3 collective-permute-start.7
  50.6 0.4 convolution_multiply_fusion
  51.0 0.7 fusion.24
  51.8 0.2 copy.124
  52.0 1.2 copy.125
  53.2 1.0 multiply_add_fusion
  54.3 1.1 multiply_reduce_fusion.2
  55.4 0.2 mul.406
  55.7 0.7 copy-done
  56.4 0.9 concatenate.40
  57.3 0.8 fusion.22
  58.2 1.9 collective-permute-start.8
  60.1 1.3 collective-permute-start.9
  61.4 1.8 copy.98
  63.2 1.9 multiply_reduce_fusion.1
  65.1 1.1 fusion.8
  66.2 0.1 multiply_add_fusion.1
  66.4 0.3 multiply_reduce_fusion.4
  66.7 0.1 copy.95
  66.9 0.2 fusion.10
  67.1 0.5 collective-permute-done.8
  67.6 4.3 %collective-permute-done.9 = f32[128,4,128]{0,2,1:T(8,128)} collective-permute-done((f32[128,4,128]{0,2,1:T(8,128)}, f32[128,4,128]{0,2,1:T(8,128)}, u32[]{:S(2)}, u32[]{:S(2)}) %collective-permute-start.9) | collective-permute-done | bytes 262176 | tf_op jit(solution)/shard_map/ppermute | solution.py:19
  71.9 1.1 fusion.7
  73.0 0.8 copy.100
  73.7 0.8 copy.99
  74.5 130.2 %all-reduce = (f32[128]{0:T(128)}, f32[128]{0:T(128)}) all-reduce(f32[128]{0:T(128)S(1)} %bitcast_reduce_fusion, f32[128]{0:T(128)S(1)} %bitcast_reduce_fusion.1), channel_id=1, replica_groups=mesh['fsdp'=8,'ctx'=32,'head'=4] {'fsdp','ctx','head'}, use_global_device_ids=true, to_apply=%region_8.9 | all-reduce | flops 256 | bytes 2048 | tf_op jit(solution)/shard_map/psum | solution.py:147
  (82 shorter events, 0.5 us)
Async XLA Ops:
  0.6 25.3 %copy-start.23 = (f32[128]{0:T(128)S(1)}, f32[128]{0:T(128)}, u32[]{:S(2)}) copy-start(f32[128]{0:T(128)} %param.13) | copy-start | bytes 1540
  0.6 12.5 %copy-start.25 = (s32[1,128]{1,0:T(1,128)S(1)}, s32[1,128]{1,0:T(1,128)}, u32[]{:S(2)}) copy-start(s32[1,128]{1,0:T(1,128)} %param.11) | copy-start | bytes 1540
  0.7 18.7 %copy-start.19 = (bf16[1,128,512]{2,1,0:T(8,128)(2,1)S(1)}, bf16[1,128,512]{2,1,0:T(8,128)(2,1)}, u32[]{:S(2)}) copy-start(bf16[1,128,512]{2,1,0:T(8,128)(2,1)} %param.9) | copy-start | bytes 393220
  0.7 25.9 %copy-start.9 = (bf16[1,128,1024]{2,1,0:T(8,128)(2,1)S(1)}, bf16[1,128,1024]{2,1,0:T(8,128)(2,1)}, u32[]{:S(2)}) copy-start(bf16[1,128,1024]{2,1,0:T(8,128)(2,1)} %param.7) | copy-start | bytes 786436
  2.3 24.9 %copy-start.3 = (f32[128,64]{1,0:T(8,128)}, f32[128,64]{1,0:T(8,128)S(1)}, u32[]{:S(2)}) copy-start(f32[128,64]{1,0:T(8,128)S(1)} %get-tuple-element.54) | copy-start | bytes 98308
  2.3 24.9 %copy-start.5 = (f32[128,64]{1,0:T(8,128)}, f32[128,64]{1,0:T(8,128)S(1)}, u32[]{:S(2)}) copy-start(f32[128,64]{1,0:T(8,128)S(1)} %get-tuple-element.55) | copy-start | bytes 98308
  3.3 23.3 %copy-start.12 = (bf16[128,4,64]{2,0,1:T(8,128)(2,1)}, bf16[128,4,64]{2,0,1:T(8,128)(2,1)S(1)}, u32[]{:S(2)}) copy-start(bf16[128,4,64]{2,0,1:T(8,128)(2,1)S(1)} %get-tuple-element.52) | copy-start | bytes 196612
  3.3 23.3 %copy-start.14 = (bf16[128,4,64]{2,0,1:T(8,128)(2,1)}, bf16[128,4,64]{2,0,1:T(8,128)(2,1)S(1)}, u32[]{:S(2)}) copy-start(bf16[128,4,64]{2,0,1:T(8,128)(2,1)S(1)} %get-tuple-element.53) | copy-start | bytes 196612
  3.3 23.6 %copy-start.21 = (f32[128]{0:T(128)S(1)}, f32[128]{0:T(128)}, u32[]{:S(2)}) copy-start(f32[128]{0:T(128)} %param.12) | copy-start | bytes 1540
  3.4 31.1 %collective-permute-start.4 = (bf16[128,4,128]{2,0,1:T(8,128)(2,1)S(1)}, bf16[128,4,128]{2,0,1:T(8,128)(2,1)S(1)}, u32[]{:S(2)}, u32[]{:S(2)}) collective-permute-start(bf16[128,4,128]{2,0,1:T(8,128)(2,1)S(1)} %pad_maximum_fusion.3), channel_id=1, source_target_pairs={{0,8},{4,12},{8,16},{12,20},{16,24},{20,28},{24,32},{28,36},{32,40... | collective-permute-start | bytes 393224 | tf_op jit(solution)/shard_map/ppermute | solution.py:19
  8.3 26.2 %collective-permute-start.5 = (bf16[128,4,128]{2,0,1:T(8,128)(2,1)S(1)}, bf16[128,4,128]{2,0,1:T(8,128)(2,1)S(1)}, u32[]{:S(2)}, u32[]{:S(2)}) collective-permute-start(bf16[128,4,128]{2,0,1:T(8,128)(2,1)S(1)} %pad_maximum_fusion.3), channel_id=1, source_target_pairs={{0,4},{4,8},{8,12},{12,16},{16,20},{20,24},{24,28},{28,32},{32,36}... | collective-permute-start | bytes 393224 | tf_op jit(solution)/shard_map/ppermute | solution.py:19
  13.1 17.4 %collective-permute-start.2 = (s32[128]{0:T(128)S(1)}, s32[128]{0:T(128)S(1)}, u32[]{:S(2)}, u32[]{:S(2)}) collective-permute-start(s32[128]{0:T(128)S(1)} %bitcast.119), channel_id=1, source_target_pairs={{0,8},{4,12},{8,16},{12,20},{16,24},{20,28},{24,32},{28,36},{32,40... | collective-permute-start | bytes 1544 | tf_op jit(solution)/shard_map/ppermute | solution.py:19
  17.1 17.1 %collective-permute-start.3 = (s32[128]{0:T(128)S(1)}, s32[128]{0:T(128)S(1)}, u32[]{:S(2)}, u32[]{:S(2)}) collective-permute-start(s32[128]{0:T(128)S(1)} %bitcast.120), channel_id=1, source_target_pairs={{0,4},{4,8},{8,12},{12,16},{16,20},{20,24},{24,28},{28,32},{32,36}... | collective-permute-start | bytes 1544 | tf_op jit(solution)/shard_map/ppermute | solution.py:19
  20.1 17.1 %collective-permute-start = (bf16[128,4,128]{0,2,1:T(8,128)(2,1)}, bf16[128,4,128]{0,2,1:T(8,128)(2,1)}, u32[]{:S(2)}, u32[]{:S(2)}) collective-permute-start(bf16[128,4,128]{0,2,1:T(8,128)(2,1)} %bitcast.2), channel_id=1, source_target_pairs={{0,8},{4,12},{8,16},{12,20},{16,24},{20,28},{24,32},{28,36},{32,40... | collective-permute-start | bytes 393224 | tf_op jit(solution)/shard_map/ppermute | solution.py:19
  27.0 2.4 %copy-start.7 = (f32[128,8]{1,0:T(8,128)}, f32[128,8]{1,0:T(8,128)S(1)}, u32[]{:S(2)}) copy-start(f32[128,8]{1,0:T(8,128)S(1)} %add_rsqrt_fusion) | copy-start | bytes 12292
  27.2 1.8 copy-start.18
  30.5 6.7 %collective-permute-start.1 = (bf16[128,4,128]{0,2,1:T(8,128)(2,1)}, bf16[128,4,128]{0,2,1:T(8,128)(2,1)S(1)}, u32[]{:S(2)}, u32[]{:S(2)}) collective-permute-start(bf16[128,4,128]{0,2,1:T(8,128)(2,1)} %bitcast.2), channel_id=1, source_target_pairs={{0,4},{4,8},{8,12},{12,16},{16,20},{20,24},{24,28},{28,32},{32,36}... | collective-permute-start | bytes 393224 | tf_op jit(solution)/shard_map/ppermute | solution.py:19
  34.5 0.7 copy-start.26
  34.5 0.7 copy-start.28
  37.2 2.3 %copy-start.16 = (bf16[128,4,128]{0,2,1:T(8,128)(2,1)}, bf16[128,4,128]{0,2,1:T(8,128)(2,1)S(1)}, u32[]{:S(2)}) copy-start(bf16[128,4,128]{0,2,1:T(8,128)(2,1)S(1)} %collective-permute-done.1) | copy-start | bytes 393220
  43.5 0.9 copy-start.17
  44.5 1.5 copy-start.10
  44.5 1.5 copy-start.11
  46.0 4.5 %copy-start.13 = (bf16[128,4,64]{2,0,1:T(8,128)(2,1)S(1)}, bf16[128,4,64]{2,0,1:T(8,128)(2,1)}, u32[]{:S(2)}) copy-start(bf16[128,4,64]{2,0,1:T(8,128)(2,1)} %copy-done.12) | copy-start | bytes 196612
  46.0 4.5 %copy-start.15 = (bf16[128,4,64]{2,0,1:T(8,128)(2,1)S(1)}, bf16[128,4,64]{2,0,1:T(8,128)(2,1)}, u32[]{:S(2)}) copy-start(bf16[128,4,64]{2,0,1:T(8,128)(2,1)} %copy-done.14) | copy-start | bytes 196612
  46.1 4.5 %copy-start.27 = (bf16[128,4,128]{2,0,1:T(8,128)(2,1)S(1)}, bf16[128,4,128]{2,0,1:T(8,128)(2,1)}, u32[]{:S(2)}) copy-start(bf16[128,4,128]{2,0,1:T(8,128)(2,1)} %copy-done.26) | copy-start | bytes 393220
  46.1 4.5 %copy-start.29 = (bf16[128,4,128]{2,0,1:T(8,128)(2,1)S(1)}, bf16[128,4,128]{2,0,1:T(8,128)(2,1)}, u32[]{:S(2)}) copy-start(bf16[128,4,128]{2,0,1:T(8,128)(2,1)} %copy-done.28) | copy-start | bytes 393220
  47.3 17.7 %collective-permute-start.6 = (f32[128,4,128]{2,0,1:T(8,128)}, f32[128,4,128]{2,0,1:T(8,128)}, u32[]{:S(2)}, u32[]{:S(2)}) collective-permute-start(f32[128,4,128]{2,0,1:T(8,128)} %get-tuple-element.42), channel_id=1, source_target_pairs={{4,0},{8,4},{12,8},{16,12},{20,16},{24,20},{28,24},{32,28},{36,32}... | collective-permute-start | bytes 786440 | tf_op jit(solution)/shard_map/ppermute | solution.py:19
  49.3 15.8 %collective-permute-start.7 = (f32[128,4,128]{2,0,1:T(8,128)}, f32[128,4,128]{2,0,1:T(8,128)}, u32[]{:S(2)}, u32[]{:S(2)}) collective-permute-start(f32[128,4,128]{2,0,1:T(8,128)} %get-tuple-element.43), channel_id=1, source_target_pairs={{8,0},{12,4},{16,8},{20,12},{24,16},{28,20},{32,24},{36,28},{40,32... | collective-permute-start | bytes 786440 | tf_op jit(solution)/shard_map/ppermute | solution.py:19
  52.0 2.2 %copy-start.22 = (f32[128]{0:T(128)S(1)}, f32[128]{0:T(128)}, u32[]{:S(2)}) copy-start(f32[128]{0:T(128)} %param.12) | copy-start | bytes 1540
  53.2 1.0 copy-start.8
  55.4 1.0 copy-start
  55.7 7.5 %copy-start.1 = (f32[1,128,1024]{2,1,0:T(8,128)S(1)}, f32[1,128,1024]{2,1,0:T(8,128)}, u32[]{:S(2)}) copy-start(f32[1,128,1024]{2,1,0:T(8,128)} %mul.390) | copy-start | bytes 1572868
  57.3 5.9 %copy-start.2 = (f32[1,128,1024]{2,1,0:T(8,128)S(1)}, f32[1,128,1024]{2,1,0:T(8,128)}, u32[]{:S(2)}) copy-start(f32[1,128,1024]{2,1,0:T(8,128)} %concatenate.40) | copy-start | bytes 1572868
  58.2 9.4 %collective-permute-start.8 = (f32[128,4,128]{0,2,1:T(8,128)}, f32[128,4,128]{0,2,1:T(8,128)}, u32[]{:S(2)}, u32[]{:S(2)}) collective-permute-start(f32[128,4,128]{0,2,1:T(8,128)} %get-tuple-element.40), channel_id=1, source_target_pairs={{4,0},{8,4},{12,8},{16,12},{20,16},{24,20},{28,24},{32,28},{36,32}... | collective-permute-start | bytes 786440 | tf_op jit(solution)/shard_map/ppermute | solution.py:19
  60.1 11.8 %collective-permute-start.9 = (f32[128,4,128]{0,2,1:T(8,128)}, f32[128,4,128]{0,2,1:T(8,128)}, u32[]{:S(2)}, u32[]{:S(2)}) collective-permute-start(f32[128,4,128]{0,2,1:T(8,128)} %get-tuple-element.41), channel_id=1, source_target_pairs={{8,0},{12,4},{16,8},{20,12},{24,16},{28,20},{32,24},{36,28},{40,32... | collective-permute-start | bytes 786440 | tf_op jit(solution)/shard_map/ppermute | solution.py:19
  63.2 3.0 %copy-start.4 = (f32[128,64]{1,0:T(8,128)S(1)}, f32[128,64]{1,0:T(8,128)}, u32[]{:S(2)}) copy-start(f32[128,64]{1,0:T(8,128)} %copy-done.3) | copy-start | bytes 98308
  63.2 3.0 %copy-start.6 = (f32[128,64]{1,0:T(8,128)S(1)}, f32[128,64]{1,0:T(8,128)}, u32[]{:S(2)}) copy-start(f32[128,64]{1,0:T(8,128)} %copy-done.5) | copy-start | bytes 98308
  65.1 1.3 copy-start.24
  66.2 0.7 copy-start.20
where the time goes:
time: 206 us; the launch traced here: 205 us
  blocking collectives  130 us (63%)
  starting transfers between devices  31.9 us (15%)
  local copies, waits for them, and re-layouts  18.5 us (9%)
  other arithmetic  11.1 us (5%)
  matrix products  6.85 us (3%)
  waiting for transfers between devices  4.8 us (2%)
    psum x1, blocking collectives, body(): q_total, k_total = lax.psum((q_term, k_term), ('fsdp', 'ctx', 'head'))  130 us
    ppermute x10, starting transfers between devices, passed_along(): return lax.ppermute(value, axis, pairs)  31.9 us
    unnamed x69, local copies, waits for them, and re-layouts  10.1 us
    ppermute x10, waiting for transfers between devices, passed_along(): return lax.ppermute(value, axis, pairs)  4.8 us
  transfers between devices with their start and end apart: 10, of which 2 were waited for; matrix products, arithmetic and copies ran while one was open for 10% of the time, Pallas kernels for 0%

commit v1 on v0

--- a/solution.py
+++ b/solution.py
@@ -17,6 +17,16 @@
     devices = lax.axis_size(axis)
     pairs = [(i, i + by) for i in range(devices) if 0 <= i + by < devices]
     return lax.ppermute(value, axis, pairs)
+
+
+def butterfly_sum(value, axis):
+    devices = lax.axis_size(axis)
+    stride = 1
+    while stride < devices:
+        pairs = [(i, i ^ stride) for i in range(devices)]
+        value = value + lax.ppermute(value, axis, pairs)
+        stride *= 2
+    return value
 
 
 def rotate(values, positions):
@@ -144,7 +154,10 @@
         grad_queries.reshape(row_count, qheads, HEAD_WIDTH), q_unit, q_inv, q_gain, positions
     )
     dk_grad, k_term = restore(key_own, k_unit, k_inv, k_gain, positions)
-    q_total, k_total = lax.psum((q_term, k_term), ("fsdp", "ctx", "head"))
+    gain_terms = jnp.concatenate([q_term, k_term])
+    for axis in ("head", "ctx", "fsdp"):
+        gain_terms = butterfly_sum(gain_terms, axis)
+    q_total, k_total = gain_terms[:HEAD_WIDTH], gain_terms[HEAD_WIDTH:]
     return (
         attended.reshape(1, row_count, -1),
         dq_grad.astype(jnp.bfloat16).reshape(1, row_count, -1),

time: 206 us -> 144 us (0.70)
  the two profiles are of different devices: /device:TPU:1 before, /device:TPU:54 now
where the time goes in v1:
time: 144 us; the launch traced here: 143 us
  starting transfers between devices  83.1 us (58%)
  waiting for transfers between devices  22.7 us (16%)
  local copies, waits for them, and re-layouts  18.2 us (13%)
  other arithmetic  10.3 us (7%)
  matrix products  6.89 us (5%)
  between operations  1.5 us (1%)
    ppermute x10, starting transfers between devices, butterfly_sum(): value = value + lax.ppermute(value, axis, pairs)  55.2 us
    ppermute x10, starting transfers between devices, passed_along(): return lax.ppermute(value, axis, pairs)  27.9 us
    ppermute x10, waiting for transfers between devices, butterfly_sum(): value = value + lax.ppermute(value, axis, pairs)  22.1 us
    unnamed x71, local copies, waits for them, and re-layouts  8.49 us
  transfers between devices with their start and end apart: 20, of which 11 were waited for; matrix products, arithmetic and copies ran while one was open for 15% of the time, Pallas kernels for 0%

profile of v1, /device:TPU:54, one launch (start us, length us, event | category | flops | bytes accessed | tf_op | source)
XLA Modules:
  0.0 142.7 jit_solution(6266584117287819680)
XLA Ops:
  0.7 1.1 copy.80
  2.3 0.8 multiply_multiply_fusion.1
  3.4 4.3 %collective-permute-start.4 = (bf16[128,4,128]{2,0,1:T(8,128)(2,1)S(1)}, bf16[128,4,128]{2,0,1:T(8,128)(2,1)S(1)}, u32[]{:S(2)}, u32[]{:S(2)}) collective-permute-start(bf16[128,4,128]{2,0,1:T(8,128)(2,1)S(1)} %pad_maximum_fusion.3), channel_id=1, source_target_pairs={{0,8},{4,12},{8,16},{12,20},{16,24},{20,28},{24,32},{28,36},{32,40... | collective-permute-start | bytes 393224 | tf_op jit(solution)/shard_map/ppermute | solution.py:19
  7.7 1.5 %collective-permute-start.5 = (bf16[128,4,128]{2,0,1:T(8,128)(2,1)S(1)}, bf16[128,4,128]{2,0,1:T(8,128)(2,1)S(1)}, u32[]{:S(2)}, u32[]{:S(2)}) collective-permute-start(bf16[128,4,128]{2,0,1:T(8,128)(2,1)S(1)} %pad_maximum_fusion.3), channel_id=1, source_target_pairs={{0,4},{4,8},{8,12},{12,16},{16,20},{20,24},{24,28},{28,32},{32,36}... | collective-permute-start | bytes 393224 | tf_op jit(solution)/shard_map/ppermute | solution.py:19
  9.2 4.7 %collective-permute-start.2 = (s32[128]{0:T(128)S(1)}, s32[128]{0:T(128)S(1)}, u32[]{:S(2)}, u32[]{:S(2)}) collective-permute-start(s32[128]{0:T(128)S(1)} %bitcast.119), channel_id=1, source_target_pairs={{0,8},{4,12},{8,16},{12,20},{16,24},{20,28},{24,32},{28,36},{32,40... | collective-permute-start | bytes 1544 | tf_op jit(solution)/shard_map/ppermute | solution.py:19
  14.0 4.1 %collective-permute-start.3 = (s32[128]{0:T(128)S(1)}, s32[128]{0:T(128)S(1)}, u32[]{:S(2)}, u32[]{:S(2)}) collective-permute-start(s32[128]{0:T(128)S(1)} %bitcast.120), channel_id=1, source_target_pairs={{0,4},{4,8},{8,12},{12,16},{16,20},{20,24},{24,28},{28,32},{32,36}... | collective-permute-start | bytes 1544 | tf_op jit(solution)/shard_map/ppermute | solution.py:19
  18.1 0.8 copy.79
  18.8 6.1 %collective-permute-start = (bf16[128,4,128]{0,2,1:T(8,128)(2,1)}, bf16[128,4,128]{0,2,1:T(8,128)(2,1)}, u32[]{:S(2)}, u32[]{:S(2)}) collective-permute-start(bf16[128,4,128]{0,2,1:T(8,128)(2,1)} %bitcast.2), channel_id=1, source_target_pairs={{0,8},{4,12},{8,16},{12,20},{16,24},{20,28},{24,32},{28,36},{32,40... | collective-permute-start | bytes 393224 | tf_op jit(solution)/shard_map/ppermute | solution.py:19
  25.0 0.6 broadcast_bitcast_fusion.1
  26.5 0.7 copy.83
  27.3 0.7 copy.82
  28.6 0.9 mul.390
  29.5 1.9 %collective-permute-start.1 = (bf16[128,4,128]{0,2,1:T(8,128)(2,1)}, bf16[128,4,128]{0,2,1:T(8,128)(2,1)S(1)}, u32[]{:S(2)}, u32[]{:S(2)}) collective-permute-start(bf16[128,4,128]{0,2,1:T(8,128)(2,1)} %bitcast.2), channel_id=1, source_target_pairs={{0,4},{4,8},{8,12},{12,16},{16,20},{20,24},{24,28},{28,32},{32,36}... | collective-permute-start | bytes 393224 | tf_op jit(solution)/shard_map/ppermute | solution.py:19
  31.7 0.6 copy-done.27
  32.4 1.8 %fusion.27 = (f32[4,2,128]{2,1,0:T(2,128)S(1)}, f32[4,2,128,384]{2,3,1,0:T(8,128)S(1)}) fusion(bf16[128,4,2,64]{3,0,2,1:T(8,128)(2,1)} %bitcast.108, bf16[128,4,2,64]{3,0,2,1:T(8,128)(2,1)} %bitcast.110, bf16[128,4,64]{2,0,1:T(8,128)(2,1)} %copy-done.15, bf16[128,4,64]{2,0,1:T(8,128)(2,1)} %copy-done.13, bf16[128,4,128]{2,0,1:T(8,128)(2,1)} %copy-done.29, ...), kind=kOutput, calls=%fused_computation.84 | convolution fusion | flops 103939072 | bytes 2281472 | tf_op jit(solution)/shard_map/qhgd,khd->hgqk/dot_general | solution.py:83
  34.4 2.4 %bitcast_convert_fusion = (f32[4,2,128,128]{2,3,1,0:T(8,128)}, bf16[4,128,2,128]{3,1,2,0:T(8,128)(2,1)}) fusion(f32[4,2,128,384]{2,3,1,0:T(8,128)S(1)} %get-tuple-element.57, f32[4,2,128]{2,1,0:T(2,128)S(1)} %bitcast.114, bf16[128,4,128]{0,2,1:T(8,128)(2,1)} %bitcast.2, bf16[128,4,128]{0,2,1:T(8,128)(2,1)S(1)} %collective-permute-done.1, ...), kind=kOutput, calls=%fused_computation.43 | convolution fusion | flops 102891520 | bytes 2756608 | tf_op jit(solution)/shard_map/hgqk,khd->qhgd/dot_general | solution.py:125
  36.8 1.4 copy.110
  38.2 1.6 %multiply_reduce_fusion = f32[4,2,128]{1,0,2:T(4,128)} fusion(f32[4,2,128,128]{3,1,0,2:T(2,128)S(1)} %copy.110, bf16[128,4,2,128]{3,2,1,0:T(2,128)(2,1)S(1)} %reshape_squeeze.7), kind=kLoop, calls=%fused_computation.16 | loop fusion | flops 392192 | bytes 790528
  39.7 1.0 copy.111
  40.8 0.4 convolution_bitcast_fusion.1
  41.2 0.5 copy-done.18
  41.7 1.5 %fusion.1 = bf16[4,2,128,384]{2,3,1,0:T(8,128)(2,1)S(1)} fusion(bf16[128,4,2,128]{0,3,2,1:T(8,128)(2,1)S(1)} %copy.97, f32[4,2,128,384]{2,3,1,0:T(8,128)S(1)} %get-tuple-element.57, f32[4,2,128]{2,1,0:T(2,128)S(1)} %copy.111, f32[4,2,128]{2,1,0:T(2,128)S(1)} %bitcast.116, bf16[128,4,128]{0,2,1:T(8,128)(2,1)} %bitcast.2, ...), kind=kOutput, calls=%fused_computation.2 | convolution fusion | flops 103415808 | bytes 3022848 | tf_op jit(solution)/shard_map/qhgd,khd->hgqk/dot_general | solution.py:131
  43.3 0.4 fusion.4
  43.8 0.8 fusion.24
  44.6 1.3 collective-permute-start.6
  45.9 1.3 collective-permute-start.7
  47.2 0.4 convolution_multiply_fusion
  47.6 0.7 fusion.25
  48.6 1.2 copy.125
  49.9 1.0 multiply_add_fusion
  50.9 1.1 multiply_reduce_fusion.2
  52.3 0.9 mul.407
  53.2 0.9 concatenate.43
  54.0 0.8 fusion.23
  54.9 1.3 collective-permute-start.8
  56.2 1.4 collective-permute-start.9
  57.6 2.0 %multiply_reduce_fusion.1 = (f32[1024]{0:T(1024)S(1)}, bf16[1,128,1024]{2,1,0:T(8,128)(2,1)}) fusion(f32[1,128,1024]{2,1,0:T(8,128)} %concatenate.43, f32[1,128,1024]{2,1,0:T(8,128)S(1)} %copy-done.1, bf16[1,128,1024]{2,1,0:T(8,128)(2,1)} %param.7, f32[1,128,1024]{2,1,0:T(8,128)S(1)} %copy-done.2, f32[1024]{0:T(1024)S(1)} %broadcast_bitcast_fusion), kind=kLoop, calls=%fused_computation.17 | loop fusion | flops 1178624 | bytes 2105344 | tf_op jit(solution)/shard_map/reduce_sum | solution.py:69
  59.6 0.6 collective-permute-done.7
  60.3 1.1 fusion.8
  61.5 0.3 multiply_reduce_fusion.4
  62.3 2.6 %collective-permute-start.10 = (f32[256]{0:T(256)S(1)}, f32[256]{0:T(256)S(1)}, u32[]{:S(2)}, u32[]{:S(2)}) collective-permute-start(f32[256]{0:T(256)S(1)} %pad_maximum_fusion.6), channel_id=1, source_target_pairs={{0,1},{1,0},{2,3},{3,2},{4,5},{5,4},{6,7},{7,6},{8,9},{9,8},{10,11... | collective-permute-start | bytes 3080 | tf_op jit(solution)/shard_map/ppermute | solution.py:27
  64.9 2.9 %collective-permute-done.10 = f32[256]{0:T(256)S(1)} collective-permute-done((f32[256]{0:T(256)S(1)}, f32[256]{0:T(256)S(1)}, u32[]{:S(2)}, u32[]{:S(2)}) %collective-permute-start.10) | collective-permute-done | bytes 1056 | tf_op jit(solution)/shard_map/ppermute | solution.py:27
  67.8 4.0 %collective-permute-start.11 = (f32[256]{0:T(256)S(1)}, f32[256]{0:T(256)S(1)}, u32[]{:S(2)}, u32[]{:S(2)}) collective-permute-start(f32[256]{0:T(256)S(1)} %fusion.22), channel_id=1, source_target_pairs={{0,2},{1,3},{2,0},{3,1},{4,6},{5,7},{6,4},{7,5},{8,10},{9,11},{10,... | collective-permute-start | bytes 3080 | tf_op jit(solution)/shard_map/ppermute | solution.py:27
  71.8 2.3 %collective-permute-done.11 = f32[256]{0:T(256)S(1)} collective-permute-done((f32[256]{0:T(256)S(1)}, f32[256]{0:T(256)S(1)}, u32[]{:S(2)}, u32[]{:S(2)}) %collective-permute-start.11) | collective-permute-done | bytes 1056 | tf_op jit(solution)/shard_map/ppermute | solution.py:27
  74.1 2.4 %collective-permute-start.12 = (f32[256]{0:T(256)S(1)}, f32[256]{0:T(256)S(1)}, u32[]{:S(2)}, u32[]{:S(2)}) collective-permute-start(f32[256]{0:T(256)S(1)} %add.129), channel_id=1, source_target_pairs={{0,4},{4,0},{8,12},{12,8},{16,20},{20,16},{24,28},{28,24},{32,36},... | collective-permute-start | bytes 3080 | tf_op jit(solution)/shard_map/ppermute | solution.py:27
  76.5 0.8 collective-permute-done.12
  77.3 7.1 %collective-permute-start.13 = (f32[256]{0:T(256)S(1)}, f32[256]{0:T(256)S(1)}, u32[]{:S(2)}, u32[]{:S(2)}) collective-permute-start(f32[256]{0:T(256)S(1)} %add.130), channel_id=1, source_target_pairs={{0,8},{4,12},{8,0},{12,4},{16,24},{20,28},{24,16},{28,20},{32,40},... | collective-permute-start | bytes 3080 | tf_op jit(solution)/shard_map/ppermute | solution.py:27
  84.5 1.5 %collective-permute-done.13 = f32[256]{0:T(256)S(1)} collective-permute-done((f32[256]{0:T(256)S(1)}, f32[256]{0:T(256)S(1)}, u32[]{:S(2)}, u32[]{:S(2)}) %collective-permute-start.13) | collective-permute-done | bytes 1056 | tf_op jit(solution)/shard_map/ppermute | solution.py:27
  86.0 6.1 %collective-permute-start.14 = (f32[256]{0:T(256)S(1)}, f32[256]{0:T(256)S(1)}, u32[]{:S(2)}, u32[]{:S(2)}) collective-permute-start(f32[256]{0:T(256)S(1)} %add.131), channel_id=1, source_target_pairs={{0,16},{4,20},{8,24},{12,28},{16,0},{20,4},{24,8},{28,12},{32,48},... | collective-permute-start | bytes 3080 | tf_op jit(solution)/shard_map/ppermute | solution.py:27
  92.1 1.5 %collective-permute-done.14 = f32[256]{0:T(256)S(1)} collective-permute-done((f32[256]{0:T(256)S(1)}, f32[256]{0:T(256)S(1)}, u32[]{:S(2)}, u32[]{:S(2)}) %collective-permute-start.14) | collective-permute-done | bytes 1056 | tf_op jit(solution)/shard_map/ppermute | solution.py:27
  93.6 11.0 %collective-permute-start.15 = (f32[256]{0:T(256)S(1)}, f32[256]{0:T(256)S(1)}, u32[]{:S(2)}, u32[]{:S(2)}) collective-permute-start(f32[256]{0:T(256)S(1)} %add.132), channel_id=1, source_target_pairs={{0,32},{4,36},{8,40},{12,44},{16,48},{20,52},{24,56},{28,60},{32,0... | collective-permute-start | bytes 3080 | tf_op jit(solution)/shard_map/ppermute | solution.py:27
  104.7 1.5 %collective-permute-done.15 = f32[256]{0:T(256)S(1)} collective-permute-done((f32[256]{0:T(256)S(1)}, f32[256]{0:T(256)S(1)}, u32[]{:S(2)}, u32[]{:S(2)}) %collective-permute-start.15) | collective-permute-done | bytes 1056 | tf_op jit(solution)/shard_map/ppermute | solution.py:27
  106.2 12.2 %collective-permute-start.16 = (f32[256]{0:T(256)S(1)}, f32[256]{0:T(256)S(1)}, u32[]{:S(2)}, u32[]{:S(2)}) collective-permute-start(f32[256]{0:T(256)S(1)} %add.133), channel_id=1, source_target_pairs={{0,64},{4,68},{8,72},{12,76},{16,80},{20,84},{24,88},{28,92},{32,9... | collective-permute-start | bytes 3080 | tf_op jit(solution)/shard_map/ppermute | solution.py:27
  118.4 2.0 %collective-permute-done.16 = f32[256]{0:T(256)S(1)} collective-permute-done((f32[256]{0:T(256)S(1)}, f32[256]{0:T(256)S(1)}, u32[]{:S(2)}, u32[]{:S(2)}) %collective-permute-start.16) | collective-permute-done | bytes 1056 | tf_op jit(solution)/shard_map/ppermute | solution.py:27
  120.4 3.8 %collective-permute-start.17 = (f32[256]{0:T(256)S(1)}, f32[256]{0:T(256)S(1)}, u32[]{:S(2)}, u32[]{:S(2)}) collective-permute-start(f32[256]{0:T(256)S(1)} %add.134), channel_id=1, source_target_pairs={{0,128},{128,0},{256,384},{384,256},{512,640},{640,512},{768,896},... | collective-permute-start | bytes 3080 | tf_op jit(solution)/shard_map/ppermute | solution.py:27
  124.2 5.6 %collective-permute-done.17 = f32[256]{0:T(256)S(1)} collective-permute-done((f32[256]{0:T(256)S(1)}, f32[256]{0:T(256)S(1)}, u32[]{:S(2)}, u32[]{:S(2)}) %collective-permute-start.17) | collective-permute-done | bytes 1056 | tf_op jit(solution)/shard_map/ppermute | solution.py:27
  129.8 2.7 %collective-permute-start.18 = (f32[256]{0:T(256)S(1)}, f32[256]{0:T(256)S(1)}, u32[]{:S(2)}, u32[]{:S(2)}) collective-permute-start(f32[256]{0:T(256)S(1)} %add.135), channel_id=1, source_target_pairs={{0,256},{128,384},{256,0},{384,128},{512,768},{640,896},{768,512},... | collective-permute-start | bytes 3080 | tf_op jit(solution)/shard_map/ppermute | solution.py:27
  132.5 0.9 copy.98
  133.4 1.9 %collective-permute-done.18 = f32[256]{0:T(256)S(1)} collective-permute-done((f32[256]{0:T(256)S(1)}, f32[256]{0:T(256)S(1)}, u32[]{:S(2)}, u32[]{:S(2)}) %collective-permute-start.18) | collective-permute-done | bytes 1056 | tf_op jit(solution)/shard_map/ppermute | solution.py:27
  135.2 3.3 %collective-permute-start.19 = (f32[256]{0:T(256)S(1)}, f32[256]{0:T(256)S(1)}, u32[]{:S(2)}, u32[]{:S(2)}) collective-permute-start(f32[256]{0:T(256)S(1)} %add.136), channel_id=1, source_target_pairs={{0,512},{128,640},{256,768},{384,896},{512,0},{640,128},{768,256},... | collective-permute-start | bytes 3080 | tf_op jit(solution)/shard_map/ppermute | solution.py:27
  138.6 0.8 copy.100
  139.4 0.8 copy.99
  140.2 2.0 %collective-permute-done.19 = f32[256]{0:T(256)S(1)} collective-permute-done((f32[256]{0:T(256)S(1)}, f32[256]{0:T(256)S(1)}, u32[]{:S(2)}, u32[]{:S(2)}) %collective-permute-start.19) | collective-permute-done | bytes 1056 | tf_op jit(solution)/shard_map/ppermute | solution.py:27
  142.2 0.5 fusion.26
  (115 shorter events, 3.9 us)
Async XLA Ops:
  0.6 24.3 %copy-start.24 = (f32[128]{0:T(128)S(1)}, f32[128]{0:T(128)}, u32[]{:S(2)}) copy-start(f32[128]{0:T(128)} %param.13) | copy-start | bytes 1540
  0.6 8.6 %copy-start.26 = (s32[1,128]{1,0:T(1,128)S(1)}, s32[1,128]{1,0:T(1,128)}, u32[]{:S(2)}) copy-start(s32[1,128]{1,0:T(1,128)} %param.11) | copy-start | bytes 1540
  0.7 17.4 %copy-start.20 = (bf16[1,128,512]{2,1,0:T(8,128)(2,1)S(1)}, bf16[1,128,512]{2,1,0:T(8,128)(2,1)}, u32[]{:S(2)}) copy-start(bf16[1,128,512]{2,1,0:T(8,128)(2,1)} %param.9) | copy-start | bytes 393220
  0.7 24.9 %copy-start.9 = (bf16[1,128,1024]{2,1,0:T(8,128)(2,1)S(1)}, bf16[1,128,1024]{2,1,0:T(8,128)(2,1)}, u32[]{:S(2)}) copy-start(bf16[1,128,1024]{2,1,0:T(8,128)(2,1)} %param.7) | copy-start | bytes 786436
  2.3 23.9 %copy-start.3 = (f32[128,64]{1,0:T(8,128)}, f32[128,64]{1,0:T(8,128)S(1)}, u32[]{:S(2)}) copy-start(f32[128,64]{1,0:T(8,128)S(1)} %get-tuple-element.54) | copy-start | bytes 98308
  2.3 23.9 %copy-start.5 = (f32[128,64]{1,0:T(8,128)}, f32[128,64]{1,0:T(8,128)S(1)}, u32[]{:S(2)}) copy-start(f32[128,64]{1,0:T(8,128)S(1)} %get-tuple-element.55) | copy-start | bytes 98308
  3.3 21.7 %copy-start.13 = (bf16[128,4,64]{2,0,1:T(8,128)(2,1)}, bf16[128,4,64]{2,0,1:T(8,128)(2,1)S(1)}, u32[]{:S(2)}) copy-start(bf16[128,4,64]{2,0,1:T(8,128)(2,1)S(1)} %get-tuple-element.50) | copy-start | bytes 196612
  3.3 21.7 %copy-start.15 = (bf16[128,4,64]{2,0,1:T(8,128)(2,1)}, bf16[128,4,64]{2,0,1:T(8,128)(2,1)S(1)}, u32[]{:S(2)}) copy-start(bf16[128,4,64]{2,0,1:T(8,128)(2,1)S(1)} %get-tuple-element.51) | copy-start | bytes 196612
  3.3 22.7 %copy-start.22 = (f32[128]{0:T(128)S(1)}, f32[128]{0:T(128)}, u32[]{:S(2)}) copy-start(f32[128]{0:T(128)} %param.12) | copy-start | bytes 1540
  3.4 28.2 %collective-permute-start.4 = (bf16[128,4,128]{2,0,1:T(8,128)(2,1)S(1)}, bf16[128,4,128]{2,0,1:T(8,128)(2,1)S(1)}, u32[]{:S(2)}, u32[]{:S(2)}) collective-permute-start(bf16[128,4,128]{2,0,1:T(8,128)(2,1)S(1)} %pad_maximum_fusion.3), channel_id=1, source_target_pairs={{0,8},{4,12},{8,16},{12,20},{16,24},{20,28},{24,32},{28,36},{32,40... | collective-permute-start | bytes 393224 | tf_op jit(solution)/shard_map/ppermute | solution.py:19
  7.7 24.0 %collective-permute-start.5 = (bf16[128,4,128]{2,0,1:T(8,128)(2,1)S(1)}, bf16[128,4,128]{2,0,1:T(8,128)(2,1)S(1)}, u32[]{:S(2)}, u32[]{:S(2)}) collective-permute-start(bf16[128,4,128]{2,0,1:T(8,128)(2,1)S(1)} %pad_maximum_fusion.3), channel_id=1, source_target_pairs={{0,4},{4,8},{8,12},{12,16},{16,20},{20,24},{24,28},{28,32},{32,36}... | collective-permute-start | bytes 393224 | tf_op jit(solution)/shard_map/ppermute | solution.py:19
  9.2 20.3 %collective-permute-start.2 = (s32[128]{0:T(128)S(1)}, s32[128]{0:T(128)S(1)}, u32[]{:S(2)}, u32[]{:S(2)}) collective-permute-start(s32[128]{0:T(128)S(1)} %bitcast.119), channel_id=1, source_target_pairs={{0,8},{4,12},{8,16},{12,20},{16,24},{20,28},{24,32},{28,36},{32,40... | collective-permute-start | bytes 1544 | tf_op jit(solution)/shard_map/ppermute | solution.py:19
  14.0 17.5 %collective-permute-start.3 = (s32[128]{0:T(128)S(1)}, s32[128]{0:T(128)S(1)}, u32[]{:S(2)}, u32[]{:S(2)}) collective-permute-start(s32[128]{0:T(128)S(1)} %bitcast.120), channel_id=1, source_target_pairs={{0,4},{4,8},{8,12},{12,16},{16,20},{20,24},{24,28},{28,32},{32,36}... | collective-permute-start | bytes 1544 | tf_op jit(solution)/shard_map/ppermute | solution.py:19
  18.8 15.6 %collective-permute-start = (bf16[128,4,128]{0,2,1:T(8,128)(2,1)}, bf16[128,4,128]{0,2,1:T(8,128)(2,1)}, u32[]{:S(2)}, u32[]{:S(2)}) collective-permute-start(bf16[128,4,128]{0,2,1:T(8,128)(2,1)} %bitcast.2), channel_id=1, source_target_pairs={{0,8},{4,12},{8,16},{12,20},{16,24},{20,28},{24,32},{28,36},{32,40... | collective-permute-start | bytes 393224 | tf_op jit(solution)/shard_map/ppermute | solution.py:19
  26.0 2.4 %copy-start.7 = (f32[128,8]{1,0:T(8,128)}, f32[128,8]{1,0:T(8,128)S(1)}, u32[]{:S(2)}) copy-start(f32[128,8]{1,0:T(8,128)S(1)} %add_rsqrt_fusion) | copy-start | bytes 12292
  26.2 1.8 %copy-start.19 = (bf16[1,128,1024]{2,1,0:T(8,128)(2,1)S(1)}, bf16[1,128,1024]{2,1,0:T(8,128)(2,1)}, u32[]{:S(2)}) copy-start(bf16[1,128,1024]{2,1,0:T(8,128)(2,1)} %param.10) | copy-start | bytes 786436
  29.5 4.9 %collective-permute-start.1 = (bf16[128,4,128]{0,2,1:T(8,128)(2,1)}, bf16[128,4,128]{0,2,1:T(8,128)(2,1)S(1)}, u32[]{:S(2)}, u32[]{:S(2)}) collective-permute-start(bf16[128,4,128]{0,2,1:T(8,128)(2,1)} %bitcast.2), channel_id=1, source_target_pairs={{0,4},{4,8},{8,12},{12,16},{16,20},{20,24},{24,28},{28,32},{32,36}... | collective-permute-start | bytes 393224 | tf_op jit(solution)/shard_map/ppermute | solution.py:19
  31.7 0.7 copy-start.27
  31.7 0.7 copy-start.29
  34.4 2.4 %copy-start.17 = (bf16[128,4,128]{0,2,1:T(8,128)(2,1)}, bf16[128,4,128]{0,2,1:T(8,128)(2,1)S(1)}, u32[]{:S(2)}) copy-start(bf16[128,4,128]{0,2,1:T(8,128)(2,1)S(1)} %collective-permute-done.1) | copy-start | bytes 393220
  40.8 0.9 copy-start.18
  41.7 1.5 %copy-start.11 = (bf16[128,8,64]{2,0,1:T(8,128)(2,1)S(1)}, bf16[128,8,64]{2,0,1:T(8,128)(2,1)}, u32[]{:S(2)}) copy-start(bf16[128,8,64]{2,0,1:T(8,128)(2,1)} %copy.83) | copy-start | bytes 393220
  41.7 1.5 %copy-start.12 = (bf16[128,8,64]{2,0,1:T(8,128)(2,1)S(1)}, bf16[128,8,64]{2,0,1:T(8,128)(2,1)}, u32[]{:S(2)}) copy-start(bf16[128,8,64]{2,0,1:T(8,128)(2,1)} %copy.82) | copy-start | bytes 393220
  43.3 3.9 %copy-start.14 = (bf16[128,4,64]{2,0,1:T(8,128)(2,1)S(1)}, bf16[128,4,64]{2,0,1:T(8,128)(2,1)}, u32[]{:S(2)}) copy-start(bf16[128,4,64]{2,0,1:T(8,128)(2,1)} %copy-done.13) | copy-start | bytes 196612
  43.3 3.9 %copy-start.16 = (bf16[128,4,64]{2,0,1:T(8,128)(2,1)S(1)}, bf16[128,4,64]{2,0,1:T(8,128)(2,1)}, u32[]{:S(2)}) copy-start(bf16[128,4,64]{2,0,1:T(8,128)(2,1)} %copy-done.15) | copy-start | bytes 196612
  43.3 3.9 %copy-start.28 = (bf16[128,4,128]{2,0,1:T(8,128)(2,1)S(1)}, bf16[128,4,128]{2,0,1:T(8,128)(2,1)}, u32[]{:S(2)}) copy-start(bf16[128,4,128]{2,0,1:T(8,128)(2,1)} %copy-done.27) | copy-start | bytes 393220
  43.3 3.9 %copy-start.30 = (bf16[128,4,128]{2,0,1:T(8,128)(2,1)S(1)}, bf16[128,4,128]{2,0,1:T(8,128)(2,1)}, u32[]{:S(2)}) copy-start(bf16[128,4,128]{2,0,1:T(8,128)(2,1)} %copy-done.29) | copy-start | bytes 393220
  44.6 15.0 %collective-permute-start.6 = (f32[128,4,128]{2,0,1:T(8,128)}, f32[128,4,128]{2,0,1:T(8,128)}, u32[]{:S(2)}, u32[]{:S(2)}) collective-permute-start(f32[128,4,128]{2,0,1:T(8,128)} %get-tuple-element.40), channel_id=1, source_target_pairs={{4,0},{8,4},{12,8},{16,12},{20,16},{24,20},{28,24},{32,28},{36,32}... | collective-permute-start | bytes 786440 | tf_op jit(solution)/shard_map/ppermute | solution.py:19
  45.9 14.4 %collective-permute-start.7 = (f32[128,4,128]{2,0,1:T(8,128)}, f32[128,4,128]{2,0,1:T(8,128)}, u32[]{:S(2)}, u32[]{:S(2)}) collective-permute-start(f32[128,4,128]{2,0,1:T(8,128)} %get-tuple-element.41), channel_id=1, source_target_pairs={{8,0},{12,4},{16,8},{20,12},{24,16},{28,20},{32,24},{36,28},{40,32... | collective-permute-start | bytes 786440 | tf_op jit(solution)/shard_map/ppermute | solution.py:19
  48.6 2.2 %copy-start.23 = (f32[128]{0:T(128)S(1)}, f32[128]{0:T(128)}, u32[]{:S(2)}) copy-start(f32[128]{0:T(128)} %param.12) | copy-start | bytes 1540
  49.8 1.0 copy-start.8
  52.0 1.1 copy-start
  52.2 5.4 %copy-start.1 = (f32[1,128,1024]{2,1,0:T(8,128)S(1)}, f32[1,128,1024]{2,1,0:T(8,128)}, u32[]{:S(2)}) copy-start(f32[1,128,1024]{2,1,0:T(8,128)} %mul.390) | copy-start | bytes 1572868
  53.1 4.5 %copy-start.2 = (f32[1,128,1024]{2,1,0:T(8,128)S(1)}, f32[1,128,1024]{2,1,0:T(8,128)}, u32[]{:S(2)}) copy-start(f32[1,128,1024]{2,1,0:T(8,128)} %mul.407) | copy-start | bytes 1572868
  54.9 83.7 %collective-permute-start.8 = (f32[128,4,128]{0,2,1:T(8,128)}, f32[128,4,128]{0,2,1:T(8,128)S(1)}, u32[]{:S(2)}, u32[]{:S(2)}) collective-permute-start(f32[128,4,128]{0,2,1:T(8,128)} %get-tuple-element.38), channel_id=1, source_target_pairs={{4,0},{8,4},{12,8},{16,12},{20,16},{24,20},{28,24},{32,28},{36,32}... | collective-permute-start | bytes 786440 | tf_op jit(solution)/shard_map/ppermute | solution.py:19
  56.2 5.2 %copy-start.4 = (f32[128,64]{1,0:T(8,128)S(1)}, f32[128,64]{1,0:T(8,128)}, u32[]{:S(2)}) copy-start(f32[128,64]{1,0:T(8,128)} %copy-done.3) | copy-start | bytes 98308
  56.2 5.2 %copy-start.6 = (f32[128,64]{1,0:T(8,128)S(1)}, f32[128,64]{1,0:T(8,128)}, u32[]{:S(2)}) copy-start(f32[128,64]{1,0:T(8,128)} %copy-done.5) | copy-start | bytes 98308
  56.2 82.4 %collective-permute-start.9 = (f32[128,4,128]{0,2,1:T(8,128)}, f32[128,4,128]{0,2,1:T(8,128)S(1)}, u32[]{:S(2)}, u32[]{:S(2)}) collective-permute-start(f32[128,4,128]{0,2,1:T(8,128)} %get-tuple-element.39), channel_id=1, source_target_pairs={{8,0},{12,4},{16,8},{20,12},{24,16},{28,20},{32,24},{36,28},{40,32... | collective-permute-start | bytes 786440 | tf_op jit(solution)/shard_map/ppermute | solution.py:19
  59.6 1.9 %copy-start.25 = (f32[128]{0:T(128)S(1)}, f32[128]{0:T(128)}, u32[]{:S(2)}) copy-start(f32[128]{0:T(128)} %param.13) | copy-start | bytes 1540
  61.4 0.7 copy-start.21
  61.4 71.1 %copy-start.10 = (bf16[4,128,2,128]{3,1,2,0:T(8,128)(2,1)S(1)}, bf16[4,128,2,128]{3,1,2,0:T(8,128)(2,1)}, u32[]{:S(2)}) copy-start(bf16[4,128,2,128]{3,1,2,0:T(8,128)(2,1)} %get-tuple-element.59) | copy-start | bytes 786436
  62.3 5.5 %collective-permute-start.10 = (f32[256]{0:T(256)S(1)}, f32[256]{0:T(256)S(1)}, u32[]{:S(2)}, u32[]{:S(2)}) collective-permute-start(f32[256]{0:T(256)S(1)} %pad_maximum_fusion.6), channel_id=1, source_target_pairs={{0,1},{1,0},{2,3},{3,2},{4,5},{5,4},{6,7},{7,6},{8,9},{9,8},{10,11... | collective-permute-start | bytes 3080 | tf_op jit(solution)/shard_map/ppermute | solution.py:27
  67.8 6.4 %collective-permute-start.11 = (f32[256]{0:T(256)S(1)}, f32[256]{0:T(256)S(1)}, u32[]{:S(2)}, u32[]{:S(2)}) collective-permute-start(f32[256]{0:T(256)S(1)} %fusion.22), channel_id=1, source_target_pairs={{0,2},{1,3},{2,0},{3,1},{4,6},{5,7},{6,4},{7,5},{8,10},{9,11},{10,... | collective-permute-start | bytes 3080 | tf_op jit(solution)/shard_map/ppermute | solution.py:27
  74.1 3.2 %collective-permute-start.12 = (f32[256]{0:T(256)S(1)}, f32[256]{0:T(256)S(1)}, u32[]{:S(2)}, u32[]{:S(2)}) collective-permute-start(f32[256]{0:T(256)S(1)} %add.129), channel_id=1, source_target_pairs={{0,4},{4,0},{8,12},{12,8},{16,20},{20,16},{24,28},{28,24},{32,36},... | collective-permute-start | bytes 3080 | tf_op jit(solution)/shard_map/ppermute | solution.py:27
  77.3 8.7 %collective-permute-start.13 = (f32[256]{0:T(256)S(1)}, f32[256]{0:T(256)S(1)}, u32[]{:S(2)}, u32[]{:S(2)}) collective-permute-start(f32[256]{0:T(256)S(1)} %add.130), channel_id=1, source_target_pairs={{0,8},{4,12},{8,0},{12,4},{16,24},{20,28},{24,16},{28,20},{32,40},... | collective-permute-start | bytes 3080 | tf_op jit(solution)/shard_map/ppermute | solution.py:27
  86.0 7.6 %collective-permute-start.14 = (f32[256]{0:T(256)S(1)}, f32[256]{0:T(256)S(1)}, u32[]{:S(2)}, u32[]{:S(2)}) collective-permute-start(f32[256]{0:T(256)S(1)} %add.131), channel_id=1, source_target_pairs={{0,16},{4,20},{8,24},{12,28},{16,0},{20,4},{24,8},{28,12},{32,48},... | collective-permute-start | bytes 3080 | tf_op jit(solution)/shard_map/ppermute | solution.py:27
  93.6 12.6 %collective-permute-start.15 = (f32[256]{0:T(256)S(1)}, f32[256]{0:T(256)S(1)}, u32[]{:S(2)}, u32[]{:S(2)}) collective-permute-start(f32[256]{0:T(256)S(1)} %add.132), channel_id=1, source_target_pairs={{0,32},{4,36},{8,40},{12,44},{16,48},{20,52},{24,56},{28,60},{32,0... | collective-permute-start | bytes 3080 | tf_op jit(solution)/shard_map/ppermute | solution.py:27
  106.2 14.2 %collective-permute-start.16 = (f32[256]{0:T(256)S(1)}, f32[256]{0:T(256)S(1)}, u32[]{:S(2)}, u32[]{:S(2)}) collective-permute-start(f32[256]{0:T(256)S(1)} %add.133), channel_id=1, source_target_pairs={{0,64},{4,68},{8,72},{12,76},{16,80},{20,84},{24,88},{28,92},{32,9... | collective-permute-start | bytes 3080 | tf_op jit(solution)/shard_map/ppermute | solution.py:27
  120.4 9.4 %collective-permute-start.17 = (f32[256]{0:T(256)S(1)}, f32[256]{0:T(256)S(1)}, u32[]{:S(2)}, u32[]{:S(2)}) collective-permute-start(f32[256]{0:T(256)S(1)} %add.134), channel_id=1, source_target_pairs={{0,128},{128,0},{256,384},{384,256},{512,640},{640,512},{768,896},... | collective-permute-start | bytes 3080 | tf_op jit(solution)/shard_map/ppermute | solution.py:27
  129.8 5.5 %collective-permute-start.18 = (f32[256]{0:T(256)S(1)}, f32[256]{0:T(256)S(1)}, u32[]{:S(2)}, u32[]{:S(2)}) collective-permute-start(f32[256]{0:T(256)S(1)} %add.135), channel_id=1, source_target_pairs={{0,256},{128,384},{256,0},{384,128},{512,768},{640,896},{768,512},... | collective-permute-start | bytes 3080 | tf_op jit(solution)/shard_map/ppermute | solution.py:27
  135.2 7.0 %collective-permute-start.19 = (f32[256]{0:T(256)S(1)}, f32[256]{0:T(256)S(1)}, u32[]{:S(2)}, u32[]{:S(2)}) collective-permute-start(f32[256]{0:T(256)S(1)} %add.136), channel_id=1, source_target_pairs={{0,512},{128,640},{256,768},{384,896},{512,0},{640,128},{768,256},... | collective-permute-start | bytes 3080 | tf_op jit(solution)/shard_map/ppermute | solution.py:27

commit v2 on v1

--- a/solution.py
+++ b/solution.py
@@ -100,12 +100,16 @@
     q_unit, q_inv, q_rot = normalize(q_raw[0], q_gain, positions, qheads)
     k_unit, k_inv, k_rot = normalize(unnormed_keys[0], k_gain, positions, kheads)
     value_own = value_input[0].reshape(row_count, kheads, HEAD_WIDTH)
+    file_slab = jnp.broadcast_to(
+        file_row.astype(jnp.bfloat16)[None, None, :], (1, 2 * kheads, HEAD_WIDTH)
+    )
+    packed = jnp.concatenate([jnp.concatenate([k_rot, value_own], axis=1), file_slab], axis=0)
     key_list, value_list, file_list = ([], [], [])
     for offset in range(reach_count, 0, -1):
-        key_far, value_far, file_far = passed_along((k_rot, value_own, file_row), "ctx", offset)
-        key_list.append(key_far)
-        value_list.append(value_far)
-        file_list.append(file_far)
+        far = passed_along(packed, "ctx", offset)
+        key_list.append(far[:row_count, :kheads])
+        value_list.append(far[:row_count, kheads:])
+        file_list.append(far[row_count, 0, :row_count].astype(jnp.int32))
     key_rows = jnp.concatenate(key_list + [k_rot], axis=0)
     value_rows = jnp.concatenate(value_list + [value_own], axis=0)
     key_files = jnp.concatenate(file_list + [file_row], axis=0)
@@ -143,11 +147,15 @@
     value_grad = grad_values[reach_count * row_count :]
     for offset in range(1, reach_count + 1):
         low_row = (reach_count - offset) * row_count
-        back_keys, back_values = passed_along(
-            (grad_keys[low_row : low_row + row_count], grad_values[low_row : low_row + row_count]),
+        back = passed_along(
+            jnp.concatenate(
+                [grad_keys[low_row : low_row + row_count], grad_values[low_row : low_row + row_count]],
+                axis=1,
+            ),
             "ctx",
             -offset,
         )
+        back_keys, back_values = back[:, :kheads], back[:, kheads:]
         key_own = key_own + back_keys
         value_grad = value_grad + back_values
     dq_grad, q_term = restore(

time: 144 us -> 139 us (0.965)
  the two profiles are of different devices: /device:TPU:54 before, /device:TPU:32 now
where the time goes in v2:
time: 139 us; the launch traced here: 138 us
  starting transfers between devices  63.2 us (45%)
  waiting for transfers between devices  37.4 us (27%)
  local copies, waits for them, and re-layouts  18.8 us (14%)
  other arithmetic  12.8 us (9%)
  matrix products  4.58 us (3%)
    ppermute x10, starting transfers between devices, butterfly_sum(): value = value + lax.ppermute(value, axis, pairs)  54.4 us
    ppermute x10, waiting for transfers between devices, butterfly_sum(): value = value + lax.ppermute(value, axis, pairs)  23.2 us
    ppermute x4, waiting for transfers between devices, passed_along(): return lax.ppermute(value, axis, pairs)  14.2 us
    unnamed x77, local copies, waits for them, and re-layouts  11.2 us
    ppermute x4, starting transfers between devices, passed_along(): return lax.ppermute(value, axis, pairs)  8.77 us
  transfers between devices with their start and end apart: 14, of which 11 were waited for; matrix products, arithmetic and copies ran while one was open for 11% of the time, Pallas kernels for 0%

profile of v2, /device:TPU:32, one launch (start us, length us, event | category | flops | bytes accessed | tf_op | source)
XLA Modules:
  0.0 138.2 jit_solution(2819185548624993201)
XLA Ops:
  0.6 1.0 copy.86
  1.9 1.0 copy.88
  3.1 0.7 bitcast_convert_fusion.1
  3.8 0.3 multiply_cosine_fusion
  4.1 0.8 multiply_multiply_fusion.1
  5.1 0.6 copy-done.21
  5.8 1.8 %collective-permute-start.1 = (bf16[129,8,128]{2,0,1:T(8,128)(2,1)S(1)}, bf16[129,8,128]{2,0,1:T(8,128)(2,1)S(1)}, u32[]{:S(2)}, u32[]{:S(2)}) collective-permute-start(bf16[129,8,128]{2,0,1:T(8,128)(2,1)S(1)} %pad_maximum_fusion.3), channel_id=1, source_target_pairs={{0,4},{4,8},{8,12},{12,16},{16,20},{20,24},{24,28},{28,32},{32,36}... | collective-permute-start | bytes 792584 | tf_op jit(solution)/shard_map/ppermute | solution.py:19
  7.6 4.5 %collective-permute-start = (bf16[129,8,128]{2,0,1:T(8,128)(2,1)S(1)}, bf16[129,8,128]{2,0,1:T(8,128)(2,1)S(1)}, u32[]{:S(2)}, u32[]{:S(2)}) collective-permute-start(bf16[129,8,128]{2,0,1:T(8,128)(2,1)S(1)} %pad_maximum_fusion.3), channel_id=1, source_target_pairs={{0,8},{4,12},{8,16},{12,20},{16,24},{20,28},{24,32},{28,36},{32,40... | collective-permute-start | bytes 792584 | tf_op jit(solution)/shard_map/ppermute | solution.py:19
  12.1 0.6 broadcast_bitcast_fusion.1
  13.3 0.3 subtract_convert_fusion
  13.6 0.7 copy.91
  14.4 0.7 copy.92
  15.7 0.9 mul.390
  16.6 1.9 %collective-permute-done = bf16[129,8,128]{2,0,1:T(8,128)(2,1)S(1)} collective-permute-done((bf16[129,8,128]{2,0,1:T(8,128)(2,1)S(1)}, bf16[129,8,128]{2,0,1:T(8,128)(2,1)S(1)}, u32[]{:S(2)}, u32[]{:S(2)}) %collective-permute-start) | collective-permute-done | bytes 264224 | tf_op jit(solution)/shard_map/ppermute | solution.py:19
  18.9 0.6 copy-done.24
  19.5 1.6 %fusion.29 = (f32[4,2,128]{2,1,0:T(2,128)S(1)}, f32[4,2,128,384]{2,3,1,0:T(8,128)S(1)}) fusion(bf16[128,4,2,64]{3,0,2,1:T(8,128)(2,1)} %bitcast.120, bf16[128,4,2,64]{3,0,2,1:T(8,128)(2,1)} %bitcast.118, bf16[128,4,64]{2,0,1:T(8,128)(2,1)} %copy-done.21, bf16[128,4,64]{2,0,1:T(8,128)(2,1)} %copy-done.19, bf16[128,4,128]{2,0,1:T(8,128)(2,1)S(1)} %get-tuple-element.56, ...), kind=kOutput, calls=%fused_computation.93 | convolution fusion | flops 103939072 | bytes 2281472 | tf_op jit(solution)/shard_map/qhgd,khd->hgqk/dot_general | solution.py:83
  21.4 0.6 copy-done.3
  22.0 1.3 bitcast_convert_fusion
  23.3 1.4 copy.121
  24.7 1.5 %multiply_reduce_fusion = f32[4,2,128]{1,0,2:T(4,128)} fusion(f32[4,2,128,128]{3,1,0,2:T(2,128)S(1)} %copy.121, bf16[128,4,2,128]{3,2,1,0:T(2,128)(2,1)S(1)} %reshape_squeeze.7), kind=kLoop, calls=%fused_computation.18 | loop fusion | flops 392192 | bytes 790528
  26.3 1.0 copy.122
  27.3 0.4 convolution_bitcast_fusion.1
  27.7 0.5 copy-done.4
  28.4 0.4 fusion.1
  28.8 0.5 copy-done.17
  29.4 0.4 fusion.4
  29.9 0.4 copy-done.20
  30.5 0.4 convolution_multiply_fusion
  31.0 0.8 pad_maximum_fusion.1
  31.8 1.3 collective-permute-start.2
  33.1 0.8 pad_maximum_fusion.2
  33.9 1.3 collective-permute-start.3
  35.2 0.7 fusion.25
  36.2 1.2 copy.137
  37.4 1.0 multiply_add_fusion
  38.5 1.2 multiply_reduce_fusion.2
  39.8 0.9 mul.407
  40.8 2.0 %multiply_reduce_fusion.1 = (f32[1024]{0:T(1024)S(1)}, bf16[1,128,1024]{2,1,0:T(8,128)(2,1)}) fusion(f32[1,128,1024]{2,1,0:T(8,128)S(1)} %concatenate.57, f32[1,128,1024]{2,1,0:T(8,128)S(1)} %copy-done.1, bf16[1,128,1024]{2,1,0:T(8,128)(2,1)} %param.7, f32[1,128,1024]{2,1,0:T(8,128)} %mul.407, f32[1024]{0:T(1024)S(1)} %broadcast_bitcast_fusion), kind=kLoop, calls=%fused_computation.19 | loop fusion | flops 1178624 | bytes 2105344 | tf_op jit(solution)/shard_map/reduce_sum | solution.py:69
  42.9 12.3 %collective-permute-done.3 = f32[128,8,128]{2,0,1:T(8,128)} collective-permute-done((f32[128,8,128]{2,0,1:T(8,128)}, f32[128,8,128]{2,0,1:T(8,128)}, u32[]{:S(2)}, u32[]{:S(2)}) %collective-permute-start.3) | collective-permute-done | bytes 524320 | tf_op jit(solution)/shard_map/ppermute | solution.py:19
  55.2 1.3 fusion.6
  56.6 0.3 multiply_reduce_fusion.4
  57.4 2.6 %collective-permute-start.4 = (f32[256]{0:T(256)S(1)}, f32[256]{0:T(256)S(1)}, u32[]{:S(2)}, u32[]{:S(2)}) collective-permute-start(f32[256]{0:T(256)S(1)} %pad_maximum_fusion.8), channel_id=1, source_target_pairs={{0,1},{1,0},{2,3},{3,2},{4,5},{5,4},{6,7},{7,6},{8,9},{9,8},{10,11... | collective-permute-start | bytes 3080 | tf_op jit(solution)/shard_map/ppermute | solution.py:27
  60.0 2.9 %collective-permute-done.4 = f32[256]{0:T(256)S(1)} collective-permute-done((f32[256]{0:T(256)S(1)}, f32[256]{0:T(256)S(1)}, u32[]{:S(2)}, u32[]{:S(2)}) %collective-permute-start.4) | collective-permute-done | bytes 1056 | tf_op jit(solution)/shard_map/ppermute | solution.py:27
  62.9 2.7 %collective-permute-start.5 = (f32[256]{0:T(256)S(1)}, f32[256]{0:T(256)S(1)}, u32[]{:S(2)}, u32[]{:S(2)}) collective-permute-start(f32[256]{0:T(256)S(1)} %fusion.22), channel_id=1, source_target_pairs={{0,2},{1,3},{2,0},{3,1},{4,6},{5,7},{6,4},{7,5},{8,10},{9,11},{10,... | collective-permute-start | bytes 3080 | tf_op jit(solution)/shard_map/ppermute | solution.py:27
  65.6 3.7 %collective-permute-done.5 = f32[256]{0:T(256)S(1)} collective-permute-done((f32[256]{0:T(256)S(1)}, f32[256]{0:T(256)S(1)}, u32[]{:S(2)}, u32[]{:S(2)}) %collective-permute-start.5) | collective-permute-done | bytes 1056 | tf_op jit(solution)/shard_map/ppermute | solution.py:27
  69.2 1.9 %collective-permute-start.6 = (f32[256]{0:T(256)S(1)}, f32[256]{0:T(256)S(1)}, u32[]{:S(2)}, u32[]{:S(2)}) collective-permute-start(f32[256]{0:T(256)S(1)} %add.129), channel_id=1, source_target_pairs={{0,4},{4,0},{8,12},{12,8},{16,20},{20,16},{24,28},{28,24},{32,36},... | collective-permute-start | bytes 3080 | tf_op jit(solution)/shard_map/ppermute | solution.py:27
  71.1 1.1 collective-permute-done.6
  72.3 4.3 %collective-permute-start.7 = (f32[256]{0:T(256)S(1)}, f32[256]{0:T(256)S(1)}, u32[]{:S(2)}, u32[]{:S(2)}) collective-permute-start(f32[256]{0:T(256)S(1)} %add.130), channel_id=1, source_target_pairs={{0,8},{4,12},{8,0},{12,4},{16,24},{20,28},{24,16},{28,20},{32,40},... | collective-permute-start | bytes 3080 | tf_op jit(solution)/shard_map/ppermute | solution.py:27
  76.5 1.5 %collective-permute-done.7 = f32[256]{0:T(256)S(1)} collective-permute-done((f32[256]{0:T(256)S(1)}, f32[256]{0:T(256)S(1)}, u32[]{:S(2)}, u32[]{:S(2)}) %collective-permute-start.7) | collective-permute-done | bytes 1056 | tf_op jit(solution)/shard_map/ppermute | solution.py:27
  78.1 8.5 %collective-permute-start.8 = (f32[256]{0:T(256)S(1)}, f32[256]{0:T(256)S(1)}, u32[]{:S(2)}, u32[]{:S(2)}) collective-permute-start(f32[256]{0:T(256)S(1)} %add.131), channel_id=1, source_target_pairs={{0,16},{4,20},{8,24},{12,28},{16,0},{20,4},{24,8},{28,12},{32,48},... | collective-permute-start | bytes 3080 | tf_op jit(solution)/shard_map/ppermute | solution.py:27
  86.6 1.5 %collective-permute-done.8 = f32[256]{0:T(256)S(1)} collective-permute-done((f32[256]{0:T(256)S(1)}, f32[256]{0:T(256)S(1)}, u32[]{:S(2)}, u32[]{:S(2)}) %collective-permute-start.8) | collective-permute-done | bytes 1056 | tf_op jit(solution)/shard_map/ppermute | solution.py:27
  88.1 11.2 %collective-permute-start.9 = (f32[256]{0:T(256)S(1)}, f32[256]{0:T(256)S(1)}, u32[]{:S(2)}, u32[]{:S(2)}) collective-permute-start(f32[256]{0:T(256)S(1)} %add.132), channel_id=1, source_target_pairs={{0,32},{4,36},{8,40},{12,44},{16,48},{20,52},{24,56},{28,60},{32,0... | collective-permute-start | bytes 3080 | tf_op jit(solution)/shard_map/ppermute | solution.py:27
  99.3 1.5 %collective-permute-done.9 = f32[256]{0:T(256)S(1)} collective-permute-done((f32[256]{0:T(256)S(1)}, f32[256]{0:T(256)S(1)}, u32[]{:S(2)}, u32[]{:S(2)}) %collective-permute-start.9) | collective-permute-done | bytes 1056 | tf_op jit(solution)/shard_map/ppermute | solution.py:27
  100.9 13.0 %collective-permute-start.10 = (f32[256]{0:T(256)S(1)}, f32[256]{0:T(256)S(1)}, u32[]{:S(2)}, u32[]{:S(2)}) collective-permute-start(f32[256]{0:T(256)S(1)} %add.133), channel_id=1, source_target_pairs={{0,64},{4,68},{8,72},{12,76},{16,80},{20,84},{24,88},{28,92},{32,9... | collective-permute-start | bytes 3080 | tf_op jit(solution)/shard_map/ppermute | solution.py:27
  113.8 1.5 %collective-permute-done.10 = f32[256]{0:T(256)S(1)} collective-permute-done((f32[256]{0:T(256)S(1)}, f32[256]{0:T(256)S(1)}, u32[]{:S(2)}, u32[]{:S(2)}) %collective-permute-start.10) | collective-permute-done | bytes 1056 | tf_op jit(solution)/shard_map/ppermute | solution.py:27
  115.4 2.0 %collective-permute-start.11 = (f32[256]{0:T(256)S(1)}, f32[256]{0:T(256)S(1)}, u32[]{:S(2)}, u32[]{:S(2)}) collective-permute-start(f32[256]{0:T(256)S(1)} %add.134), channel_id=1, source_target_pairs={{0,128},{128,0},{256,384},{384,256},{512,640},{640,512},{768,896},... | collective-permute-start | bytes 3080 | tf_op jit(solution)/shard_map/ppermute | solution.py:27
  117.4 7.3 %collective-permute-done.11 = f32[256]{0:T(256)S(1)} collective-permute-done((f32[256]{0:T(256)S(1)}, f32[256]{0:T(256)S(1)}, u32[]{:S(2)}, u32[]{:S(2)}) %collective-permute-start.11) | collective-permute-done | bytes 1056 | tf_op jit(solution)/shard_map/ppermute | solution.py:27
  124.7 3.4 %collective-permute-start.12 = (f32[256]{0:T(256)S(1)}, f32[256]{0:T(256)S(1)}, u32[]{:S(2)}, u32[]{:S(2)}) collective-permute-start(f32[256]{0:T(256)S(1)} %add.135), channel_id=1, source_target_pairs={{0,256},{128,384},{256,0},{384,128},{512,768},{640,896},{768,512},... | collective-permute-start | bytes 3080 | tf_op jit(solution)/shard_map/ppermute | solution.py:27
  128.1 2.1 %collective-permute-done.12 = f32[256]{0:T(256)S(1)} collective-permute-done((f32[256]{0:T(256)S(1)}, f32[256]{0:T(256)S(1)}, u32[]{:S(2)}, u32[]{:S(2)}) %collective-permute-start.12) | collective-permute-done | bytes 1056 | tf_op jit(solution)/shard_map/ppermute | solution.py:27
  130.2 4.9 %collective-permute-start.13 = (f32[256]{0:T(256)S(1)}, f32[256]{0:T(256)S(1)}, u32[]{:S(2)}, u32[]{:S(2)}) collective-permute-start(f32[256]{0:T(256)S(1)} %add.136), channel_id=1, source_target_pairs={{0,512},{128,640},{256,768},{384,896},{512,0},{640,128},{768,256},... | collective-permute-start | bytes 3080 | tf_op jit(solution)/shard_map/ppermute | solution.py:27
  135.1 0.9 copy.109
  136.0 0.8 copy.110
  136.9 0.8 copy.111
  137.7 0.5 fusion.28
  (117 shorter events, 4.1 us)
Async XLA Ops:
  1.7 10.4 %copy-start.31 = (f32[128]{0:T(128)S(1)}, f32[128]{0:T(128)}, u32[]{:S(2)}) copy-start(f32[128]{0:T(128)} %param.13) | copy-start | bytes 1540
  1.7 11.0 %copy-start.15 = (bf16[1,128,1024]{2,1,0:T(8,128)(2,1)S(1)}, bf16[1,128,1024]{2,1,0:T(8,128)(2,1)}, u32[]{:S(2)}) copy-start(bf16[1,128,1024]{2,1,0:T(8,128)(2,1)} %param.7) | copy-start | bytes 786436
  3.1 9.6 %copy-start.2 = (bf16[128,4,128]{2,0,1:T(8,128)(2,1)}, bf16[128,4,128]{2,0,1:T(8,128)(2,1)S(1)}, u32[]{:S(2)}) copy-start(bf16[128,4,128]{2,0,1:T(8,128)(2,1)S(1)} %copy.89) | copy-start | bytes 393220
  4.1 9.2 %copy-start.5 = (f32[128,64]{1,0:T(8,128)}, f32[128,64]{1,0:T(8,128)S(1)}, u32[]{:S(2)}) copy-start(f32[128,64]{1,0:T(8,128)S(1)} %get-tuple-element.60) | copy-start | bytes 98308
  4.1 9.2 %copy-start.7 = (f32[128,64]{1,0:T(8,128)}, f32[128,64]{1,0:T(8,128)S(1)}, u32[]{:S(2)}) copy-start(f32[128,64]{1,0:T(8,128)S(1)} %get-tuple-element.61) | copy-start | bytes 98308
  5.1 0.7 copy-start.21
  5.1 7.6 %copy-start.19 = (bf16[128,4,64]{2,0,1:T(8,128)(2,1)}, bf16[128,4,64]{2,0,1:T(8,128)(2,1)S(1)}, u32[]{:S(2)}) copy-start(bf16[128,4,64]{2,0,1:T(8,128)(2,1)S(1)} %get-tuple-element.52) | copy-start | bytes 196612
  5.7 7.3 %copy-start.29 = (f32[128]{0:T(128)S(1)}, f32[128]{0:T(128)}, u32[]{:S(2)}) copy-start(f32[128]{0:T(128)} %param.12) | copy-start | bytes 1540
  5.8 10.8 %collective-permute-start.1 = (bf16[129,8,128]{2,0,1:T(8,128)(2,1)S(1)}, bf16[129,8,128]{2,0,1:T(8,128)(2,1)S(1)}, u32[]{:S(2)}, u32[]{:S(2)}) collective-permute-start(bf16[129,8,128]{2,0,1:T(8,128)(2,1)S(1)} %pad_maximum_fusion.3), channel_id=1, source_target_pairs={{0,4},{4,8},{8,12},{12,16},{16,20},{20,24},{24,28},{28,32},{32,36}... | collective-permute-start | bytes 792584 | tf_op jit(solution)/shard_map/ppermute | solution.py:19
  7.6 10.9 %collective-permute-start = (bf16[129,8,128]{2,0,1:T(8,128)(2,1)S(1)}, bf16[129,8,128]{2,0,1:T(8,128)(2,1)S(1)}, u32[]{:S(2)}, u32[]{:S(2)}) collective-permute-start(bf16[129,8,128]{2,0,1:T(8,128)(2,1)S(1)} %pad_maximum_fusion.3), channel_id=1, source_target_pairs={{0,8},{4,12},{8,16},{12,20},{16,24},{20,28},{24,32},{28,36},{32,40... | collective-permute-start | bytes 792584 | tf_op jit(solution)/shard_map/ppermute | solution.py:19
  13.1 2.4 %copy-start.13 = (f32[128,8]{1,0:T(8,128)}, f32[128,8]{1,0:T(8,128)S(1)}, u32[]{:S(2)}) copy-start(f32[128,8]{1,0:T(8,128)S(1)} %add_rsqrt_fusion) | copy-start | bytes 12292
  13.3 1.8 %copy-start.23 = (bf16[1,128,1024]{2,1,0:T(8,128)(2,1)S(1)}, bf16[1,128,1024]{2,1,0:T(8,128)(2,1)}, u32[]{:S(2)}) copy-start(bf16[1,128,1024]{2,1,0:T(8,128)(2,1)} %param.10) | copy-start | bytes 786436
  14.4 4.2 %copy-start.33 = (s32[1,128]{1,0:T(1,128)S(1)}, s32[1,128]{1,0:T(1,128)}, u32[]{:S(2)}) copy-start(s32[1,128]{1,0:T(1,128)} %param.11) | copy-start | bytes 1540
  18.8 0.7 copy-start.24
  18.8 2.6 %copy-start.9 = (bf16[128,4,128]{2,0,1:T(8,128)(2,1)}, bf16[128,4,128]{2,0,1:T(8,128)(2,1)S(1)}, u32[]{:S(2)}) copy-start(bf16[128,4,128]{2,0,1:T(8,128)(2,1)S(1)} %get-tuple-element.55) | copy-start | bytes 393220
  18.9 2.3 %copy-start.26 = (bf16[128,4,128]{2,0,1:T(8,128)(2,1)}, bf16[128,4,128]{2,0,1:T(8,128)(2,1)S(1)}, u32[]{:S(2)}) copy-start(bf16[128,4,128]{2,0,1:T(8,128)(2,1)S(1)} %get-tuple-element.56) | copy-start | bytes 393220
  18.9 2.5 %copy-start.11 = (bf16[128,4,128]{2,0,1:T(8,128)(2,1)}, bf16[128,4,128]{2,0,1:T(8,128)(2,1)S(1)}, u32[]{:S(2)}) copy-start(bf16[128,4,128]{2,0,1:T(8,128)(2,1)S(1)} %get-tuple-element.57) | copy-start | bytes 393220
  21.1 0.9 copy-start.3
  27.3 0.9 copy-start.4
  27.3 1.0 copy-start.10
  27.3 1.1 copy-start.12
  28.4 0.9 copy-start.17
  28.4 1.0 copy-start.18
  29.4 0.9 copy-start.20
  29.4 1.0 copy-start.22
  29.4 1.0 copy-start.25
  29.4 1.1 copy-start.27
  31.8 11.1 %collective-permute-start.2 = (f32[128,8,128]{2,0,1:T(8,128)}, f32[128,8,128]{2,0,1:T(8,128)}, u32[]{:S(2)}, u32[]{:S(2)}) collective-permute-start(f32[128,8,128]{2,0,1:T(8,128)} %pad_maximum_fusion.1), channel_id=1, source_target_pairs={{4,0},{8,4},{12,8},{16,12},{20,16},{24,20},{28,24},{32,28},{36,32}... | collective-permute-start | bytes 1572872 | tf_op jit(solution)/shard_map/ppermute | solution.py:19
  33.9 21.2 %collective-permute-start.3 = (f32[128,8,128]{2,0,1:T(8,128)}, f32[128,8,128]{2,0,1:T(8,128)}, u32[]{:S(2)}, u32[]{:S(2)}) collective-permute-start(f32[128,8,128]{2,0,1:T(8,128)} %pad_maximum_fusion.2), channel_id=1, source_target_pairs={{8,0},{12,4},{16,8},{20,12},{24,16},{28,20},{32,24},{36,28},{40,32... | collective-permute-start | bytes 1572872 | tf_op jit(solution)/shard_map/ppermute | solution.py:19
  36.2 2.2 %copy-start.30 = (f32[128]{0:T(128)S(1)}, f32[128]{0:T(128)}, u32[]{:S(2)}) copy-start(f32[128]{0:T(128)} %param.12) | copy-start | bytes 1540
  37.4 1.0 copy-start.14
  39.6 1.1 copy-start
  39.6 1.2 copy-start.1
  40.8 15.6 %copy-start.6 = (f32[128,64]{1,0:T(8,128)S(1)}, f32[128,64]{1,0:T(8,128)}, u32[]{:S(2)}) copy-start(f32[128,64]{1,0:T(8,128)} %copy-done.5) | copy-start | bytes 98308
  40.8 15.6 %copy-start.8 = (f32[128,64]{1,0:T(8,128)S(1)}, f32[128,64]{1,0:T(8,128)}, u32[]{:S(2)}) copy-start(f32[128,64]{1,0:T(8,128)} %copy-done.7) | copy-start | bytes 98308
  42.9 13.7 %copy-start.32 = (f32[128]{0:T(128)S(1)}, f32[128]{0:T(128)}, u32[]{:S(2)}) copy-start(f32[128]{0:T(128)} %param.13) | copy-start | bytes 1540
  56.4 0.7 copy-start.28
  56.5 78.7 %copy-start.16 = (bf16[4,128,2,128]{3,1,2,0:T(8,128)(2,1)S(1)}, bf16[4,128,2,128]{3,1,2,0:T(8,128)(2,1)}, u32[]{:S(2)}) copy-start(bf16[4,128,2,128]{3,1,2,0:T(8,128)(2,1)} %get-tuple-element.65) | copy-start | bytes 786436
  57.4 5.5 %collective-permute-start.4 = (f32[256]{0:T(256)S(1)}, f32[256]{0:T(256)S(1)}, u32[]{:S(2)}, u32[]{:S(2)}) collective-permute-start(f32[256]{0:T(256)S(1)} %pad_maximum_fusion.8), channel_id=1, source_target_pairs={{0,1},{1,0},{2,3},{3,2},{4,5},{5,4},{6,7},{7,6},{8,9},{9,8},{10,11... | collective-permute-start | bytes 3080 | tf_op jit(solution)/shard_map/ppermute | solution.py:27
  62.9 6.4 %collective-permute-start.5 = (f32[256]{0:T(256)S(1)}, f32[256]{0:T(256)S(1)}, u32[]{:S(2)}, u32[]{:S(2)}) collective-permute-start(f32[256]{0:T(256)S(1)} %fusion.22), channel_id=1, source_target_pairs={{0,2},{1,3},{2,0},{3,1},{4,6},{5,7},{6,4},{7,5},{8,10},{9,11},{10,... | collective-permute-start | bytes 3080 | tf_op jit(solution)/shard_map/ppermute | solution.py:27
  69.2 3.0 %collective-permute-start.6 = (f32[256]{0:T(256)S(1)}, f32[256]{0:T(256)S(1)}, u32[]{:S(2)}, u32[]{:S(2)}) collective-permute-start(f32[256]{0:T(256)S(1)} %add.129), channel_id=1, source_target_pairs={{0,4},{4,0},{8,12},{12,8},{16,20},{20,16},{24,28},{28,24},{32,36},... | collective-permute-start | bytes 3080 | tf_op jit(solution)/shard_map/ppermute | solution.py:27
  72.3 5.8 %collective-permute-start.7 = (f32[256]{0:T(256)S(1)}, f32[256]{0:T(256)S(1)}, u32[]{:S(2)}, u32[]{:S(2)}) collective-permute-start(f32[256]{0:T(256)S(1)} %add.130), channel_id=1, source_target_pairs={{0,8},{4,12},{8,0},{12,4},{16,24},{20,28},{24,16},{28,20},{32,40},... | collective-permute-start | bytes 3080 | tf_op jit(solution)/shard_map/ppermute | solution.py:27
  78.1 10.0 %collective-permute-start.8 = (f32[256]{0:T(256)S(1)}, f32[256]{0:T(256)S(1)}, u32[]{:S(2)}, u32[]{:S(2)}) collective-permute-start(f32[256]{0:T(256)S(1)} %add.131), channel_id=1, source_target_pairs={{0,16},{4,20},{8,24},{12,28},{16,0},{20,4},{24,8},{28,12},{32,48},... | collective-permute-start | bytes 3080 | tf_op jit(solution)/shard_map/ppermute | solution.py:27
  88.1 12.7 %collective-permute-start.9 = (f32[256]{0:T(256)S(1)}, f32[256]{0:T(256)S(1)}, u32[]{:S(2)}, u32[]{:S(2)}) collective-permute-start(f32[256]{0:T(256)S(1)} %add.132), channel_id=1, source_target_pairs={{0,32},{4,36},{8,40},{12,44},{16,48},{20,52},{24,56},{28,60},{32,0... | collective-permute-start | bytes 3080 | tf_op jit(solution)/shard_map/ppermute | solution.py:27
  100.9 14.5 %collective-permute-start.10 = (f32[256]{0:T(256)S(1)}, f32[256]{0:T(256)S(1)}, u32[]{:S(2)}, u32[]{:S(2)}) collective-permute-start(f32[256]{0:T(256)S(1)} %add.133), channel_id=1, source_target_pairs={{0,64},{4,68},{8,72},{12,76},{16,80},{20,84},{24,88},{28,92},{32,9... | collective-permute-start | bytes 3080 | tf_op jit(solution)/shard_map/ppermute | solution.py:27
  115.4 9.4 %collective-permute-start.11 = (f32[256]{0:T(256)S(1)}, f32[256]{0:T(256)S(1)}, u32[]{:S(2)}, u32[]{:S(2)}) collective-permute-start(f32[256]{0:T(256)S(1)} %add.134), channel_id=1, source_target_pairs={{0,128},{128,0},{256,384},{384,256},{512,640},{640,512},{768,896},... | collective-permute-start | bytes 3080 | tf_op jit(solution)/shard_map/ppermute | solution.py:27
  124.7 5.5 %collective-permute-start.12 = (f32[256]{0:T(256)S(1)}, f32[256]{0:T(256)S(1)}, u32[]{:S(2)}, u32[]{:S(2)}) collective-permute-start(f32[256]{0:T(256)S(1)} %add.135), channel_id=1, source_target_pairs={{0,256},{128,384},{256,0},{384,128},{512,768},{640,896},{768,512},... | collective-permute-start | bytes 3080 | tf_op jit(solution)/shard_map/ppermute | solution.py:27
  130.2 7.5 %collective-permute-start.13 = (f32[256]{0:T(256)S(1)}, f32[256]{0:T(256)S(1)}, u32[]{:S(2)}, u32[]{:S(2)}) collective-permute-start(f32[256]{0:T(256)S(1)} %add.136), channel_id=1, source_target_pairs={{0,512},{128,640},{256,768},{384,896},{512,0},{640,128},{768,256},... | collective-permute-start | bytes 3080 | tf_op jit(solution)/shard_map/ppermute | solution.py:27

commit v3 on v2

--- a/solution.py
+++ b/solution.py
@@ -147,15 +147,10 @@
     value_grad = grad_values[reach_count * row_count :]
     for offset in range(1, reach_count + 1):
         low_row = (reach_count - offset) * row_count
-        back = passed_along(
-            jnp.concatenate(
-                [grad_keys[low_row : low_row + row_count], grad_values[low_row : low_row + row_count]],
-                axis=1,
-            ),
-            "ctx",
-            -offset,
-        )
-        back_keys, back_values = back[:, :kheads], back[:, kheads:]
+        back_keys = passed_along(
+            grad_keys[low_row : low_row + row_count].astype(jnp.bfloat16), "ctx", -offset
+        ).astype(jnp.float32)
+        back_values = passed_along(grad_values[low_row : low_row + row_count], "ctx", -offset)
         key_own = key_own + back_keys
         value_grad = value_grad + back_values
     dq_grad, q_term = restore(

time: 139 us -> 136 us (0.978)
  the two profiles are of different devices: /device:TPU:32 before, /device:TPU:18 now
where the time goes in v3:
time: 136 us; the launch traced here: 135 us
  starting transfers between devices  71.1 us (52%)
  waiting for transfers between devices  26.1 us (19%)
  local copies, waits for them, and re-layouts  18 us (13%)
  other arithmetic  11.9 us (9%)
  matrix products  6.64 us (5%)
  between operations  1.52 us (1%)
    ppermute x10, starting transfers between devices, butterfly_sum(): value = value + lax.ppermute(value, axis, pairs)  59.7 us
    ppermute x10, waiting for transfers between devices, butterfly_sum(): value = value + lax.ppermute(value, axis, pairs)  19.7 us
    ppermute x6, starting transfers between devices, passed_along(): return lax.ppermute(value, axis, pairs)  11.4 us
    unnamed x73, local copies, waits for them, and re-layouts  9.86 us
    ppermute x6, waiting for transfers between devices, passed_along(): return lax.ppermute(value, axis, pairs)  6.41 us
  transfers between devices with their start and end apart: 16, of which 11 were waited for; matrix products, arithmetic and copies ran while one was open for 6% of the time, Pallas kernels for 0%

profile of v3, /device:TPU:18, one launch (start us, length us, event | category | flops | bytes accessed | tf_op | source)
XLA Modules:
  0.0 135.3 jit_solution(3176380715835074621)
XLA Ops:
  0.6 1.0 copy.82
  1.9 0.7 bitcast_convert_fusion.1
  2.6 1.0 copy.84
  3.7 0.3 multiply_cosine_fusion
  4.1 0.8 multiply_multiply_fusion.1
  5.2 1.8 %collective-permute-start.1 = (bf16[129,8,128]{2,0,1:T(8,128)(2,1)S(1)}, bf16[129,8,128]{2,0,1:T(8,128)(2,1)S(1)}, u32[]{:S(2)}, u32[]{:S(2)}) collective-permute-start(bf16[129,8,128]{2,0,1:T(8,128)(2,1)S(1)} %pad_maximum_fusion.1), channel_id=1, source_target_pairs={{0,4},{4,8},{8,12},{12,16},{16,20},{20,24},{24,28},{28,32},{32,36}... | collective-permute-start | bytes 792584 | tf_op jit(solution)/shard_map/ppermute | solution.py:19
  7.0 4.5 %collective-permute-start = (bf16[129,8,128]{2,0,1:T(8,128)(2,1)S(1)}, bf16[129,8,128]{2,0,1:T(8,128)(2,1)S(1)}, u32[]{:S(2)}, u32[]{:S(2)}) collective-permute-start(bf16[129,8,128]{2,0,1:T(8,128)(2,1)S(1)} %pad_maximum_fusion.1), channel_id=1, source_target_pairs={{0,8},{4,12},{8,16},{12,20},{16,24},{20,28},{24,32},{28,36},{32,40... | collective-permute-start | bytes 792584 | tf_op jit(solution)/shard_map/ppermute | solution.py:19
  12.1 0.3 subtract_convert_fusion
  12.5 0.8 copy.87
  13.9 0.9 mul.390
  14.8 3.1 %collective-permute-done = bf16[129,8,128]{2,0,1:T(8,128)(2,1)S(1)} collective-permute-done((bf16[129,8,128]{2,0,1:T(8,128)(2,1)S(1)}, bf16[129,8,128]{2,0,1:T(8,128)(2,1)S(1)}, u32[]{:S(2)}, u32[]{:S(2)}) %collective-permute-start) | collective-permute-done | bytes 264224 | tf_op jit(solution)/shard_map/ppermute | solution.py:19
  17.9 0.2 fusion.15
  18.3 1.6 %fusion.31 = (f32[4,2,128]{2,1,0:T(2,128)S(1)}, f32[4,2,128,384]{2,3,1,0:T(8,128)S(1)}) fusion(bf16[128,4,2,64]{3,0,2,1:T(8,128)(2,1)S(1)} %bitcast.118, bf16[128,4,2,64]{3,0,2,1:T(8,128)(2,1)} %bitcast.120, bf16[128,4,64]{2,0,1:T(8,128)(2,1)} %copy-done.20, bf16[128,4,64]{2,0,1:T(8,128)(2,1)S(1)} %get-tuple-element.50, ...), kind=kOutput, calls=%fused_computation.91 | convolution fusion | flops 103939072 | bytes 2281472 | tf_op jit(solution)/shard_map/qhgd,khd->hgqk/dot_general | solution.py:83
  19.9 0.2 exponential_reduce_fusion
  20.2 1.3 bitcast_convert_fusion
  21.5 1.4 %copy.115 = f32[4,2,128,128]{3,1,0,2:T(2,128)S(1)} copy(f32[4,2,128,128]{2,3,1,0:T(8,128)} %get-tuple-element.62) | data formatting | bytes 1048576
  22.8 1.5 %multiply_reduce_fusion = f32[4,2,128]{1,0,2:T(4,128)} fusion(f32[4,2,128,128]{3,1,0,2:T(2,128)S(1)} %copy.115, bf16[128,4,2,128]{3,2,1,0:T(2,128)(2,1)S(1)} %reshape_squeeze.7), kind=kLoop, calls=%fused_computation.16 | loop fusion | flops 392192 | bytes 790528
  24.4 1.0 copy.116
  25.5 1.5 %fusion.1 = bf16[4,2,128,384]{2,3,1,0:T(8,128)(2,1)S(1)} fusion(bf16[128,4,2,128]{0,3,2,1:T(8,128)(2,1)S(1)} %copy.102, f32[4,2,128,384]{2,3,1,0:T(8,128)S(1)} %get-tuple-element.61, f32[4,2,128]{2,1,0:T(2,128)S(1)} %copy.116, f32[4,2,128]{2,1,0:T(2,128)S(1)} %bitcast.127, bf16[128,4,128]{2,0,1:T(8,128)(2,1)} %copy-done.1, ...), kind=kOutput, calls=%fused_computation.2 | convolution fusion | flops 103415808 | bytes 3022848 | tf_op jit(solution)/shard_map/qhgd,khd->hgqk/dot_general | solution.py:135
  27.0 0.4 convolution_multiply_fusion
  27.4 0.5 copy-done.13
  28.0 1.5 %fusion.32 = (bf16[384,4,128]{2,0,1:T(8,128)(2,1)}, f32[384,4,128]{2,0,1:T(8,128)}) fusion(bf16[4,2,128,384]{2,3,1,0:T(8,128)(2,1)S(1)} %fusion.1, bf16[128,4,2,64]{3,0,2,1:T(8,128)(2,1)S(1)} %bitcast.119, bf16[128,4,2,64]{3,0,2,1:T(8,128)(2,1)S(1)} %bitcast.121), kind=kOutput, calls=%fused_computation.92 | convolution fusion | flops 101580800 | bytes 2228224 | tf_op jit(solution)/shard_map/hgqk,qhgd->khd/dot_general | solution.py:140
  29.5 0.8 fusion.26
  30.4 1.2 copy.130
  31.6 2.0 %copy.129 = f32[128,8,64]{2,1,0:T(8,128)} copy(f32[128,8,64]{0,2,1:T(8,128)} %get-tuple-element.43) | data formatting | bytes 524288
  33.6 1.2 multiply_add_fusion
  34.8 1.1 multiply_reduce_fusion.2
  35.9 0.9 concatenate.51
  36.8 0.9 broadcast_multiply_fusion
  37.9 0.9 mul.407
  38.8 1.0 fusion.27
  39.8 1.3 collective-permute-start.3
  41.1 1.3 collective-permute-start.2
  42.4 2.1 %multiply_reduce_fusion.1 = (f32[1024]{0:T(1024)S(1)}, bf16[1,128,1024]{2,1,0:T(8,128)(2,1)}) fusion(f32[1,128,1024]{2,1,0:T(8,128)} %concatenate.51, f32[1,128,1024]{2,1,0:T(8,128)S(1)} %copy-done, bf16[1,128,1024]{2,1,0:T(8,128)(2,1)S(1)} %copy-done.16, f32[1,128,1024]{2,1,0:T(8,128)} %mul.407, f32[1024]{0:T(1024)S(1)} %broadcast_bitcast_fusion), kind=kLoop, calls=%fused_computation.17 | loop fusion | flops 1178624 | bytes 2105344 | tf_op jit(solution)/shard_map/reduce_sum | solution.py:69
  44.5 0.4 convolution_bitcast_fusion.1
  44.9 3.3 %collective-permute-done.3 = bf16[128,4,128]{2,0,1:T(8,128)(2,1)S(1)} collective-permute-done((bf16[128,4,128]{2,0,1:T(8,128)(2,1)S(1)}, bf16[128,4,128]{2,0,1:T(8,128)(2,1)S(1)}, u32[]{:S(2)}, u32[]{:S(2)}) %collective-permute-start.3) | collective-permute-done | bytes 131104 | tf_op jit(solution)/shard_map/ppermute | solution.py:19
  48.2 1.0 fusion.8
  49.4 0.3 multiply_reduce_fusion.4
  49.9 0.2 fusion.10
  50.1 3.5 %collective-permute-start.6 = (f32[256]{0:T(256)S(1)}, f32[256]{0:T(256)S(1)}, u32[]{:S(2)}, u32[]{:S(2)}) collective-permute-start(f32[256]{0:T(256)S(1)} %pad_maximum_fusion.6), channel_id=1, source_target_pairs={{0,1},{1,0},{2,3},{3,2},{4,5},{5,4},{6,7},{7,6},{8,9},{9,8},{10,11... | collective-permute-start | bytes 3080 | tf_op jit(solution)/shard_map/ppermute | solution.py:27
  53.6 1.3 collective-permute-start.5
  54.9 1.3 collective-permute-start.4
  56.3 2.3 %collective-permute-start.7 = (f32[256]{0:T(256)S(1)}, f32[256]{0:T(256)S(1)}, u32[]{:S(2)}, u32[]{:S(2)}) collective-permute-start(f32[256]{0:T(256)S(1)} %fusion.24), channel_id=1, source_target_pairs={{0,2},{1,3},{2,0},{3,1},{4,6},{5,7},{6,4},{7,5},{8,10},{9,11},{10,... | collective-permute-start | bytes 3080 | tf_op jit(solution)/shard_map/ppermute | solution.py:27
  58.5 4.1 %collective-permute-done.7 = f32[256]{0:T(256)S(1)} collective-permute-done((f32[256]{0:T(256)S(1)}, f32[256]{0:T(256)S(1)}, u32[]{:S(2)}, u32[]{:S(2)}) %collective-permute-start.7) | collective-permute-done | bytes 1056 | tf_op jit(solution)/shard_map/ppermute | solution.py:27
  62.6 2.7 %collective-permute-start.8 = (f32[256]{0:T(256)S(1)}, f32[256]{0:T(256)S(1)}, u32[]{:S(2)}, u32[]{:S(2)}) collective-permute-start(f32[256]{0:T(256)S(1)} %add.129), channel_id=1, source_target_pairs={{0,4},{4,0},{8,12},{12,8},{16,20},{20,16},{24,28},{28,24},{32,36},... | collective-permute-start | bytes 3080 | tf_op jit(solution)/shard_map/ppermute | solution.py:27
  65.3 0.8 collective-permute-done.8
  66.1 5.1 %collective-permute-start.9 = (f32[256]{0:T(256)S(1)}, f32[256]{0:T(256)S(1)}, u32[]{:S(2)}, u32[]{:S(2)}) collective-permute-start(f32[256]{0:T(256)S(1)} %add.130), channel_id=1, source_target_pairs={{0,8},{4,12},{8,0},{12,4},{16,24},{20,28},{24,16},{28,20},{32,40},... | collective-permute-start | bytes 3080 | tf_op jit(solution)/shard_map/ppermute | solution.py:27
  71.2 1.5 %collective-permute-done.9 = f32[256]{0:T(256)S(1)} collective-permute-done((f32[256]{0:T(256)S(1)}, f32[256]{0:T(256)S(1)}, u32[]{:S(2)}, u32[]{:S(2)}) %collective-permute-start.9) | collective-permute-done | bytes 1056 | tf_op jit(solution)/shard_map/ppermute | solution.py:27
  72.8 8.7 %collective-permute-start.10 = (f32[256]{0:T(256)S(1)}, f32[256]{0:T(256)S(1)}, u32[]{:S(2)}, u32[]{:S(2)}) collective-permute-start(f32[256]{0:T(256)S(1)} %add.131), channel_id=1, source_target_pairs={{0,16},{4,20},{8,24},{12,28},{16,0},{20,4},{24,8},{28,12},{32,48},... | collective-permute-start | bytes 3080 | tf_op jit(solution)/shard_map/ppermute | solution.py:27
  81.5 1.5 %collective-permute-done.10 = f32[256]{0:T(256)S(1)} collective-permute-done((f32[256]{0:T(256)S(1)}, f32[256]{0:T(256)S(1)}, u32[]{:S(2)}, u32[]{:S(2)}) %collective-permute-start.10) | collective-permute-done | bytes 1056 | tf_op jit(solution)/shard_map/ppermute | solution.py:27
  83.0 11.2 %collective-permute-start.11 = (f32[256]{0:T(256)S(1)}, f32[256]{0:T(256)S(1)}, u32[]{:S(2)}, u32[]{:S(2)}) collective-permute-start(f32[256]{0:T(256)S(1)} %add.132), channel_id=1, source_target_pairs={{0,32},{4,36},{8,40},{12,44},{16,48},{20,52},{24,56},{28,60},{32,0... | collective-permute-start | bytes 3080 | tf_op jit(solution)/shard_map/ppermute | solution.py:27
  94.2 1.5 %collective-permute-done.11 = f32[256]{0:T(256)S(1)} collective-permute-done((f32[256]{0:T(256)S(1)}, f32[256]{0:T(256)S(1)}, u32[]{:S(2)}, u32[]{:S(2)}) %collective-permute-start.11) | collective-permute-done | bytes 1056 | tf_op jit(solution)/shard_map/ppermute | solution.py:27
  95.8 14.8 %collective-permute-start.12 = (f32[256]{0:T(256)S(1)}, f32[256]{0:T(256)S(1)}, u32[]{:S(2)}, u32[]{:S(2)}) collective-permute-start(f32[256]{0:T(256)S(1)} %add.133), channel_id=1, source_target_pairs={{0,64},{4,68},{8,72},{12,76},{16,80},{20,84},{24,88},{28,92},{32,9... | collective-permute-start | bytes 3080 | tf_op jit(solution)/shard_map/ppermute | solution.py:27
  110.6 1.5 %collective-permute-done.12 = f32[256]{0:T(256)S(1)} collective-permute-done((f32[256]{0:T(256)S(1)}, f32[256]{0:T(256)S(1)}, u32[]{:S(2)}, u32[]{:S(2)}) %collective-permute-start.12) | collective-permute-done | bytes 1056 | tf_op jit(solution)/shard_map/ppermute | solution.py:27
  112.2 5.0 %collective-permute-start.13 = (f32[256]{0:T(256)S(1)}, f32[256]{0:T(256)S(1)}, u32[]{:S(2)}, u32[]{:S(2)}) collective-permute-start(f32[256]{0:T(256)S(1)} %add.134), channel_id=1, source_target_pairs={{0,128},{128,0},{256,384},{384,256},{512,640},{640,512},{768,896},... | collective-permute-start | bytes 3080 | tf_op jit(solution)/shard_map/ppermute | solution.py:27
  117.2 4.3 %collective-permute-done.13 = f32[256]{0:T(256)S(1)} collective-permute-done((f32[256]{0:T(256)S(1)}, f32[256]{0:T(256)S(1)}, u32[]{:S(2)}, u32[]{:S(2)}) %collective-permute-start.13) | collective-permute-done | bytes 1056 | tf_op jit(solution)/shard_map/ppermute | solution.py:27
  121.5 2.4 %collective-permute-start.14 = (f32[256]{0:T(256)S(1)}, f32[256]{0:T(256)S(1)}, u32[]{:S(2)}, u32[]{:S(2)}) collective-permute-start(f32[256]{0:T(256)S(1)} %add.135), channel_id=1, source_target_pairs={{0,256},{128,384},{256,0},{384,128},{512,768},{640,896},{768,512},... | collective-permute-start | bytes 3080 | tf_op jit(solution)/shard_map/ppermute | solution.py:27
  124.0 3.0 %collective-permute-done.14 = f32[256]{0:T(256)S(1)} collective-permute-done((f32[256]{0:T(256)S(1)}, f32[256]{0:T(256)S(1)}, u32[]{:S(2)}, u32[]{:S(2)}) %collective-permute-start.14) | collective-permute-done | bytes 1056 | tf_op jit(solution)/shard_map/ppermute | solution.py:27
  127.0 4.0 %collective-permute-start.15 = (f32[256]{0:T(256)S(1)}, f32[256]{0:T(256)S(1)}, u32[]{:S(2)}, u32[]{:S(2)}) collective-permute-start(f32[256]{0:T(256)S(1)} %add.136), channel_id=1, source_target_pairs={{0,512},{128,640},{256,768},{384,896},{512,0},{640,128},{768,256},... | collective-permute-start | bytes 3080 | tf_op jit(solution)/shard_map/ppermute | solution.py:27
  131.0 0.9 copy.103
  131.9 0.8 copy.104
  132.6 1.3 collective-permute-done.15
  134.0 0.5 fusion.30
  134.5 0.8 copy.105
  (116 shorter events, 2.7 us)
Async XLA Ops:
  1.7 9.8 %copy-start.29 = (f32[128]{0:T(128)S(1)}, f32[128]{0:T(128)}, u32[]{:S(2)}) copy-start(f32[128]{0:T(128)} %param.13) | copy-start | bytes 1540
  1.7 9.8 %copy-start.15 = (bf16[1,128,1024]{2,1,0:T(8,128)(2,1)S(1)}, bf16[1,128,1024]{2,1,0:T(8,128)(2,1)}, u32[]{:S(2)}) copy-start(bf16[1,128,1024]{2,1,0:T(8,128)(2,1)} %param.7) | copy-start | bytes 786436
  3.7 16.4 %copy-start.1 = (bf16[128,4,128]{2,0,1:T(8,128)(2,1)}, bf16[128,4,128]{2,0,1:T(8,128)(2,1)S(1)}, u32[]{:S(2)}) copy-start(bf16[128,4,128]{2,0,1:T(8,128)(2,1)S(1)} %copy.85) | copy-start | bytes 393220
  4.0 8.1 %copy-start.2 = (f32[128,64]{1,0:T(8,128)}, f32[128,64]{1,0:T(8,128)S(1)}, u32[]{:S(2)}) copy-start(f32[128,64]{1,0:T(8,128)S(1)} %get-tuple-element.58) | copy-start | bytes 98308
  4.1 8.1 %copy-start.5 = (f32[128,64]{1,0:T(8,128)}, f32[128,64]{1,0:T(8,128)S(1)}, u32[]{:S(2)}) copy-start(f32[128,64]{1,0:T(8,128)S(1)} %get-tuple-element.59) | copy-start | bytes 98308
  5.0 6.4 %copy-start.20 = (bf16[128,4,64]{2,0,1:T(8,128)(2,1)}, bf16[128,4,64]{2,0,1:T(8,128)(2,1)S(1)}, u32[]{:S(2)}) copy-start(bf16[128,4,64]{2,0,1:T(8,128)(2,1)S(1)} %get-tuple-element.51) | copy-start | bytes 196612
  5.0 13.2 %copy-start.18 = (bf16[128,4,64]{2,0,1:T(8,128)(2,1)}, bf16[128,4,64]{2,0,1:T(8,128)(2,1)S(1)}, u32[]{:S(2)}) copy-start(bf16[128,4,64]{2,0,1:T(8,128)(2,1)S(1)} %get-tuple-element.50) | copy-start | bytes 196612
  5.1 6.8 %copy-start.27 = (f32[128]{0:T(128)S(1)}, f32[128]{0:T(128)}, u32[]{:S(2)}) copy-start(f32[128]{0:T(128)} %param.12) | copy-start | bytes 1540
  5.2 9.6 %collective-permute-start.1 = (bf16[129,8,128]{2,0,1:T(8,128)(2,1)S(1)}, bf16[129,8,128]{2,0,1:T(8,128)(2,1)S(1)}, u32[]{:S(2)}, u32[]{:S(2)}) collective-permute-start(bf16[129,8,128]{2,0,1:T(8,128)(2,1)S(1)} %pad_maximum_fusion.1), channel_id=1, source_target_pairs={{0,4},{4,8},{8,12},{12,16},{16,20},{20,24},{24,28},{28,32},{32,36}... | collective-permute-start | bytes 792584 | tf_op jit(solution)/shard_map/ppermute | solution.py:19
  7.0 10.9 %collective-permute-start = (bf16[129,8,128]{2,0,1:T(8,128)(2,1)S(1)}, bf16[129,8,128]{2,0,1:T(8,128)(2,1)S(1)}, u32[]{:S(2)}, u32[]{:S(2)}) collective-permute-start(bf16[129,8,128]{2,0,1:T(8,128)(2,1)S(1)} %pad_maximum_fusion.1), channel_id=1, source_target_pairs={{0,8},{4,12},{8,16},{12,20},{16,24},{20,28},{24,32},{28,36},{32,40... | collective-permute-start | bytes 792584 | tf_op jit(solution)/shard_map/ppermute | solution.py:19
  11.9 1.8 %copy-start.10 = (f32[128,8]{1,0:T(8,128)}, f32[128,8]{1,0:T(8,128)S(1)}, u32[]{:S(2)}) copy-start(f32[128,8]{1,0:T(8,128)S(1)} %add_rsqrt_fusion) | copy-start | bytes 12292
  12.1 1.2 copy-start.22
  12.5 5.8 %copy-start.12 = (bf16[128,8,64]{2,0,1:T(8,128)(2,1)}, bf16[128,8,64]{2,0,1:T(8,128)(2,1)S(1)}, u32[]{:S(2)}) copy-start(bf16[128,8,64]{2,0,1:T(8,128)(2,1)S(1)} %copy.88) | copy-start | bytes 393220
  12.5 5.4 %copy-start.31 = (s32[1,128]{1,0:T(1,128)S(1)}, s32[1,128]{1,0:T(1,128)}, u32[]{:S(2)}) copy-start(s32[1,128]{1,0:T(1,128)} %param.11) | copy-start | bytes 1540
  18.2 1.7 %copy-start.23 = (bf16[128,4,128]{2,0,1:T(8,128)(2,1)}, bf16[128,4,128]{2,0,1:T(8,128)(2,1)S(1)}, u32[]{:S(2)}) copy-start(bf16[128,4,128]{2,0,1:T(8,128)(2,1)S(1)} %get-tuple-element.54) | copy-start | bytes 393220
  18.2 2.0 %copy-start.8 = (bf16[128,4,128]{2,0,1:T(8,128)(2,1)}, bf16[128,4,128]{2,0,1:T(8,128)(2,1)S(1)}, u32[]{:S(2)}) copy-start(bf16[128,4,128]{2,0,1:T(8,128)(2,1)S(1)} %get-tuple-element.55) | copy-start | bytes 393220
  18.2 1.7 %copy-start.25 = (bf16[128,4,128]{2,0,1:T(8,128)(2,1)}, bf16[128,4,128]{2,0,1:T(8,128)(2,1)S(1)}, u32[]{:S(2)}) copy-start(bf16[128,4,128]{2,0,1:T(8,128)(2,1)S(1)} %get-tuple-element.52) | copy-start | bytes 393220
  18.2 1.9 %copy-start.9 = (bf16[128,4,128]{2,0,1:T(8,128)(2,1)}, bf16[128,4,128]{2,0,1:T(8,128)(2,1)S(1)}, u32[]{:S(2)}) copy-start(bf16[128,4,128]{2,0,1:T(8,128)(2,1)S(1)} %get-tuple-element.53) | copy-start | bytes 393220
  25.4 1.6 %copy-start.19 = (bf16[128,4,64]{2,0,1:T(8,128)(2,1)S(1)}, bf16[128,4,64]{2,0,1:T(8,128)(2,1)}, u32[]{:S(2)}) copy-start(bf16[128,4,64]{2,0,1:T(8,128)(2,1)} %copy-done.18) | copy-start | bytes 196612
  25.4 1.6 %copy-start.21 = (bf16[128,4,64]{2,0,1:T(8,128)(2,1)S(1)}, bf16[128,4,64]{2,0,1:T(8,128)(2,1)}, u32[]{:S(2)}) copy-start(bf16[128,4,64]{2,0,1:T(8,128)(2,1)} %copy-done.20) | copy-start | bytes 196612
  25.4 1.6 %copy-start.24 = (bf16[128,4,128]{2,0,1:T(8,128)(2,1)S(1)}, bf16[128,4,128]{2,0,1:T(8,128)(2,1)}, u32[]{:S(2)}) copy-start(bf16[128,4,128]{2,0,1:T(8,128)(2,1)} %copy-done.23) | copy-start | bytes 393220
  25.4 1.6 %copy-start.26 = (bf16[128,4,128]{2,0,1:T(8,128)(2,1)S(1)}, bf16[128,4,128]{2,0,1:T(8,128)(2,1)}, u32[]{:S(2)}) copy-start(bf16[128,4,128]{2,0,1:T(8,128)(2,1)} %copy-done.25) | copy-start | bytes 393220
  27.0 1.0 copy-start.13
  27.0 1.0 copy-start.14
  29.5 4.1 %copy-start.3 = (f32[128,64]{1,0:T(8,128)S(1)}, f32[128,64]{1,0:T(8,128)}, u32[]{:S(2)}) copy-start(f32[128,64]{1,0:T(8,128)} %copy-done.2) | copy-start | bytes 98308
  29.5 4.1 %copy-start.6 = (f32[128,64]{1,0:T(8,128)S(1)}, f32[128,64]{1,0:T(8,128)}, u32[]{:S(2)}) copy-start(f32[128,64]{1,0:T(8,128)} %copy-done.5) | copy-start | bytes 98308
  31.6 3.2 %copy-start.11 = (f32[128,8]{1,0:T(8,128)S(1)}, f32[128,8]{1,0:T(8,128)}, u32[]{:S(2)}) copy-start(f32[128,8]{1,0:T(8,128)} %copy-done.10) | copy-start | bytes 12292
  31.6 3.2 %copy-start.28 = (f32[128]{0:T(128)S(1)}, f32[128]{0:T(128)}, u32[]{:S(2)}) copy-start(f32[128]{0:T(128)} %param.12) | copy-start | bytes 1540
  35.9 6.5 %copy-start.16 = (bf16[1,128,1024]{2,1,0:T(8,128)(2,1)S(1)}, bf16[1,128,1024]{2,1,0:T(8,128)(2,1)}, u32[]{:S(2)}) copy-start(bf16[1,128,1024]{2,1,0:T(8,128)(2,1)} %param.7) | copy-start | bytes 786436
  36.8 5.6 %copy-start = (f32[1,128,1024]{2,1,0:T(8,128)S(1)}, f32[1,128,1024]{2,1,0:T(8,128)}, u32[]{:S(2)}) copy-start(f32[1,128,1024]{2,1,0:T(8,128)} %mul.390) | copy-start | bytes 1572868
  39.8 8.4 %collective-permute-start.3 = (bf16[128,4,128]{2,0,1:T(8,128)(2,1)S(1)}, bf16[128,4,128]{2,0,1:T(8,128)(2,1)S(1)}, u32[]{:S(2)}, u32[]{:S(2)}) collective-permute-start(bf16[128,4,128]{2,0,1:T(8,128)(2,1)S(1)} %get-tuple-element.49), channel_id=1, source_target_pairs={{8,0},{12,4},{16,8},{20,12},{24,16},{28,20},{32,24},{36,28},{40,32... | collective-permute-start | bytes 393224 | tf_op jit(solution)/shard_map/ppermute | solution.py:19
  41.1 7.1 %collective-permute-start.2 = (bf16[128,4,128]{2,0,1:T(8,128)(2,1)S(1)}, bf16[128,4,128]{2,0,1:T(8,128)(2,1)S(1)}, u32[]{:S(2)}, u32[]{:S(2)}) collective-permute-start(bf16[128,4,128]{2,0,1:T(8,128)(2,1)S(1)} %get-tuple-element.48), channel_id=1, source_target_pairs={{4,0},{8,4},{12,8},{16,12},{20,16},{24,20},{28,24},{32,28},{36,32}... | collective-permute-start | bytes 393224 | tf_op jit(solution)/shard_map/ppermute | solution.py:19
  44.5 4.7 %copy-start.4 = (f32[128,64]{1,0:T(8,128)S(1)}, f32[128,64]{1,0:T(8,128)}, u32[]{:S(2)}) copy-start(f32[128,64]{1,0:T(8,128)} %copy-done.2) | copy-start | bytes 98308
  44.5 4.7 %copy-start.7 = (f32[128,64]{1,0:T(8,128)S(1)}, f32[128,64]{1,0:T(8,128)}, u32[]{:S(2)}) copy-start(f32[128,64]{1,0:T(8,128)} %copy-done.5) | copy-start | bytes 98308
  44.9 4.5 %copy-start.30 = (f32[128]{0:T(128)S(1)}, f32[128]{0:T(128)}, u32[]{:S(2)}) copy-start(f32[128]{0:T(128)} %param.13) | copy-start | bytes 1540
  49.4 81.6 %copy-start.17 = (bf16[4,128,2,128]{3,1,2,0:T(8,128)(2,1)S(1)}, bf16[4,128,2,128]{3,1,2,0:T(8,128)(2,1)}, u32[]{:S(2)}) copy-start(bf16[4,128,2,128]{3,1,2,0:T(8,128)(2,1)} %get-tuple-element.63) | copy-start | bytes 786436
  50.1 6.1 %collective-permute-start.6 = (f32[256]{0:T(256)S(1)}, f32[256]{0:T(256)S(1)}, u32[]{:S(2)}, u32[]{:S(2)}) collective-permute-start(f32[256]{0:T(256)S(1)} %pad_maximum_fusion.6), channel_id=1, source_target_pairs={{0,1},{1,0},{2,3},{3,2},{4,5},{5,4},{6,7},{7,6},{8,9},{9,8},{10,11... | collective-permute-start | bytes 3080 | tf_op jit(solution)/shard_map/ppermute | solution.py:27
  53.6 80.8 %collective-permute-start.5 = (f32[128,4,128]{0,2,1:T(8,128)S(1)}, f32[128,4,128]{0,2,1:T(8,128)S(1)}, u32[]{:S(2)}, u32[]{:S(2)}) collective-permute-start(f32[128,4,128]{0,2,1:T(8,128)S(1)} %get-tuple-element.39), channel_id=1, source_target_pairs={{8,0},{12,4},{16,8},{20,12},{24,16},{28,20},{32,24},{36,28},{40,32... | collective-permute-start | bytes 786440 | tf_op jit(solution)/shard_map/ppermute | solution.py:19
  54.9 79.5 %collective-permute-start.4 = (f32[128,4,128]{0,2,1:T(8,128)S(1)}, f32[128,4,128]{0,2,1:T(8,128)S(1)}, u32[]{:S(2)}, u32[]{:S(2)}) collective-permute-start(f32[128,4,128]{0,2,1:T(8,128)S(1)} %get-tuple-element.38), channel_id=1, source_target_pairs={{4,0},{8,4},{12,8},{16,12},{20,16},{24,20},{28,24},{32,28},{36,32}... | collective-permute-start | bytes 786440 | tf_op jit(solution)/shard_map/ppermute | solution.py:19
  56.3 6.4 %collective-permute-start.7 = (f32[256]{0:T(256)S(1)}, f32[256]{0:T(256)S(1)}, u32[]{:S(2)}, u32[]{:S(2)}) collective-permute-start(f32[256]{0:T(256)S(1)} %fusion.24), channel_id=1, source_target_pairs={{0,2},{1,3},{2,0},{3,1},{4,6},{5,7},{6,4},{7,5},{8,10},{9,11},{10,... | collective-permute-start | bytes 3080 | tf_op jit(solution)/shard_map/ppermute | solution.py:27
  62.6 3.5 %collective-permute-start.8 = (f32[256]{0:T(256)S(1)}, f32[256]{0:T(256)S(1)}, u32[]{:S(2)}, u32[]{:S(2)}) collective-permute-start(f32[256]{0:T(256)S(1)} %add.129), channel_id=1, source_target_pairs={{0,4},{4,0},{8,12},{12,8},{16,20},{20,16},{24,28},{28,24},{32,36},... | collective-permute-start | bytes 3080 | tf_op jit(solution)/shard_map/ppermute | solution.py:27
  66.1 6.7 %collective-permute-start.9 = (f32[256]{0:T(256)S(1)}, f32[256]{0:T(256)S(1)}, u32[]{:S(2)}, u32[]{:S(2)}) collective-permute-start(f32[256]{0:T(256)S(1)} %add.130), channel_id=1, source_target_pairs={{0,8},{4,12},{8,0},{12,4},{16,24},{20,28},{24,16},{28,20},{32,40},... | collective-permute-start | bytes 3080 | tf_op jit(solution)/shard_map/ppermute | solution.py:27
  72.8 10.2 %collective-permute-start.10 = (f32[256]{0:T(256)S(1)}, f32[256]{0:T(256)S(1)}, u32[]{:S(2)}, u32[]{:S(2)}) collective-permute-start(f32[256]{0:T(256)S(1)} %add.131), channel_id=1, source_target_pairs={{0,16},{4,20},{8,24},{12,28},{16,0},{20,4},{24,8},{28,12},{32,48},... | collective-permute-start | bytes 3080 | tf_op jit(solution)/shard_map/ppermute | solution.py:27
  83.0 12.8 %collective-permute-start.11 = (f32[256]{0:T(256)S(1)}, f32[256]{0:T(256)S(1)}, u32[]{:S(2)}, u32[]{:S(2)}) collective-permute-start(f32[256]{0:T(256)S(1)} %add.132), channel_id=1, source_target_pairs={{0,32},{4,36},{8,40},{12,44},{16,48},{20,52},{24,56},{28,60},{32,0... | collective-permute-start | bytes 3080 | tf_op jit(solution)/shard_map/ppermute | solution.py:27
  95.8 16.4 %collective-permute-start.12 = (f32[256]{0:T(256)S(1)}, f32[256]{0:T(256)S(1)}, u32[]{:S(2)}, u32[]{:S(2)}) collective-permute-start(f32[256]{0:T(256)S(1)} %add.133), channel_id=1, source_target_pairs={{0,64},{4,68},{8,72},{12,76},{16,80},{20,84},{24,88},{28,92},{32,9... | collective-permute-start | bytes 3080 | tf_op jit(solution)/shard_map/ppermute | solution.py:27
  112.2 9.4 %collective-permute-start.13 = (f32[256]{0:T(256)S(1)}, f32[256]{0:T(256)S(1)}, u32[]{:S(2)}, u32[]{:S(2)}) collective-permute-start(f32[256]{0:T(256)S(1)} %add.134), channel_id=1, source_target_pairs={{0,128},{128,0},{256,384},{384,256},{512,640},{640,512},{768,896},... | collective-permute-start | bytes 3080 | tf_op jit(solution)/shard_map/ppermute | solution.py:27
  121.5 5.5 %collective-permute-start.14 = (f32[256]{0:T(256)S(1)}, f32[256]{0:T(256)S(1)}, u32[]{:S(2)}, u32[]{:S(2)}) collective-permute-start(f32[256]{0:T(256)S(1)} %add.135), channel_id=1, source_target_pairs={{0,256},{128,384},{256,0},{384,128},{512,768},{640,896},{768,512},... | collective-permute-start | bytes 3080 | tf_op jit(solution)/shard_map/ppermute | solution.py:27
  127.0 7.0 %collective-permute-start.15 = (f32[256]{0:T(256)S(1)}, f32[256]{0:T(256)S(1)}, u32[]{:S(2)}, u32[]{:S(2)}) collective-permute-start(f32[256]{0:T(256)S(1)} %add.136), channel_id=1, source_target_pairs={{0,512},{128,640},{256,768},{384,896},{512,0},{640,128},{768,256},... | collective-permute-start | bytes 3080 | tf_op jit(solution)/shard_map/ppermute | solution.py:27

commit v4 on v3

--- a/solution.py
+++ b/solution.py
@@ -104,8 +104,9 @@
         file_row.astype(jnp.bfloat16)[None, None, :], (1, 2 * kheads, HEAD_WIDTH)
     )
     packed = jnp.concatenate([jnp.concatenate([k_rot, value_own], axis=1), file_slab], axis=0)
-    key_list, value_list, file_list = ([], [], [])
+    key_list, value_list, file_list, unit_list = ([], [], [], [])
     for offset in range(reach_count, 0, -1):
+        unit_list.append(passed_along(k_unit, "ctx", offset))
         far = passed_along(packed, "ctx", offset)
         key_list.append(far[:row_count, :kheads])
         value_list.append(far[:row_count, kheads:])
@@ -143,6 +144,8 @@
     grad_values = jnp.einsum(
         "hgqk,qhgd->khd", weights_low, out_grads, preferred_element_type=jnp.float32
     )
+    key_units = jnp.concatenate(unit_list + [k_unit], axis=0)
+    k_term = jnp.sum(unrotate(grad_keys, key_pos) * key_units, axis=(0, 1))
     key_own = grad_keys[reach_count * row_count :]
     value_grad = grad_values[reach_count * row_count :]
     for offset in range(1, reach_count + 1):
@@ -156,7 +159,7 @@
     dq_grad, q_term = restore(
         grad_queries.reshape(row_count, qheads, HEAD_WIDTH), q_unit, q_inv, q_gain, positions
     )
-    dk_grad, k_term = restore(key_own, k_unit, k_inv, k_gain, positions)
+    dk_grad, _ = restore(key_own, k_unit, k_inv, k_gain, positions)
     gain_terms = jnp.concatenate([q_term, k_term])
     for axis in ("head", "ctx", "fsdp"):
         gain_terms = butterfly_sum(gain_terms, axis)

time: 136 us -> 154 us (1.13)
  the two profiles are of different devices: /device:TPU:18 before, /device:TPU:1 now
where the time goes in v4:
time: 154 us; the launch traced here: 153 us
  starting transfers between devices  80.1 us (52%)
  local copies, waits for them, and re-layouts  24.5 us (16%)
  waiting for transfers between devices  22.2 us (14%)
  other arithmetic  17.8 us (12%)
  matrix products  6.49 us (4%)
    ppermute x10, starting transfers between devices, butterfly_sum(): value = value + lax.ppermute(value, axis, pairs)  51.6 us
    ppermute x8, starting transfers between devices, passed_along(): return lax.ppermute(value, axis, pairs)  28.5 us
    ppermute x10, waiting for transfers between devices, butterfly_sum(): value = value + lax.ppermute(value, axis, pairs)  13.7 us
    unnamed x69, local copies, waits for them, and re-layouts  12.2 us
    ppermute x8, waiting for transfers between devices, passed_along(): return lax.ppermute(value, axis, pairs)  8.53 us
  transfers between devices with their start and end apart: 18, of which 10 were waited for; matrix products, arithmetic and copies ran while one was open for 26% of the time, Pallas kernels for 0%

profile of v4, /device:TPU:1, one launch (start us, length us, event | category | flops | bytes accessed | tf_op | source)
XLA Modules:
  0.0 152.6 jit_solution(6069087758460935575)
XLA Ops:
  0.6 1.0 copy.82
  1.9 0.7 bitcast_convert_fusion.1
  2.6 1.0 copy.84
  4.1 0.8 broadcast_multiply_fusion
  5.2 5.4 %collective-permute-start.1 = (bf16[129,8,128]{2,0,1:T(8,128)(2,1)S(1)}, bf16[129,8,128]{2,0,1:T(8,128)(2,1)}, u32[]{:S(2)}, u32[]{:S(2)}) collective-permute-start(bf16[129,8,128]{2,0,1:T(8,128)(2,1)S(1)} %pad_maximum_fusion.1), channel_id=1, source_target_pairs={{0,4},{4,8},{8,12},{12,16},{16,20},{20,24},{24,28},{28,32},{32,36}... | collective-permute-start | bytes 792584 | tf_op jit(solution)/shard_map/ppermute | solution.py:19
  10.6 4.7 %collective-permute-start = (bf16[129,8,128]{2,0,1:T(8,128)(2,1)S(1)}, bf16[129,8,128]{2,0,1:T(8,128)(2,1)}, u32[]{:S(2)}, u32[]{:S(2)}) collective-permute-start(bf16[129,8,128]{2,0,1:T(8,128)(2,1)S(1)} %pad_maximum_fusion.1), channel_id=1, source_target_pairs={{0,8},{4,12},{8,16},{12,20},{16,24},{20,28},{24,32},{28,36},{32,40... | collective-permute-start | bytes 792584 | tf_op jit(solution)/shard_map/ppermute | solution.py:19
  15.3 1.9 %collective-permute-start.7 = (f32[128,4,128]{2,0,1:T(8,128)S(1)}, f32[128,4,128]{2,0,1:T(8,128)}, u32[]{:S(2)}, u32[]{:S(2)}) collective-permute-start(f32[128,4,128]{2,0,1:T(8,128)S(1)} %get-tuple-element.35), channel_id=1, source_target_pairs={{0,4},{4,8},{8,12},{12,16},{16,20},{20,24},{24,28},{28,32},{32,36}... | collective-permute-start | bytes 786440 | tf_op jit(solution)/shard_map/ppermute | solution.py:19
  17.2 4.3 %collective-permute-start.6 = (f32[128,4,128]{2,0,1:T(8,128)S(1)}, f32[128,4,128]{2,0,1:T(8,128)}, u32[]{:S(2)}, u32[]{:S(2)}) collective-permute-start(f32[128,4,128]{2,0,1:T(8,128)S(1)} %get-tuple-element.35), channel_id=1, source_target_pairs={{0,8},{4,12},{8,16},{12,20},{16,24},{20,28},{24,32},{28,36},{32,40... | collective-permute-start | bytes 786440 | tf_op jit(solution)/shard_map/ppermute | solution.py:19
  22.5 1.5 multiply_cosine_fusion
  24.1 0.7 copy.88
  24.8 0.7 copy.87
  26.2 0.9 mul.437
  27.0 0.7 fusion.19
  27.7 0.7 fusion.20
  28.6 1.0 fusion.32
  29.6 1.1 fusion.31
  30.8 1.7 %fusion.34 = (f32[4,2,128]{2,1,0:T(2,128)S(1)}, f32[4,2,128,384]{2,3,1,0:T(8,128)S(1)}) fusion(bf16[128,4,2,64]{3,0,2,1:T(8,128)(2,1)} %bitcast.111, bf16[128,4,2,64]{3,0,2,1:T(8,128)(2,1)} %bitcast.113, bf16[128,4,64]{2,0,1:T(8,128)(2,1)} %copy-done.20, bf16[128,4,64]{2,0,1:T(8,128)(2,1)} %copy-done.18, bf16[128,4,128]{2,0,1:T(8,128)(2,1)S(1)} %get-tuple-element.56, ...), kind=kOutput, calls=%fused_computation.96 | convolution fusion | flops 103939072 | bytes 2281472 | tf_op jit(solution)/shard_map/qhgd,khd->hgqk/dot_general | solution.py:83
  32.8 0.6 copy-done.3
  33.4 1.3 bitcast_convert_fusion
  34.7 1.4 copy.115
  36.1 1.5 %multiply_reduce_fusion = f32[4,2,128]{1,0,2:T(4,128)} fusion(f32[4,2,128,128]{3,1,0,2:T(2,128)S(1)} %copy.115, bf16[128,4,2,128]{3,2,1,0:T(2,128)(2,1)S(1)} %reshape_squeeze.7), kind=kLoop, calls=%fused_computation.20 | loop fusion | flops 392192 | bytes 790528
  37.6 1.0 copy.116
  38.7 1.5 fusion.1
  41.3 1.2 fusion.35
  42.5 0.8 fusion.29
  43.3 2.0 %copy.130 = f32[128,8,64]{2,1,0:T(8,128)} copy(f32[128,8,64]{0,2,1:T(8,128)} %get-tuple-element.46) | data formatting | bytes 524288
  45.3 2.0 %copy.129 = f32[128,8,64]{2,1,0:T(8,128)} copy(f32[128,8,64]{0,2,1:T(8,128)} %get-tuple-element.47) | data formatting | bytes 524288
  47.3 1.3 multiply_add_fusion.1
  48.6 1.8 %multiply_reduce_fusion.2 = (f32[128,8]{1,0:T(8,128)}, f32[128,8,128]{2,1,0:T(8,128)}) fusion(f32[128,8,128]{2,1,0:T(8,128)S(1)} %bitcast.108, f32[128]{0:T(128)S(1)} %copy-done.27, f32[128,8]{1,0:T(8,128)S(1)} %copy-done.12, f32[128,8,64]{2,1,0:T(8,128)S(1)} %get-tuple-element.41, f32[128,8,64]{2,1,0:T(8,128)S(1)} %get-tuple-element.40), kind=kLoop, calls=%fused_computation.23 | loop fusion | flops 654336 | bytes 1581568 | tf_op jit(solution)/shard_map/reduce_sum | solution.py:71
  50.4 1.9 %concatenate.57 = f32[1,128,1024]{2,1,0:T(8,128)} reshape(f32[128,8,128]{2,1,0:T(8,128)} %get-tuple-element.33) | data formatting | bytes 1048576 | tf_op jit(solution)/shard_map/concatenate | solution.py:54
  52.3 0.8 broadcast_multiply_fusion.2
  53.4 0.9 mul.454
  54.3 2.4 %multiply_reduce_fusion.1 = (f32[1024]{0:T(1024)S(1)}, bf16[1,128,1024]{2,1,0:T(8,128)(2,1)}) fusion(f32[1,128,1024]{2,1,0:T(8,128)} %concatenate.57, f32[1,128,1024]{2,1,0:T(8,128)} %mul.437, bf16[1,128,1024]{2,1,0:T(8,128)(2,1)} %param.7, f32[1,128,1024]{2,1,0:T(8,128)} %mul.454, f32[1024]{0:T(1024)S(1)} %broadcast_bitcast_fusion), kind=kLoop, calls=%fused_computation.21 | loop fusion | flops 1178624 | bytes 2105344 | tf_op jit(solution)/shard_map/reduce_sum | solution.py:69
  57.1 1.4 fusion.5
  58.5 3.2 %collective-permute-start.8 = (f32[256]{0:T(256)S(1)}, f32[256]{0:T(256)S(1)}, u32[]{:S(2)}, u32[]{:S(2)}) collective-permute-start(f32[256]{0:T(256)S(1)} %pad_maximum_fusion.6), channel_id=1, source_target_pairs={{0,1},{1,0},{2,3},{3,2},{4,5},{5,4},{6,7},{7,6},{8,9},{9,8},{10,11... | collective-permute-start | bytes 3080 | tf_op jit(solution)/shard_map/ppermute | solution.py:27
  61.7 1.1 collective-permute-done.8
  62.8 4.2 %collective-permute-start.9 = (f32[256]{0:T(256)S(1)}, f32[256]{0:T(256)S(1)}, u32[]{:S(2)}, u32[]{:S(2)}) collective-permute-start(f32[256]{0:T(256)S(1)} %fusion.27), channel_id=1, source_target_pairs={{0,2},{1,3},{2,0},{3,1},{4,6},{5,7},{6,4},{7,5},{8,10},{9,11},{10,... | collective-permute-start | bytes 3080 | tf_op jit(solution)/shard_map/ppermute | solution.py:27
  67.0 1.0 collective-permute-done.9
  68.0 10.0 %collective-permute-start.10 = (f32[256]{0:T(256)S(1)}, f32[256]{0:T(256)S(1)}, u32[]{:S(2)}, u32[]{:S(2)}) collective-permute-start(f32[256]{0:T(256)S(1)} %add.137), channel_id=1, source_target_pairs={{0,4},{4,0},{8,12},{12,8},{16,20},{20,16},{24,28},{28,24},{32,36},... | collective-permute-start | bytes 3080 | tf_op jit(solution)/shard_map/ppermute | solution.py:27
  78.0 0.8 collective-permute-done.10
  78.8 1.9 %collective-permute-start.11 = (f32[256]{0:T(256)S(1)}, f32[256]{0:T(256)S(1)}, u32[]{:S(2)}, u32[]{:S(2)}) collective-permute-start(f32[256]{0:T(256)S(1)} %add.138), channel_id=1, source_target_pairs={{0,8},{4,12},{8,0},{12,4},{16,24},{20,28},{24,16},{28,20},{32,40},... | collective-permute-start | bytes 3080 | tf_op jit(solution)/shard_map/ppermute | solution.py:27
  80.7 2.4 %collective-permute-done.11 = f32[256]{0:T(256)S(1)} collective-permute-done((f32[256]{0:T(256)S(1)}, f32[256]{0:T(256)S(1)}, u32[]{:S(2)}, u32[]{:S(2)}) %collective-permute-start.11) | collective-permute-done | bytes 1056 | tf_op jit(solution)/shard_map/ppermute | solution.py:27
  83.1 1.9 %collective-permute-start.12 = (f32[256]{0:T(256)S(1)}, f32[256]{0:T(256)S(1)}, u32[]{:S(2)}, u32[]{:S(2)}) collective-permute-start(f32[256]{0:T(256)S(1)} %add.139), channel_id=1, source_target_pairs={{0,16},{4,20},{8,24},{12,28},{16,0},{20,4},{24,8},{28,12},{32,48},... | collective-permute-start | bytes 3080 | tf_op jit(solution)/shard_map/ppermute | solution.py:27
  85.1 3.3 %collective-permute-done.12 = f32[256]{0:T(256)S(1)} collective-permute-done((f32[256]{0:T(256)S(1)}, f32[256]{0:T(256)S(1)}, u32[]{:S(2)}, u32[]{:S(2)}) %collective-permute-start.12) | collective-permute-done | bytes 1056 | tf_op jit(solution)/shard_map/ppermute | solution.py:27
  88.3 6.5 %collective-permute-start.13 = (f32[256]{0:T(256)S(1)}, f32[256]{0:T(256)S(1)}, u32[]{:S(2)}, u32[]{:S(2)}) collective-permute-start(f32[256]{0:T(256)S(1)} %add.140), channel_id=1, source_target_pairs={{0,32},{4,36},{8,40},{12,44},{16,48},{20,52},{24,56},{28,60},{32,0... | collective-permute-start | bytes 3080 | tf_op jit(solution)/shard_map/ppermute | solution.py:27
  94.9 1.7 %collective-permute-done.13 = f32[256]{0:T(256)S(1)} collective-permute-done((f32[256]{0:T(256)S(1)}, f32[256]{0:T(256)S(1)}, u32[]{:S(2)}, u32[]{:S(2)}) %collective-permute-start.13) | collective-permute-done | bytes 1056 | tf_op jit(solution)/shard_map/ppermute | solution.py:27
  96.6 10.4 %collective-permute-start.14 = (f32[256]{0:T(256)S(1)}, f32[256]{0:T(256)S(1)}, u32[]{:S(2)}, u32[]{:S(2)}) collective-permute-start(f32[256]{0:T(256)S(1)} %add.141), channel_id=1, source_target_pairs={{0,64},{4,68},{8,72},{12,76},{16,80},{20,84},{24,88},{28,92},{32,9... | collective-permute-start | bytes 3080 | tf_op jit(solution)/shard_map/ppermute | solution.py:27
  107.0 2.6 %collective-permute-done.14 = f32[256]{0:T(256)S(1)} collective-permute-done((f32[256]{0:T(256)S(1)}, f32[256]{0:T(256)S(1)}, u32[]{:S(2)}, u32[]{:S(2)}) %collective-permute-start.14) | collective-permute-done | bytes 1056 | tf_op jit(solution)/shard_map/ppermute | solution.py:27
  109.6 6.7 %collective-permute-start.15 = (f32[256]{0:T(256)S(1)}, f32[256]{0:T(256)S(1)}, u32[]{:S(2)}, u32[]{:S(2)}) collective-permute-start(f32[256]{0:T(256)S(1)} %add.142), channel_id=1, source_target_pairs={{0,128},{128,0},{256,384},{384,256},{512,640},{640,512},{768,896},... | collective-permute-start | bytes 3080 | tf_op jit(solution)/shard_map/ppermute | solution.py:27
  116.3 0.7 fusion.30
  117.0 0.8 collective-permute-done.15
  118.4 2.5 %collective-permute-start.16 = (f32[256]{0:T(256)}, f32[256]{0:T(256)}, u32[]{:S(2)}, u32[]{:S(2)}) collective-permute-start(f32[256]{0:T(256)} %add.143), channel_id=1, source_target_pairs={{0,256},{128,384},{256,0},{384,128},{512,768},{640,896},{768,512},... | collective-permute-start | bytes 3080 | tf_op jit(solution)/shard_map/ppermute | solution.py:27
  121.3 1.8 %copy.103 = bf16[1,128,1024]{2,1,0:T(8,128)(2,1)} copy(bf16[1,128,1024]{1,2,0:T(8,128)(2,1)} %bitcast.115) | data formatting | bytes 524288
  123.1 1.4 collective-permute-start.3
  124.6 7.5 %collective-permute-start.2 = (bf16[128,4,128]{2,0,1:T(8,128)(2,1)}, bf16[128,4,128]{2,0,1:T(8,128)(2,1)S(1)}, u32[]{:S(2)}, u32[]{:S(2)}) collective-permute-start(bf16[128,4,128]{2,0,1:T(8,128)(2,1)} %get-tuple-element.50), channel_id=1, source_target_pairs={{4,0},{8,4},{12,8},{16,12},{20,16},{24,20},{28,24},{32,28},{36,32}... | collective-permute-start | bytes 393224 | tf_op jit(solution)/shard_map/ppermute | solution.py:19
  132.1 0.7 add.144
  132.8 4.3 %collective-permute-start.17 = (f32[256]{0:T(256)S(1)}, f32[256]{0:T(256)S(1)}, u32[]{:S(2)}, u32[]{:S(2)}) collective-permute-start(f32[256]{0:T(256)S(1)} %add.144), channel_id=1, source_target_pairs={{0,512},{128,640},{256,768},{384,896},{512,0},{640,128},{768,256},... | collective-permute-start | bytes 3080 | tf_op jit(solution)/shard_map/ppermute | solution.py:27
  137.2 0.7 fusion.28
  137.9 1.3 collective-permute-start.5
  139.2 1.9 %collective-permute-start.4 = (f32[128,4,128]{0,2,1:T(8,128)S(1)}, f32[128,4,128]{0,2,1:T(8,128)S(1)}, u32[]{:S(2)}, u32[]{:S(2)}) collective-permute-start(f32[128,4,128]{0,2,1:T(8,128)S(1)} %get-tuple-element.42), channel_id=1, source_target_pairs={{4,0},{8,4},{12,8},{16,12},{20,16},{24,20},{28,24},{32,28},{36,32}... | collective-permute-start | bytes 786440 | tf_op jit(solution)/shard_map/ppermute | solution.py:19
  142.5 0.8 copy.104
  143.2 5.5 %collective-permute-done.5 = f32[128,4,128]{0,2,1:T(8,128)S(1)} collective-permute-done((f32[128,4,128]{0,2,1:T(8,128)}, f32[128,4,128]{0,2,1:T(8,128)S(1)}, u32[]{:S(2)}, u32[]{:S(2)}) %collective-permute-start.5) | collective-permute-done | bytes 262176 | tf_op jit(solution)/shard_map/ppermute | solution.py:19
  148.8 3.0 %collective-permute-done.4 = f32[128,4,128]{0,2,1:T(8,128)S(1)} collective-permute-done((f32[128,4,128]{0,2,1:T(8,128)S(1)}, f32[128,4,128]{0,2,1:T(8,128)S(1)}, u32[]{:S(2)}, u32[]{:S(2)}) %collective-permute-start.4) | collective-permute-done | bytes 262176 | tf_op jit(solution)/shard_map/ppermute | solution.py:19
  151.8 0.8 copy.105
  (119 shorter events, 6.8 us)
Async XLA Ops:
  1.8 19.8 %copy-start.15 = (bf16[1,128,1024]{2,1,0:T(8,128)(2,1)S(1)}, bf16[1,128,1024]{2,1,0:T(8,128)(2,1)}, u32[]{:S(2)}) copy-start(bf16[1,128,1024]{2,1,0:T(8,128)(2,1)} %param.7) | copy-start | bytes 786436
  3.7 17.9 %copy-start.2 = (bf16[128,4,128]{2,0,1:T(8,128)(2,1)}, bf16[128,4,128]{2,0,1:T(8,128)(2,1)S(1)}, u32[]{:S(2)}) copy-start(bf16[128,4,128]{2,0,1:T(8,128)(2,1)S(1)} %copy.85) | copy-start | bytes 393220
  4.0 18.2 %copy-start.4 = (f32[128,64]{1,0:T(8,128)}, f32[128,64]{1,0:T(8,128)S(1)}, u32[]{:S(2)}) copy-start(f32[128,64]{1,0:T(8,128)S(1)} %get-tuple-element.62) | copy-start | bytes 98308
  4.0 18.2 %copy-start.6 = (f32[128,64]{1,0:T(8,128)}, f32[128,64]{1,0:T(8,128)S(1)}, u32[]{:S(2)}) copy-start(f32[128,64]{1,0:T(8,128)S(1)} %get-tuple-element.63) | copy-start | bytes 98308
  4.9 52.2 %copy-start = (f32[128,4,128]{2,0,1:T(8,128)}, f32[128,4,128]{2,0,1:T(8,128)S(1)}, u32[]{:S(2)}) copy-start(f32[128,4,128]{2,0,1:T(8,128)S(1)} %get-tuple-element.35) | copy-start | bytes 786436
  5.1 16.9 %copy-start.18 = (bf16[128,4,64]{2,0,1:T(8,128)(2,1)}, bf16[128,4,64]{2,0,1:T(8,128)(2,1)S(1)}, u32[]{:S(2)}) copy-start(bf16[128,4,64]{2,0,1:T(8,128)(2,1)S(1)} %get-tuple-element.52) | copy-start | bytes 196612
  5.1 16.9 %copy-start.20 = (bf16[128,4,64]{2,0,1:T(8,128)(2,1)}, bf16[128,4,64]{2,0,1:T(8,128)(2,1)S(1)}, u32[]{:S(2)}) copy-start(bf16[128,4,64]{2,0,1:T(8,128)(2,1)S(1)} %get-tuple-element.53) | copy-start | bytes 196612
  5.1 16.9 %copy-start.27 = (f32[128]{0:T(128)S(1)}, f32[128]{0:T(128)}, u32[]{:S(2)}) copy-start(f32[128]{0:T(128)} %param.12) | copy-start | bytes 1540
  5.2 21.8 %collective-permute-start.1 = (bf16[129,8,128]{2,0,1:T(8,128)(2,1)S(1)}, bf16[129,8,128]{2,0,1:T(8,128)(2,1)}, u32[]{:S(2)}, u32[]{:S(2)}) collective-permute-start(bf16[129,8,128]{2,0,1:T(8,128)(2,1)S(1)} %pad_maximum_fusion.1), channel_id=1, source_target_pairs={{0,4},{4,8},{8,12},{12,16},{16,20},{20,24},{24,28},{28,32},{32,36}... | collective-permute-start | bytes 792584 | tf_op jit(solution)/shard_map/ppermute | solution.py:19
  10.6 17.1 %collective-permute-start = (bf16[129,8,128]{2,0,1:T(8,128)(2,1)S(1)}, bf16[129,8,128]{2,0,1:T(8,128)(2,1)}, u32[]{:S(2)}, u32[]{:S(2)}) collective-permute-start(bf16[129,8,128]{2,0,1:T(8,128)(2,1)S(1)} %pad_maximum_fusion.1), channel_id=1, source_target_pairs={{0,8},{4,12},{8,16},{12,20},{16,24},{20,28},{24,32},{28,36},{32,40... | collective-permute-start | bytes 792584 | tf_op jit(solution)/shard_map/ppermute | solution.py:19
  15.3 41.7 %collective-permute-start.7 = (f32[128,4,128]{2,0,1:T(8,128)S(1)}, f32[128,4,128]{2,0,1:T(8,128)}, u32[]{:S(2)}, u32[]{:S(2)}) collective-permute-start(f32[128,4,128]{2,0,1:T(8,128)S(1)} %get-tuple-element.35), channel_id=1, source_target_pairs={{0,4},{4,8},{8,12},{12,16},{16,20},{20,24},{24,28},{28,32},{32,36}... | collective-permute-start | bytes 786440 | tf_op jit(solution)/shard_map/ppermute | solution.py:19
  17.2 39.8 %collective-permute-start.6 = (f32[128,4,128]{2,0,1:T(8,128)S(1)}, f32[128,4,128]{2,0,1:T(8,128)}, u32[]{:S(2)}, u32[]{:S(2)}) collective-permute-start(f32[128,4,128]{2,0,1:T(8,128)S(1)} %get-tuple-element.35), channel_id=1, source_target_pairs={{0,8},{4,12},{8,16},{12,20},{16,24},{20,28},{24,32},{28,36},{32,40... | collective-permute-start | bytes 786440 | tf_op jit(solution)/shard_map/ppermute | solution.py:19
  22.0 4.0 %copy-start.11 = (f32[128,8]{1,0:T(8,128)}, f32[128,8]{1,0:T(8,128)S(1)}, u32[]{:S(2)}) copy-start(f32[128,8]{1,0:T(8,128)S(1)} %add_rsqrt_fusion) | copy-start | bytes 12292
  22.2 3.3 %copy-start.22 = (bf16[1,128,1024]{2,1,0:T(8,128)(2,1)S(1)}, bf16[1,128,1024]{2,1,0:T(8,128)(2,1)}, u32[]{:S(2)}) copy-start(bf16[1,128,1024]{2,1,0:T(8,128)(2,1)} %param.10) | copy-start | bytes 786436
  24.8 3.6 %copy-start.29 = (s32[1,128]{1,0:T(1,128)S(1)}, s32[1,128]{1,0:T(1,128)}, u32[]{:S(2)}) copy-start(s32[1,128]{1,0:T(1,128)} %param.11) | copy-start | bytes 1540
  29.6 1.1 copy-start.23
  29.6 3.1 %copy-start.8 = (bf16[128,4,128]{2,0,1:T(8,128)(2,1)}, bf16[128,4,128]{2,0,1:T(8,128)(2,1)S(1)}, u32[]{:S(2)}) copy-start(bf16[128,4,128]{2,0,1:T(8,128)(2,1)S(1)} %get-tuple-element.57) | copy-start | bytes 393220
  30.7 1.8 %copy-start.25 = (bf16[128,4,128]{2,0,1:T(8,128)(2,1)}, bf16[128,4,128]{2,0,1:T(8,128)(2,1)S(1)}, u32[]{:S(2)}) copy-start(bf16[128,4,128]{2,0,1:T(8,128)(2,1)S(1)} %get-tuple-element.54) | copy-start | bytes 393220
  30.7 2.0 %copy-start.9 = (bf16[128,4,128]{2,0,1:T(8,128)(2,1)}, bf16[128,4,128]{2,0,1:T(8,128)(2,1)S(1)}, u32[]{:S(2)}) copy-start(bf16[128,4,128]{2,0,1:T(8,128)(2,1)S(1)} %get-tuple-element.55) | copy-start | bytes 393220
  32.5 0.9 copy-start.3
  38.7 1.6 %copy-start.19 = (bf16[128,4,64]{2,0,1:T(8,128)(2,1)S(1)}, bf16[128,4,64]{2,0,1:T(8,128)(2,1)}, u32[]{:S(2)}) copy-start(bf16[128,4,64]{2,0,1:T(8,128)(2,1)} %copy-done.18) | copy-start | bytes 196612
  38.7 1.6 %copy-start.21 = (bf16[128,4,64]{2,0,1:T(8,128)(2,1)S(1)}, bf16[128,4,64]{2,0,1:T(8,128)(2,1)}, u32[]{:S(2)}) copy-start(bf16[128,4,64]{2,0,1:T(8,128)(2,1)} %copy-done.20) | copy-start | bytes 196612
  38.7 1.6 %copy-start.24 = (bf16[128,4,128]{2,0,1:T(8,128)(2,1)S(1)}, bf16[128,4,128]{2,0,1:T(8,128)(2,1)}, u32[]{:S(2)}) copy-start(bf16[128,4,128]{2,0,1:T(8,128)(2,1)} %copy-done.23) | copy-start | bytes 393220
  38.7 1.6 %copy-start.26 = (bf16[128,4,128]{2,0,1:T(8,128)(2,1)S(1)}, bf16[128,4,128]{2,0,1:T(8,128)(2,1)}, u32[]{:S(2)}) copy-start(bf16[128,4,128]{2,0,1:T(8,128)(2,1)} %copy-done.25) | copy-start | bytes 393220
  40.3 1.0 copy-start.13
  40.3 1.0 copy-start.14
  47.3 1.4 copy-start.12
  54.3 2.4 %copy-start.16 = (f32[384,64]{1,0:T(8,128)S(1)}, f32[384,64]{1,0:T(8,128)}, u32[]{:S(2)}) copy-start(f32[384,64]{1,0:T(8,128)} %get-tuple-element.58) | copy-start | bytes 294916
  54.3 2.4 %copy-start.17 = (f32[384,64]{1,0:T(8,128)S(1)}, f32[384,64]{1,0:T(8,128)}, u32[]{:S(2)}) copy-start(f32[384,64]{1,0:T(8,128)} %get-tuple-element.59) | copy-start | bytes 294916
  57.0 49.9 %copy-start.28 = (f32[128]{0:T(128)S(1)}, f32[128]{0:T(128)}, u32[]{:S(2)}) copy-start(f32[128]{0:T(128)} %param.13) | copy-start | bytes 1540
  57.0 59.2 %copy-start.10 = (bf16[384,4,128]{2,0,1:T(8,128)(2,1)S(1)}, bf16[384,4,128]{2,0,1:T(8,128)(2,1)}, u32[]{:S(2)}) copy-start(bf16[384,4,128]{2,0,1:T(8,128)(2,1)} %get-tuple-element.68) | copy-start | bytes 1179652
  58.5 4.3 %collective-permute-start.8 = (f32[256]{0:T(256)S(1)}, f32[256]{0:T(256)S(1)}, u32[]{:S(2)}, u32[]{:S(2)}) collective-permute-start(f32[256]{0:T(256)S(1)} %pad_maximum_fusion.6), channel_id=1, source_target_pairs={{0,1},{1,0},{2,3},{3,2},{4,5},{5,4},{6,7},{7,6},{8,9},{9,8},{10,11... | collective-permute-start | bytes 3080 | tf_op jit(solution)/shard_map/ppermute | solution.py:27
  62.8 5.2 %collective-permute-start.9 = (f32[256]{0:T(256)S(1)}, f32[256]{0:T(256)S(1)}, u32[]{:S(2)}, u32[]{:S(2)}) collective-permute-start(f32[256]{0:T(256)S(1)} %fusion.27), channel_id=1, source_target_pairs={{0,2},{1,3},{2,0},{3,1},{4,6},{5,7},{6,4},{7,5},{8,10},{9,11},{10,... | collective-permute-start | bytes 3080 | tf_op jit(solution)/shard_map/ppermute | solution.py:27
  68.0 10.8 %collective-permute-start.10 = (f32[256]{0:T(256)S(1)}, f32[256]{0:T(256)S(1)}, u32[]{:S(2)}, u32[]{:S(2)}) collective-permute-start(f32[256]{0:T(256)S(1)} %add.137), channel_id=1, source_target_pairs={{0,4},{4,0},{8,12},{12,8},{16,20},{20,16},{24,28},{28,24},{32,36},... | collective-permute-start | bytes 3080 | tf_op jit(solution)/shard_map/ppermute | solution.py:27
  78.8 4.3 %collective-permute-start.11 = (f32[256]{0:T(256)S(1)}, f32[256]{0:T(256)S(1)}, u32[]{:S(2)}, u32[]{:S(2)}) collective-permute-start(f32[256]{0:T(256)S(1)} %add.138), channel_id=1, source_target_pairs={{0,8},{4,12},{8,0},{12,4},{16,24},{20,28},{24,16},{28,20},{32,40},... | collective-permute-start | bytes 3080 | tf_op jit(solution)/shard_map/ppermute | solution.py:27
  83.1 5.2 %collective-permute-start.12 = (f32[256]{0:T(256)S(1)}, f32[256]{0:T(256)S(1)}, u32[]{:S(2)}, u32[]{:S(2)}) collective-permute-start(f32[256]{0:T(256)S(1)} %add.139), channel_id=1, source_target_pairs={{0,16},{4,20},{8,24},{12,28},{16,0},{20,4},{24,8},{28,12},{32,48},... | collective-permute-start | bytes 3080 | tf_op jit(solution)/shard_map/ppermute | solution.py:27
  88.3 8.2 %collective-permute-start.13 = (f32[256]{0:T(256)S(1)}, f32[256]{0:T(256)S(1)}, u32[]{:S(2)}, u32[]{:S(2)}) collective-permute-start(f32[256]{0:T(256)S(1)} %add.140), channel_id=1, source_target_pairs={{0,32},{4,36},{8,40},{12,44},{16,48},{20,52},{24,56},{28,60},{32,0... | collective-permute-start | bytes 3080 | tf_op jit(solution)/shard_map/ppermute | solution.py:27
  96.6 13.0 %collective-permute-start.14 = (f32[256]{0:T(256)S(1)}, f32[256]{0:T(256)S(1)}, u32[]{:S(2)}, u32[]{:S(2)}) collective-permute-start(f32[256]{0:T(256)S(1)} %add.141), channel_id=1, source_target_pairs={{0,64},{4,68},{8,72},{12,76},{16,80},{20,84},{24,88},{28,92},{32,9... | collective-permute-start | bytes 3080 | tf_op jit(solution)/shard_map/ppermute | solution.py:27
  109.6 8.2 %collective-permute-start.15 = (f32[256]{0:T(256)S(1)}, f32[256]{0:T(256)S(1)}, u32[]{:S(2)}, u32[]{:S(2)}) collective-permute-start(f32[256]{0:T(256)S(1)} %add.142), channel_id=1, source_target_pairs={{0,128},{128,0},{256,384},{384,256},{512,640},{640,512},{768,896},... | collective-permute-start | bytes 3080 | tf_op jit(solution)/shard_map/ppermute | solution.py:27
  118.4 13.7 %collective-permute-start.16 = (f32[256]{0:T(256)}, f32[256]{0:T(256)}, u32[]{:S(2)}, u32[]{:S(2)}) collective-permute-start(f32[256]{0:T(256)} %add.143), channel_id=1, source_target_pairs={{0,256},{128,384},{256,0},{384,128},{512,768},{640,896},{768,512},... | collective-permute-start | bytes 3080 | tf_op jit(solution)/shard_map/ppermute | solution.py:27
  121.3 20.4 %copy-start.5 = (f32[128,64]{1,0:T(8,128)S(1)}, f32[128,64]{1,0:T(8,128)}, u32[]{:S(2)}) copy-start(f32[128,64]{1,0:T(8,128)} %copy-done.4) | copy-start | bytes 98308
  121.3 20.4 %copy-start.7 = (f32[128,64]{1,0:T(8,128)S(1)}, f32[128,64]{1,0:T(8,128)}, u32[]{:S(2)}) copy-start(f32[128,64]{1,0:T(8,128)} %copy-done.6) | copy-start | bytes 98308
  123.1 18.8 %copy-start.1 = (f32[128,4,128]{2,0,1:T(8,128)S(1)}, f32[128,4,128]{2,0,1:T(8,128)}, u32[]{:S(2)}) copy-start(f32[128,4,128]{2,0,1:T(8,128)} %copy-done) | copy-start | bytes 786436
  123.1 18.5 %collective-permute-start.3 = (bf16[128,4,128]{2,0,1:T(8,128)(2,1)}, bf16[128,4,128]{2,0,1:T(8,128)(2,1)S(1)}, u32[]{:S(2)}, u32[]{:S(2)}) collective-permute-start(bf16[128,4,128]{2,0,1:T(8,128)(2,1)} %get-tuple-element.51), channel_id=1, source_target_pairs={{8,0},{12,4},{16,8},{20,12},{24,16},{28,20},{32,24},{36,28},{40,32... | collective-permute-start | bytes 393224 | tf_op jit(solution)/shard_map/ppermute | solution.py:19
  124.6 17.1 %collective-permute-start.2 = (bf16[128,4,128]{2,0,1:T(8,128)(2,1)}, bf16[128,4,128]{2,0,1:T(8,128)(2,1)S(1)}, u32[]{:S(2)}, u32[]{:S(2)}) collective-permute-start(bf16[128,4,128]{2,0,1:T(8,128)(2,1)} %get-tuple-element.50), channel_id=1, source_target_pairs={{4,0},{8,4},{12,8},{16,12},{20,16},{24,20},{28,24},{32,28},{36,32}... | collective-permute-start | bytes 393224 | tf_op jit(solution)/shard_map/ppermute | solution.py:19
  132.8 8.3 %collective-permute-start.17 = (f32[256]{0:T(256)S(1)}, f32[256]{0:T(256)S(1)}, u32[]{:S(2)}, u32[]{:S(2)}) collective-permute-start(f32[256]{0:T(256)S(1)} %add.144), channel_id=1, source_target_pairs={{0,512},{128,640},{256,768},{384,896},{512,0},{640,128},{768,256},... | collective-permute-start | bytes 3080 | tf_op jit(solution)/shard_map/ppermute | solution.py:27
  137.9 10.8 %collective-permute-start.5 = (f32[128,4,128]{0,2,1:T(8,128)}, f32[128,4,128]{0,2,1:T(8,128)S(1)}, u32[]{:S(2)}, u32[]{:S(2)}) collective-permute-start(f32[128,4,128]{0,2,1:T(8,128)} %get-tuple-element.43), channel_id=1, source_target_pairs={{8,0},{12,4},{16,8},{20,12},{24,16},{28,20},{32,24},{36,28},{40,32... | collective-permute-start | bytes 786440 | tf_op jit(solution)/shard_map/ppermute | solution.py:19
  139.2 12.6 %collective-permute-start.4 = (f32[128,4,128]{0,2,1:T(8,128)S(1)}, f32[128,4,128]{0,2,1:T(8,128)S(1)}, u32[]{:S(2)}, u32[]{:S(2)}) collective-permute-start(f32[128,4,128]{0,2,1:T(8,128)S(1)} %get-tuple-element.42), channel_id=1, source_target_pairs={{4,0},{8,4},{12,8},{16,12},{20,16},{24,20},{28,24},{32,28},{36,32}... | collective-permute-start | bytes 786440 | tf_op jit(solution)/shard_map/ppermute | solution.py:19

commit v5 on v3

--- a/solution.py
+++ b/solution.py
@@ -150,7 +150,9 @@
         back_keys = passed_along(
             grad_keys[low_row : low_row + row_count].astype(jnp.bfloat16), "ctx", -offset
         ).astype(jnp.float32)
-        back_values = passed_along(grad_values[low_row : low_row + row_count], "ctx", -offset)
+        back_values = passed_along(
+            grad_values[low_row : low_row + row_count].astype(jnp.bfloat16), "ctx", -offset
+        ).astype(jnp.float32)
         key_own = key_own + back_keys
         value_grad = value_grad + back_values
     dq_grad, q_term = restore(

time: 136 us -> 129 us (0.949)
  the two profiles are of different devices: /device:TPU:18 before, /device:TPU:16 now
where the time goes in v5:
time: 129 us; the launch traced here: 128 us
  starting transfers between devices  75.5 us (59%)
  waiting for transfers between devices  22 us (17%)
  local copies, waits for them, and re-layouts  12.3 us (10%)
  other arithmetic  9.12 us (7%)
  matrix products  7.59 us (6%)
  between operations  1.56 us (1%)
    ppermute x10, starting transfers between devices, butterfly_sum(): value = value + lax.ppermute(value, axis, pairs)  64.1 us
    ppermute x10, waiting for transfers between devices, butterfly_sum(): value = value + lax.ppermute(value, axis, pairs)  14 us
    ppermute x6, starting transfers between devices, passed_along(): return lax.ppermute(value, axis, pairs)  11.4 us
    ppermute x6, waiting for transfers between devices, passed_along(): return lax.ppermute(value, axis, pairs)  8 us
    unnamed x71, local copies, waits for them, and re-layouts  7.61 us
  transfers between devices with their start and end apart: 16, of which 10 were waited for; matrix products, arithmetic and copies ran while one was open for 6% of the time, Pallas kernels for 0%

profile of v5, /device:TPU:16, one launch (start us, length us, event | category | flops | bytes accessed | tf_op | source)
XLA Modules:
  0.0 128.1 jit_solution(2341713489159245351)
XLA Ops:
  0.6 1.0 copy.82
  1.9 0.7 bitcast_convert_fusion.1
  2.6 1.0 copy.84
  3.7 0.3 multiply_cosine_fusion
  4.1 0.8 multiply_multiply_fusion.1
  5.2 1.8 %collective-permute-start.1 = (bf16[129,8,128]{2,0,1:T(8,128)(2,1)S(1)}, bf16[129,8,128]{2,0,1:T(8,128)(2,1)S(1)}, u32[]{:S(2)}, u32[]{:S(2)}) collective-permute-start(bf16[129,8,128]{2,0,1:T(8,128)(2,1)S(1)} %pad_maximum_fusion.1), channel_id=1, source_target_pairs={{0,4},{4,8},{8,12},{12,16},{16,20},{20,24},{24,28},{28,32},{32,36}... | collective-permute-start | bytes 792584 | tf_op jit(solution)/shard_map/ppermute | solution.py:19
  7.0 4.5 %collective-permute-start = (bf16[129,8,128]{2,0,1:T(8,128)(2,1)S(1)}, bf16[129,8,128]{2,0,1:T(8,128)(2,1)S(1)}, u32[]{:S(2)}, u32[]{:S(2)}) collective-permute-start(bf16[129,8,128]{2,0,1:T(8,128)(2,1)S(1)} %pad_maximum_fusion.1), channel_id=1, source_target_pairs={{0,8},{4,12},{8,16},{12,20},{16,24},{20,28},{24,32},{28,36},{32,40... | collective-permute-start | bytes 792584 | tf_op jit(solution)/shard_map/ppermute | solution.py:19
  11.6 0.2 multiply_reduce_fusion.3
  11.9 0.2 multiply_multiply_fusion
  12.1 0.3 subtract_convert_fusion
  12.5 0.8 copy.87
  13.5 0.2 copy.102
  13.7 0.2 mul.377
  13.9 0.9 mul.390
  14.8 3.1 %collective-permute-done = bf16[129,8,128]{2,0,1:T(8,128)(2,1)S(1)} collective-permute-done((bf16[129,8,128]{2,0,1:T(8,128)(2,1)S(1)}, bf16[129,8,128]{2,0,1:T(8,128)(2,1)S(1)}, u32[]{:S(2)}, u32[]{:S(2)}) %collective-permute-start) | collective-permute-done | bytes 264224 | tf_op jit(solution)/shard_map/ppermute | solution.py:19
  17.9 0.2 fusion.15
  18.3 1.6 %fusion.31 = (f32[4,2,128]{2,1,0:T(2,128)S(1)}, f32[4,2,128,384]{2,3,1,0:T(8,128)S(1)}) fusion(bf16[128,4,2,64]{3,0,2,1:T(8,128)(2,1)S(1)} %bitcast.118, bf16[128,4,2,64]{3,0,2,1:T(8,128)(2,1)} %bitcast.120, bf16[128,4,64]{2,0,1:T(8,128)(2,1)} %copy-done.19, bf16[128,4,64]{2,0,1:T(8,128)(2,1)S(1)} %get-tuple-element.50, ...), kind=kOutput, calls=%fused_computation.91 | convolution fusion | flops 103939072 | bytes 2281472 | tf_op jit(solution)/shard_map/qhgd,khd->hgqk/dot_general | solution.py:83
  19.9 0.2 exponential_reduce_fusion
  20.2 1.3 %bitcast_convert_fusion = (f32[4,2,128,128]{2,3,1,0:T(8,128)}, bf16[4,128,2,128]{3,1,2,0:T(8,128)(2,1)}) fusion(f32[4,2,128,384]{2,3,1,0:T(8,128)S(1)} %get-tuple-element.61, f32[4,2,128]{2,1,0:T(2,128)S(1)} %bitcast.126, bf16[128,4,128]{2,0,1:T(8,128)(2,1)S(1)} %copy.85, bf16[128,4,128]{2,0,1:T(8,128)(2,1)S(1)} %get-tuple-element.55, ...), kind=kOutput, calls=%fused_computation.44 | convolution fusion | flops 102891520 | bytes 2756608 | tf_op jit(solution)/shard_map/hgqk,khd->qhgd/dot_general | solution.py:129
  21.5 1.4 %copy.115 = f32[4,2,128,128]{3,1,0,2:T(2,128)S(1)} copy(f32[4,2,128,128]{2,3,1,0:T(8,128)} %get-tuple-element.62) | data formatting | bytes 1048576
  22.8 1.5 %multiply_reduce_fusion = f32[4,2,128]{1,0,2:T(4,128)} fusion(f32[4,2,128,128]{3,1,0,2:T(2,128)S(1)} %copy.115, bf16[128,4,2,128]{3,2,1,0:T(2,128)(2,1)S(1)} %reshape_squeeze.7), kind=kLoop, calls=%fused_computation.16 | loop fusion | flops 392192 | bytes 790528
  24.4 1.0 copy.116
  25.4 1.5 %fusion.1 = bf16[4,2,128,384]{2,3,1,0:T(8,128)(2,1)S(1)} fusion(bf16[128,4,2,128]{0,3,2,1:T(8,128)(2,1)S(1)} %copy.102, f32[4,2,128,384]{2,3,1,0:T(8,128)S(1)} %get-tuple-element.61, f32[4,2,128]{2,1,0:T(2,128)S(1)} %copy.116, f32[4,2,128]{2,1,0:T(2,128)S(1)} %bitcast.127, bf16[128,4,128]{2,0,1:T(8,128)(2,1)} %copy-done.1, ...), kind=kOutput, calls=%fused_computation.2 | convolution fusion | flops 103415808 | bytes 3022848 | tf_op jit(solution)/shard_map/qhgd,khd->hgqk/dot_general | solution.py:135
  27.0 0.4 convolution_multiply_fusion
  27.4 0.5 copy-done.12
  28.0 1.4 %fusion.32 = (bf16[384,4,128]{2,0,1:T(8,128)(2,1)S(1)}, f32[384,4,128]{2,0,1:T(8,128)}) fusion(bf16[4,2,128,384]{2,3,1,0:T(8,128)(2,1)S(1)} %fusion.1, bf16[128,4,2,64]{3,0,2,1:T(8,128)(2,1)S(1)} %bitcast.119, bf16[128,4,2,64]{3,0,2,1:T(8,128)(2,1)S(1)} %bitcast.121), kind=kOutput, calls=%fused_computation.92 | convolution fusion | flops 101580800 | bytes 2228224 | tf_op jit(solution)/shard_map/hgqk,qhgd->khd/dot_general | solution.py:140
  29.4 1.4 %fusion.33 = (bf16[384,4,128]{0,2,1:T(8,128)(2,1)}, f32[384,4,128]{0,2,1:T(8,128)}) fusion(bf16[128,4,2,128]{0,3,2,1:T(8,128)(2,1)S(1)} %copy.102, f32[4,2,128,384]{2,3,1,0:T(8,128)S(1)} %get-tuple-element.61, f32[4,2,128]{2,1,0:T(2,128)S(1)} %bitcast.128), kind=kOutput, calls=%fused_computation.93 | convolution fusion | flops 101646336 | bytes 3018752 | tf_op jit(solution)/shard_map/hgqk,qhgd->khd/dot_general | solution.py:143
  30.9 0.2 copy.130
  31.1 0.2 copy.129
  31.4 0.3 copy-done.3
  32.0 0.5 multiply_reduce_fusion.2
  32.6 0.2 mul.406
  32.9 1.3 %collective-permute-start.3 = (bf16[128,4,128]{2,0,1:T(8,128)(2,1)S(1)}, bf16[128,4,128]{2,0,1:T(8,128)(2,1)S(1)}, u32[]{:S(2)}, u32[]{:S(2)}) collective-permute-start(bf16[128,4,128]{2,0,1:T(8,128)(2,1)S(1)} %get-tuple-element.49), channel_id=1, source_target_pairs={{8,0},{12,4},{16,8},{20,12},{24,16},{28,20},{32,24},{36,28},{40,32... | collective-permute-start | bytes 393224 | tf_op jit(solution)/shard_map/ppermute | solution.py:19
  34.2 1.3 %collective-permute-start.2 = (bf16[128,4,128]{2,0,1:T(8,128)(2,1)S(1)}, bf16[128,4,128]{2,0,1:T(8,128)(2,1)S(1)}, u32[]{:S(2)}, u32[]{:S(2)}) collective-permute-start(bf16[128,4,128]{2,0,1:T(8,128)(2,1)S(1)} %get-tuple-element.48), channel_id=1, source_target_pairs={{4,0},{8,4},{12,8},{16,12},{20,16},{24,20},{28,24},{32,28},{36,32}... | collective-permute-start | bytes 393224 | tf_op jit(solution)/shard_map/ppermute | solution.py:19
  35.5 0.9 multiply_reduce_fusion.1
  36.5 4.8 %collective-permute-done.3 = bf16[128,4,128]{2,0,1:T(8,128)(2,1)S(1)} collective-permute-done((bf16[128,4,128]{2,0,1:T(8,128)(2,1)S(1)}, bf16[128,4,128]{2,0,1:T(8,128)(2,1)S(1)}, u32[]{:S(2)}, u32[]{:S(2)}) %collective-permute-start.3) | collective-permute-done | bytes 131104 | tf_op jit(solution)/shard_map/ppermute | solution.py:19
  41.3 1.0 fusion.8
  42.5 0.3 multiply_reduce_fusion.4
  43.0 0.2 fusion.10
  43.2 3.5 %collective-permute-start.6 = (f32[256]{0:T(256)S(1)}, f32[256]{0:T(256)S(1)}, u32[]{:S(2)}, u32[]{:S(2)}) collective-permute-start(f32[256]{0:T(256)S(1)} %pad_maximum_fusion.6), channel_id=1, source_target_pairs={{0,1},{1,0},{2,3},{3,2},{4,5},{5,4},{6,7},{7,6},{8,9},{9,8},{10,11... | collective-permute-start | bytes 3080 | tf_op jit(solution)/shard_map/ppermute | solution.py:27
  46.8 1.3 %collective-permute-start.5 = (bf16[128,4,128]{0,2,1:T(8,128)(2,1)S(1)}, bf16[128,4,128]{0,2,1:T(8,128)(2,1)S(1)}, u32[]{:S(2)}, u32[]{:S(2)}) collective-permute-start(bf16[128,4,128]{0,2,1:T(8,128)(2,1)S(1)} %get-tuple-element.45), channel_id=1, source_target_pairs={{8,0},{12,4},{16,8},{20,12},{24,16},{28,20},{32,24},{36,28},{40,32... | collective-permute-start | bytes 393224 | tf_op jit(solution)/shard_map/ppermute | solution.py:19
  48.1 1.3 %collective-permute-start.4 = (bf16[128,4,128]{0,2,1:T(8,128)(2,1)S(1)}, bf16[128,4,128]{0,2,1:T(8,128)(2,1)S(1)}, u32[]{:S(2)}, u32[]{:S(2)}) collective-permute-start(bf16[128,4,128]{0,2,1:T(8,128)(2,1)S(1)} %get-tuple-element.44), channel_id=1, source_target_pairs={{4,0},{8,4},{12,8},{16,12},{20,16},{24,20},{28,24},{32,28},{36,32}... | collective-permute-start | bytes 393224 | tf_op jit(solution)/shard_map/ppermute | solution.py:19
  49.4 7.1 %collective-permute-start.7 = (f32[256]{0:T(256)S(1)}, f32[256]{0:T(256)S(1)}, u32[]{:S(2)}, u32[]{:S(2)}) collective-permute-start(f32[256]{0:T(256)S(1)} %fusion.24), channel_id=1, source_target_pairs={{0,2},{1,3},{2,0},{3,1},{4,6},{5,7},{6,4},{7,5},{8,10},{9,11},{10,... | collective-permute-start | bytes 3080 | tf_op jit(solution)/shard_map/ppermute | solution.py:27
  56.5 1.5 %collective-permute-done.7 = f32[256]{0:T(256)S(1)} collective-permute-done((f32[256]{0:T(256)S(1)}, f32[256]{0:T(256)S(1)}, u32[]{:S(2)}, u32[]{:S(2)}) %collective-permute-start.7) | collective-permute-done | bytes 1056 | tf_op jit(solution)/shard_map/ppermute | solution.py:27
  58.0 2.6 %collective-permute-start.8 = (f32[256]{0:T(256)S(1)}, f32[256]{0:T(256)S(1)}, u32[]{:S(2)}, u32[]{:S(2)}) collective-permute-start(f32[256]{0:T(256)S(1)} %add.129), channel_id=1, source_target_pairs={{0,4},{4,0},{8,12},{12,8},{16,20},{20,16},{24,28},{28,24},{32,36},... | collective-permute-start | bytes 3080 | tf_op jit(solution)/shard_map/ppermute | solution.py:27
  60.6 0.8 collective-permute-done.8
  61.4 4.7 %collective-permute-start.9 = (f32[256]{0:T(256)S(1)}, f32[256]{0:T(256)S(1)}, u32[]{:S(2)}, u32[]{:S(2)}) collective-permute-start(f32[256]{0:T(256)S(1)} %add.130), channel_id=1, source_target_pairs={{0,8},{4,12},{8,0},{12,4},{16,24},{20,28},{24,16},{28,20},{32,40},... | collective-permute-start | bytes 3080 | tf_op jit(solution)/shard_map/ppermute | solution.py:27
  66.1 1.5 %collective-permute-done.9 = f32[256]{0:T(256)S(1)} collective-permute-done((f32[256]{0:T(256)S(1)}, f32[256]{0:T(256)S(1)}, u32[]{:S(2)}, u32[]{:S(2)}) %collective-permute-start.9) | collective-permute-done | bytes 1056 | tf_op jit(solution)/shard_map/ppermute | solution.py:27
  67.7 6.9 %collective-permute-start.10 = (f32[256]{0:T(256)S(1)}, f32[256]{0:T(256)S(1)}, u32[]{:S(2)}, u32[]{:S(2)}) collective-permute-start(f32[256]{0:T(256)S(1)} %add.131), channel_id=1, source_target_pairs={{0,16},{4,20},{8,24},{12,28},{16,0},{20,4},{24,8},{28,12},{32,48},... | collective-permute-start | bytes 3080 | tf_op jit(solution)/shard_map/ppermute | solution.py:27
  74.6 1.5 %collective-permute-done.10 = f32[256]{0:T(256)S(1)} collective-permute-done((f32[256]{0:T(256)S(1)}, f32[256]{0:T(256)S(1)}, u32[]{:S(2)}, u32[]{:S(2)}) %collective-permute-start.10) | collective-permute-done | bytes 1056 | tf_op jit(solution)/shard_map/ppermute | solution.py:27
  76.1 11.2 %collective-permute-start.11 = (f32[256]{0:T(256)S(1)}, f32[256]{0:T(256)S(1)}, u32[]{:S(2)}, u32[]{:S(2)}) collective-permute-start(f32[256]{0:T(256)S(1)} %add.132), channel_id=1, source_target_pairs={{0,32},{4,36},{8,40},{12,44},{16,48},{20,52},{24,56},{28,60},{32,0... | collective-permute-start | bytes 3080 | tf_op jit(solution)/shard_map/ppermute | solution.py:27
  87.4 1.5 %collective-permute-done.11 = f32[256]{0:T(256)S(1)} collective-permute-done((f32[256]{0:T(256)S(1)}, f32[256]{0:T(256)S(1)}, u32[]{:S(2)}, u32[]{:S(2)}) %collective-permute-start.11) | collective-permute-done | bytes 1056 | tf_op jit(solution)/shard_map/ppermute | solution.py:27
  88.9 14.8 %collective-permute-start.12 = (f32[256]{0:T(256)S(1)}, f32[256]{0:T(256)S(1)}, u32[]{:S(2)}, u32[]{:S(2)}) collective-permute-start(f32[256]{0:T(256)S(1)} %add.133), channel_id=1, source_target_pairs={{0,64},{4,68},{8,72},{12,76},{16,80},{20,84},{24,88},{28,92},{32,9... | collective-permute-start | bytes 3080 | tf_op jit(solution)/shard_map/ppermute | solution.py:27
  103.7 1.5 %collective-permute-done.12 = f32[256]{0:T(256)S(1)} collective-permute-done((f32[256]{0:T(256)S(1)}, f32[256]{0:T(256)S(1)}, u32[]{:S(2)}, u32[]{:S(2)}) %collective-permute-start.12) | collective-permute-done | bytes 1056 | tf_op jit(solution)/shard_map/ppermute | solution.py:27
  105.3 5.0 %collective-permute-start.13 = (f32[256]{0:T(256)S(1)}, f32[256]{0:T(256)S(1)}, u32[]{:S(2)}, u32[]{:S(2)}) collective-permute-start(f32[256]{0:T(256)S(1)} %add.134), channel_id=1, source_target_pairs={{0,128},{128,0},{256,384},{384,256},{512,640},{640,512},{768,896},... | collective-permute-start | bytes 3080 | tf_op jit(solution)/shard_map/ppermute | solution.py:27
  110.3 4.3 %collective-permute-done.13 = f32[256]{0:T(256)S(1)} collective-permute-done((f32[256]{0:T(256)S(1)}, f32[256]{0:T(256)S(1)}, u32[]{:S(2)}, u32[]{:S(2)}) %collective-permute-start.13) | collective-permute-done | bytes 1056 | tf_op jit(solution)/shard_map/ppermute | solution.py:27
  114.6 3.4 %collective-permute-start.14 = (f32[256]{0:T(256)S(1)}, f32[256]{0:T(256)S(1)}, u32[]{:S(2)}, u32[]{:S(2)}) collective-permute-start(f32[256]{0:T(256)S(1)} %add.135), channel_id=1, source_target_pairs={{0,256},{128,384},{256,0},{384,128},{512,768},{640,896},{768,512},... | collective-permute-start | bytes 3080 | tf_op jit(solution)/shard_map/ppermute | solution.py:27
  118.0 0.9 copy.103
  118.9 1.2 collective-permute-done.14
  120.1 4.9 %collective-permute-start.15 = (f32[256]{0:T(256)S(1)}, f32[256]{0:T(256)S(1)}, u32[]{:S(2)}, u32[]{:S(2)}) collective-permute-start(f32[256]{0:T(256)S(1)} %add.136), channel_id=1, source_target_pairs={{0,512},{128,640},{256,768},{384,896},{512,0},{640,128},{768,256},... | collective-permute-start | bytes 3080 | tf_op jit(solution)/shard_map/ppermute | solution.py:27
  125.0 1.0 fusion.7
  126.1 0.8 copy.104
  126.8 0.8 copy.105
  127.6 0.5 fusion.30
  (114 shorter events, 2.2 us)
Async XLA Ops:
  1.7 9.8 %copy-start.28 = (f32[128]{0:T(128)S(1)}, f32[128]{0:T(128)}, u32[]{:S(2)}) copy-start(f32[128]{0:T(128)} %param.13) | copy-start | bytes 1540
  1.7 9.8 %copy-start.14 = (bf16[1,128,1024]{2,1,0:T(8,128)(2,1)S(1)}, bf16[1,128,1024]{2,1,0:T(8,128)(2,1)}, u32[]{:S(2)}) copy-start(bf16[1,128,1024]{2,1,0:T(8,128)(2,1)} %param.7) | copy-start | bytes 786436
  3.7 16.4 %copy-start.1 = (bf16[128,4,128]{2,0,1:T(8,128)(2,1)}, bf16[128,4,128]{2,0,1:T(8,128)(2,1)S(1)}, u32[]{:S(2)}) copy-start(bf16[128,4,128]{2,0,1:T(8,128)(2,1)S(1)} %copy.85) | copy-start | bytes 393220
  4.0 8.1 %copy-start.2 = (f32[128,64]{1,0:T(8,128)}, f32[128,64]{1,0:T(8,128)S(1)}, u32[]{:S(2)}) copy-start(f32[128,64]{1,0:T(8,128)S(1)} %get-tuple-element.58) | copy-start | bytes 98308
  4.1 8.1 %copy-start.4 = (f32[128,64]{1,0:T(8,128)}, f32[128,64]{1,0:T(8,128)S(1)}, u32[]{:S(2)}) copy-start(f32[128,64]{1,0:T(8,128)S(1)} %get-tuple-element.59) | copy-start | bytes 98308
  5.0 6.4 %copy-start.19 = (bf16[128,4,64]{2,0,1:T(8,128)(2,1)}, bf16[128,4,64]{2,0,1:T(8,128)(2,1)S(1)}, u32[]{:S(2)}) copy-start(bf16[128,4,64]{2,0,1:T(8,128)(2,1)S(1)} %get-tuple-element.51) | copy-start | bytes 196612
  5.0 13.2 %copy-start.17 = (bf16[128,4,64]{2,0,1:T(8,128)(2,1)}, bf16[128,4,64]{2,0,1:T(8,128)(2,1)S(1)}, u32[]{:S(2)}) copy-start(bf16[128,4,64]{2,0,1:T(8,128)(2,1)S(1)} %get-tuple-element.50) | copy-start | bytes 196612
  5.1 6.8 %copy-start.26 = (f32[128]{0:T(128)S(1)}, f32[128]{0:T(128)}, u32[]{:S(2)}) copy-start(f32[128]{0:T(128)} %param.12) | copy-start | bytes 1540
  5.2 9.6 %collective-permute-start.1 = (bf16[129,8,128]{2,0,1:T(8,128)(2,1)S(1)}, bf16[129,8,128]{2,0,1:T(8,128)(2,1)S(1)}, u32[]{:S(2)}, u32[]{:S(2)}) collective-permute-start(bf16[129,8,128]{2,0,1:T(8,128)(2,1)S(1)} %pad_maximum_fusion.1), channel_id=1, source_target_pairs={{0,4},{4,8},{8,12},{12,16},{16,20},{20,24},{24,28},{28,32},{32,36}... | collective-permute-start | bytes 792584 | tf_op jit(solution)/shard_map/ppermute | solution.py:19
  7.0 10.9 %collective-permute-start = (bf16[129,8,128]{2,0,1:T(8,128)(2,1)S(1)}, bf16[129,8,128]{2,0,1:T(8,128)(2,1)S(1)}, u32[]{:S(2)}, u32[]{:S(2)}) collective-permute-start(bf16[129,8,128]{2,0,1:T(8,128)(2,1)S(1)} %pad_maximum_fusion.1), channel_id=1, source_target_pairs={{0,8},{4,12},{8,16},{12,20},{16,24},{20,28},{24,32},{28,36},{32,40... | collective-permute-start | bytes 792584 | tf_op jit(solution)/shard_map/ppermute | solution.py:19
  11.9 1.8 %copy-start.9 = (f32[128,8]{1,0:T(8,128)}, f32[128,8]{1,0:T(8,128)S(1)}, u32[]{:S(2)}) copy-start(f32[128,8]{1,0:T(8,128)S(1)} %add_rsqrt_fusion) | copy-start | bytes 12292
  12.1 1.2 copy-start.21
  12.5 5.8 %copy-start.11 = (bf16[128,8,64]{2,0,1:T(8,128)(2,1)}, bf16[128,8,64]{2,0,1:T(8,128)(2,1)S(1)}, u32[]{:S(2)}) copy-start(bf16[128,8,64]{2,0,1:T(8,128)(2,1)S(1)} %copy.88) | copy-start | bytes 393220
  12.5 5.4 %copy-start.30 = (s32[1,128]{1,0:T(1,128)S(1)}, s32[1,128]{1,0:T(1,128)}, u32[]{:S(2)}) copy-start(s32[1,128]{1,0:T(1,128)} %param.11) | copy-start | bytes 1540
  18.2 1.7 %copy-start.22 = (bf16[128,4,128]{2,0,1:T(8,128)(2,1)}, bf16[128,4,128]{2,0,1:T(8,128)(2,1)S(1)}, u32[]{:S(2)}) copy-start(bf16[128,4,128]{2,0,1:T(8,128)(2,1)S(1)} %get-tuple-element.54) | copy-start | bytes 393220
  18.2 3.3 %copy-start.6 = (bf16[128,4,128]{2,0,1:T(8,128)(2,1)}, bf16[128,4,128]{2,0,1:T(8,128)(2,1)S(1)}, u32[]{:S(2)}) copy-start(bf16[128,4,128]{2,0,1:T(8,128)(2,1)S(1)} %get-tuple-element.55) | copy-start | bytes 393220
  18.2 1.7 %copy-start.24 = (bf16[128,4,128]{2,0,1:T(8,128)(2,1)}, bf16[128,4,128]{2,0,1:T(8,128)(2,1)S(1)}, u32[]{:S(2)}) copy-start(bf16[128,4,128]{2,0,1:T(8,128)(2,1)S(1)} %get-tuple-element.52) | copy-start | bytes 393220
  18.2 3.2 %copy-start.7 = (bf16[128,4,128]{2,0,1:T(8,128)(2,1)}, bf16[128,4,128]{2,0,1:T(8,128)(2,1)S(1)}, u32[]{:S(2)}) copy-start(bf16[128,4,128]{2,0,1:T(8,128)(2,1)S(1)} %get-tuple-element.53) | copy-start | bytes 393220
  25.4 1.6 %copy-start.18 = (bf16[128,4,64]{2,0,1:T(8,128)(2,1)S(1)}, bf16[128,4,64]{2,0,1:T(8,128)(2,1)}, u32[]{:S(2)}) copy-start(bf16[128,4,64]{2,0,1:T(8,128)(2,1)} %copy-done.17) | copy-start | bytes 196612
  25.4 1.6 %copy-start.20 = (bf16[128,4,64]{2,0,1:T(8,128)(2,1)S(1)}, bf16[128,4,64]{2,0,1:T(8,128)(2,1)}, u32[]{:S(2)}) copy-start(bf16[128,4,64]{2,0,1:T(8,128)(2,1)} %copy-done.19) | copy-start | bytes 196612
  25.4 1.6 %copy-start.23 = (bf16[128,4,128]{2,0,1:T(8,128)(2,1)S(1)}, bf16[128,4,128]{2,0,1:T(8,128)(2,1)}, u32[]{:S(2)}) copy-start(bf16[128,4,128]{2,0,1:T(8,128)(2,1)} %copy-done.22) | copy-start | bytes 393220
  25.4 1.6 %copy-start.25 = (bf16[128,4,128]{2,0,1:T(8,128)(2,1)S(1)}, bf16[128,4,128]{2,0,1:T(8,128)(2,1)}, u32[]{:S(2)}) copy-start(bf16[128,4,128]{2,0,1:T(8,128)(2,1)} %copy-done.24) | copy-start | bytes 393220
  27.0 1.0 copy-start.12
  27.0 1.0 copy-start.13
  30.8 0.8 copy-start.3
  30.8 0.9 copy-start.5
  31.1 0.9 copy-start.10
  31.1 0.8 copy-start.27
  32.5 3.1 %copy-start = (f32[1,128,1024]{2,1,0:T(8,128)S(1)}, f32[1,128,1024]{2,1,0:T(8,128)}, u32[]{:S(2)}) copy-start(f32[1,128,1024]{2,1,0:T(8,128)} %mul.390) | copy-start | bytes 1572868
  32.5 3.1 %copy-start.15 = (bf16[1,128,1024]{2,1,0:T(8,128)(2,1)S(1)}, bf16[1,128,1024]{2,1,0:T(8,128)(2,1)}, u32[]{:S(2)}) copy-start(bf16[1,128,1024]{2,1,0:T(8,128)(2,1)} %param.7) | copy-start | bytes 786436
  32.9 8.4 %collective-permute-start.3 = (bf16[128,4,128]{2,0,1:T(8,128)(2,1)S(1)}, bf16[128,4,128]{2,0,1:T(8,128)(2,1)S(1)}, u32[]{:S(2)}, u32[]{:S(2)}) collective-permute-start(bf16[128,4,128]{2,0,1:T(8,128)(2,1)S(1)} %get-tuple-element.49), channel_id=1, source_target_pairs={{8,0},{12,4},{16,8},{20,12},{24,16},{28,20},{32,24},{36,28},{40,32... | collective-permute-start | bytes 393224 | tf_op jit(solution)/shard_map/ppermute | solution.py:19
  34.2 8.3 %copy-start.29 = (f32[128]{0:T(128)S(1)}, f32[128]{0:T(128)}, u32[]{:S(2)}) copy-start(f32[128]{0:T(128)} %param.13) | copy-start | bytes 1540
  34.2 7.1 %collective-permute-start.2 = (bf16[128,4,128]{2,0,1:T(8,128)(2,1)S(1)}, bf16[128,4,128]{2,0,1:T(8,128)(2,1)S(1)}, u32[]{:S(2)}, u32[]{:S(2)}) collective-permute-start(bf16[128,4,128]{2,0,1:T(8,128)(2,1)S(1)} %get-tuple-element.48), channel_id=1, source_target_pairs={{4,0},{8,4},{12,8},{16,12},{20,16},{24,20},{28,24},{32,28},{36,32}... | collective-permute-start | bytes 393224 | tf_op jit(solution)/shard_map/ppermute | solution.py:19
  42.3 4.4 %copy-start.8 = (bf16[384,4,128]{0,2,1:T(8,128)(2,1)S(1)}, bf16[384,4,128]{0,2,1:T(8,128)(2,1)}, u32[]{:S(2)}) copy-start(bf16[384,4,128]{0,2,1:T(8,128)(2,1)} %get-tuple-element.66) | copy-start | bytes 1179652
  42.5 75.6 %copy-start.16 = (bf16[4,128,2,128]{3,1,2,0:T(8,128)(2,1)S(1)}, bf16[4,128,2,128]{3,1,2,0:T(8,128)(2,1)}, u32[]{:S(2)}) copy-start(bf16[4,128,2,128]{3,1,2,0:T(8,128)(2,1)} %get-tuple-element.63) | copy-start | bytes 786436
  43.2 6.1 %collective-permute-start.6 = (f32[256]{0:T(256)S(1)}, f32[256]{0:T(256)S(1)}, u32[]{:S(2)}, u32[]{:S(2)}) collective-permute-start(f32[256]{0:T(256)S(1)} %pad_maximum_fusion.6), channel_id=1, source_target_pairs={{0,1},{1,0},{2,3},{3,2},{4,5},{5,4},{6,7},{7,6},{8,9},{9,8},{10,11... | collective-permute-start | bytes 3080 | tf_op jit(solution)/shard_map/ppermute | solution.py:27
  46.8 78.3 %collective-permute-start.5 = (bf16[128,4,128]{0,2,1:T(8,128)(2,1)S(1)}, bf16[128,4,128]{0,2,1:T(8,128)(2,1)S(1)}, u32[]{:S(2)}, u32[]{:S(2)}) collective-permute-start(bf16[128,4,128]{0,2,1:T(8,128)(2,1)S(1)} %get-tuple-element.45), channel_id=1, source_target_pairs={{8,0},{12,4},{16,8},{20,12},{24,16},{28,20},{32,24},{36,28},{40,32... | collective-permute-start | bytes 393224 | tf_op jit(solution)/shard_map/ppermute | solution.py:19
  48.1 77.0 %collective-permute-start.4 = (bf16[128,4,128]{0,2,1:T(8,128)(2,1)S(1)}, bf16[128,4,128]{0,2,1:T(8,128)(2,1)S(1)}, u32[]{:S(2)}, u32[]{:S(2)}) collective-permute-start(bf16[128,4,128]{0,2,1:T(8,128)(2,1)S(1)} %get-tuple-element.44), channel_id=1, source_target_pairs={{4,0},{8,4},{12,8},{16,12},{20,16},{24,20},{28,24},{32,28},{36,32}... | collective-permute-start | bytes 393224 | tf_op jit(solution)/shard_map/ppermute | solution.py:19
  49.4 8.6 %collective-permute-start.7 = (f32[256]{0:T(256)S(1)}, f32[256]{0:T(256)S(1)}, u32[]{:S(2)}, u32[]{:S(2)}) collective-permute-start(f32[256]{0:T(256)S(1)} %fusion.24), channel_id=1, source_target_pairs={{0,2},{1,3},{2,0},{3,1},{4,6},{5,7},{6,4},{7,5},{8,10},{9,11},{10,... | collective-permute-start | bytes 3080 | tf_op jit(solution)/shard_map/ppermute | solution.py:27
  58.0 3.4 %collective-permute-start.8 = (f32[256]{0:T(256)S(1)}, f32[256]{0:T(256)S(1)}, u32[]{:S(2)}, u32[]{:S(2)}) collective-permute-start(f32[256]{0:T(256)S(1)} %add.129), channel_id=1, source_target_pairs={{0,4},{4,0},{8,12},{12,8},{16,20},{20,16},{24,28},{28,24},{32,36},... | collective-permute-start | bytes 3080 | tf_op jit(solution)/shard_map/ppermute | solution.py:27
  61.4 6.3 %collective-permute-start.9 = (f32[256]{0:T(256)S(1)}, f32[256]{0:T(256)S(1)}, u32[]{:S(2)}, u32[]{:S(2)}) collective-permute-start(f32[256]{0:T(256)S(1)} %add.130), channel_id=1, source_target_pairs={{0,8},{4,12},{8,0},{12,4},{16,24},{20,28},{24,16},{28,20},{32,40},... | collective-permute-start | bytes 3080 | tf_op jit(solution)/shard_map/ppermute | solution.py:27
  67.7 8.5 %collective-permute-start.10 = (f32[256]{0:T(256)S(1)}, f32[256]{0:T(256)S(1)}, u32[]{:S(2)}, u32[]{:S(2)}) collective-permute-start(f32[256]{0:T(256)S(1)} %add.131), channel_id=1, source_target_pairs={{0,16},{4,20},{8,24},{12,28},{16,0},{20,4},{24,8},{28,12},{32,48},... | collective-permute-start | bytes 3080 | tf_op jit(solution)/shard_map/ppermute | solution.py:27
  76.1 12.8 %collective-permute-start.11 = (f32[256]{0:T(256)S(1)}, f32[256]{0:T(256)S(1)}, u32[]{:S(2)}, u32[]{:S(2)}) collective-permute-start(f32[256]{0:T(256)S(1)} %add.132), channel_id=1, source_target_pairs={{0,32},{4,36},{8,40},{12,44},{16,48},{20,52},{24,56},{28,60},{32,0... | collective-permute-start | bytes 3080 | tf_op jit(solution)/shard_map/ppermute | solution.py:27
  88.9 16.4 %collective-permute-start.12 = (f32[256]{0:T(256)S(1)}, f32[256]{0:T(256)S(1)}, u32[]{:S(2)}, u32[]{:S(2)}) collective-permute-start(f32[256]{0:T(256)S(1)} %add.133), channel_id=1, source_target_pairs={{0,64},{4,68},{8,72},{12,76},{16,80},{20,84},{24,88},{28,92},{32,9... | collective-permute-start | bytes 3080 | tf_op jit(solution)/shard_map/ppermute | solution.py:27
  105.3 9.4 %collective-permute-start.13 = (f32[256]{0:T(256)S(1)}, f32[256]{0:T(256)S(1)}, u32[]{:S(2)}, u32[]{:S(2)}) collective-permute-start(f32[256]{0:T(256)S(1)} %add.134), channel_id=1, source_target_pairs={{0,128},{128,0},{256,384},{384,256},{512,640},{640,512},{768,896},... | collective-permute-start | bytes 3080 | tf_op jit(solution)/shard_map/ppermute | solution.py:27
  114.6 5.5 %collective-permute-start.14 = (f32[256]{0:T(256)S(1)}, f32[256]{0:T(256)S(1)}, u32[]{:S(2)}, u32[]{:S(2)}) collective-permute-start(f32[256]{0:T(256)S(1)} %add.135), channel_id=1, source_target_pairs={{0,256},{128,384},{256,0},{384,128},{512,768},{640,896},{768,512},... | collective-permute-start | bytes 3080 | tf_op jit(solution)/shard_map/ppermute | solution.py:27
  120.1 7.5 %collective-permute-start.15 = (f32[256]{0:T(256)S(1)}, f32[256]{0:T(256)S(1)}, u32[]{:S(2)}, u32[]{:S(2)}) collective-permute-start(f32[256]{0:T(256)S(1)} %add.136), channel_id=1, source_target_pairs={{0,512},{128,640},{256,768},{384,896},{512,0},{640,128},{768,256},... | collective-permute-start | bytes 3080 | tf_op jit(solution)/shard_map/ppermute | solution.py:27
